TPU v7x, 512 devices: a whole 4x4x16 slice. The times are simulated.
512 devices in a mesh: seq: 8 (over x, core), tp: 16 (over z), req: 4 (over y).
Axes of the slice: x: 4, y: 4, z: 16, core: 2. Of those that a mesh axis runs over, the one named last changes fastest.
Arguments:
- tokens: bfloat16 [32768, 1792], P(('req', 'seq'), 'tp'), parts along dimension 0, may hold values from -6 to 6
- w_in: bfloat16 [1792, 4096], P(None, 'tp'), may hold values from -0.125 to 0.125
- conv_w: float32 [3, 1792], P(None, 'tp'), may hold values from -3 to 3
- head_gain: float32 [1792], P('tp'), may hold values from 0.1 to 1.9
- w_out: bfloat16 [1792, 1792], P('tp'), may hold values from -0.125 to 0.125
- prompt_lens: int32 [16], P('req'), parts along dimension 0, may hold values from 1 to 4096, 8192 in all
- req_group: int32 [128], P('req'), parts along dimension 0, may hold values from 0 to 3, as said below
- row_request: int32 [128], P('req'), parts along dimension 0, may hold values from 0 to 31, each once
Outputs:
- mixed: bfloat16 [32768, 1792], P(('req', 'seq'), 'tp'), parts along dimension 0
- req_state: float32 [128, 16, 273, 112], P(('req', 'seq'), 'tp'), parts along dimension 0
- req_norm: float32 [128, 16, 273], P(('req', 'seq'), 'tp'), parts along dimension 0
- req_edge: bfloat16 [128, 2, 1792], P(('req', 'seq'), None, 'tp'), parts along dimension 0
There are 4 independent parts, one for each index of `req`. A program takes and returns all parts, laid end to end along the dimension named above; an argument that names none is the same for every part. Nothing has to cross between parts.
Inputs may be any that keep to these rules, and one draw needn't show every extreme that they name: `prompt_lens`: the lengths sum to 8192, and the largest is half of 8192. `req_group`: every one of the 4 prompts is shared by at least one request. `row_request`: each request appears once; rows i * 4 to (i + 1) * 4 - 1 lie on index i of seq.
All inputs are finite; a program needn't handle non-finite values.
Results may differ from a plain program's by a relative error of at most 0.019.
Values may be sent and summed in bfloat16 or wider, within the bound.
No kernel may reach another device: no remote copies, remote signals or barrier semaphores. Data moves between devices by JAX's collectives and lax.ppermute only.
A program may use at most 64 MiB of HBM per device.

v0:
```python
import jax
import jax.numpy as jnp
from jax import lax
from jax.sharding import PartitionSpec as P

FEAT = 16
HD = 112
KW = 3
PROMPTS = 4
SLOTS = 4


EPS = 1e-05
HIGH = lax.Precision.HIGHEST


def passed_along(shard, axis, by):
    size = lax.axis_size(axis)
    pairs = [(i, i + by) for i in range(size) if 0 <= i + by < size]
    return lax.ppermute(shard, axis, pairs)


def prefix(shard, axis, combine, identity):
    size, here = (lax.axis_size(axis), lax.axis_index(axis))
    everything = jax.tree.map(
        lambda part, kind: lax.all_gather(part.astype(kind), axis),
        shard,
        (jnp.bfloat16, jnp.bfloat16),
    )
    start = jax.tree.map(
        lambda part, zero: jnp.broadcast_to(jnp.asarray(zero, part.dtype), part.shape),
        shard,
        identity,
    )

    def step(k, before):
        reached = k < here
        new = combine(
            before, jax.tree.map(lambda part, own: part[k].astype(own.dtype), everything, shard)
        )
        return jax.tree.map(lambda a, b: jnp.where(reached, a, b), new, before)

    return lax.fori_loop(0, size, step, start)


def taylor_map(values):
    size = values.shape[-1]
    ones = jnp.ones(values.shape[:-1] + (1,), jnp.float32)
    pairs = (values[..., :, None] * values[..., None, :]).reshape(
        values.shape[:-1] + (size * size,)
    )
    return jnp.concatenate([ones, values, pairs * 0.5**0.5], axis=-1)


def segment_ids(positions, ends):
    return jnp.sum((positions[:, None] >= ends[None, :]).astype(jnp.int32), axis=1)


def chain_combine(earlier, later):
    keep = 1.0 - later[1]
    return (later[0] + keep * earlier[0], jnp.maximum(earlier[1], later[1]))


def local(tokens, w_in, conv_w, head_gain, w_out, prompt_lens, req_group, row_request):
    tok_rows = tokens.shape[0]
    width = 2 * FEAT + 2 * HD
    local_heads = w_in.shape[1] // width
    local_cols = local_heads * HD
    seq_pos = lax.axis_index("seq")
    first_row = seq_pos * tok_rows
    ends = jnp.cumsum(prompt_lens)
    starts = ends - prompt_lens
    positions = first_row + jnp.arange(tok_rows, dtype=jnp.int32)
    seg = segment_ids(positions, ends)
    proj = jnp.dot(
        lax.all_gather(tokens, "tp", axis=1, tiled=True), w_in, preferred_element_type=jnp.float32
    )
    proj = proj.astype(jnp.bfloat16).reshape(tok_rows, local_heads, width)
    gate_pre = proj[:, :, 2 * FEAT + HD :].reshape(tok_rows, local_cols)
    rim = passed_along(gate_pre[tok_rows - (KW - 1) :], "seq", 1)
    extended = jnp.concatenate([rim, gate_pre], 0)
    ext_pos = first_row - (KW - 1) + jnp.arange(tok_rows + KW - 1, dtype=jnp.int32)
    ext_seg = segment_ids(ext_pos, ends)
    gate = jnp.zeros((tok_rows, local_cols), jnp.float32)
    for tap in range(KW):
        low = KW - 1 - tap
        same = (ext_seg[low : low + tok_rows] == seg).astype(jnp.float32)
        gate = (
            gate
            + conv_w[tap][None, :]
            * extended[low : low + tok_rows].astype(jnp.float32)
            * same[:, None]
        )
    qs = proj[:, :, :FEAT].astype(jnp.float32) * FEAT ** (-0.25)
    ks = proj[:, :, FEAT : 2 * FEAT].astype(jnp.float32) * FEAT ** (-0.25)
    values = proj[:, :, 2 * FEAT : 2 * FEAT + HD]
    values_f = values.astype(jnp.float32)
    dots = jnp.einsum("thf,shf->hts", qs, ks, precision=HIGH)
    visible = ((positions[None, :] <= positions[:, None]) & (seg[:, None] == seg[None, :])).astype(
        jnp.float32
    )
    weights = (1.0 + dots + 0.5 * dots * dots) * visible[None]
    numer = jnp.einsum(
        "hts,shd->thd", weights.astype(jnp.bfloat16), values, preferred_element_type=jnp.float32
    )
    phi_q = taylor_map(qs)
    phi_k = taylor_map(ks)
    tail = (seg == seg[-1]).astype(jnp.float32)
    tail_keys = phi_k * tail[:, None, None]
    tail_state = jnp.einsum("thf,thd->hfd", tail_keys, values_f, precision=HIGH)
    restart = jnp.any((starts >= first_row) & (starts < first_row + tok_rows)).astype(jnp.float32)
    identity = (jnp.zeros_like(tail_state), jnp.zeros((), jnp.float32))
    carry_state, reached = prefix((tail_state, restart), "seq", chain_combine, identity)
    seg_before = jnp.sum((first_row - 1 >= ends).astype(jnp.int32))
    carried = ((seg == seg_before) & (first_row > 0)).astype(jnp.float32)
    attended = (
        numer
        + jnp.einsum("thf,hfd->thd", phi_q, carry_state, precision=HIGH) * carried[:, None, None]
    )
    inv_rms = lax.rsqrt(jnp.mean(attended * attended, axis=2, keepdims=True) + EPS)
    gain = head_gain.reshape(local_heads, HD)
    hidden = (
        attended * inv_rms * gain[None] * jax.nn.silu(gate.reshape(tok_rows, local_heads, HD))
    ).astype(jnp.bfloat16)
    hidden = hidden.reshape(tok_rows, local_cols)
    product = lax.dot_general(
        w_out, hidden, (((0,), (1,)), ((), ())), preferred_element_type=jnp.float32
    )
    summed = lax.psum_scatter(
        lax.optimization_barrier(product.astype(jnp.bfloat16))
        .astype(jnp.float32)
        .astype(jnp.bfloat16),
        "tp",
        scatter_dimension=0,
        tiled=True,
    ).astype(jnp.float32)
    mixed = summed.T.astype(jnp.bfloat16)
    prompt_index = jnp.arange(PROMPTS, dtype=jnp.int32)
    onehot = (seg[:, None] == prompt_index[None, :]).astype(jnp.float32)
    contrib_state = jnp.einsum("tg,thf,thd->ghfd", onehot, phi_k, values_f, precision=HIGH)
    contrib_norm = jnp.einsum("tg,thf->ghf", onehot, phi_k, precision=HIGH)
    offsets = jnp.arange(KW - 1, dtype=jnp.int32)
    edge_rows = ends[:, None] - (KW - 1) + offsets[None, :]
    edge_valid = edge_rows >= starts[:, None]
    scale = lax.rsqrt(prompt_lens.astype(jnp.float32))
    match = ((positions[:, None, None] == edge_rows[None]) & edge_valid[None]).astype(jnp.float32)
    contrib_edge = jnp.einsum("tgj,tc->gjc", match, gate_pre.astype(jnp.float32), precision=HIGH)
    all_state, all_norm, all_edge = (
        lax.psum(contrib_state.astype(jnp.bfloat16), "seq").astype(jnp.float32),
        lax.psum(contrib_norm.astype(jnp.bfloat16), "seq").astype(jnp.float32),
        lax.psum(contrib_edge.astype(jnp.bfloat16), "seq").astype(jnp.float32),
    )
    my_requests = lax.dynamic_slice_in_dim(row_request, seq_pos * SLOTS, SLOTS)
    my_groups = jnp.take(req_group, my_requests)
    pick = (my_groups[:, None] == prompt_index[None, :]).astype(jnp.float32)
    req_state = jnp.einsum("sg,ghfd->shfd", pick * scale[None, :], all_state, precision=HIGH)
    req_norm = jnp.einsum("sg,ghf->shf", pick * scale[None, :], all_norm, precision=HIGH)
    req_edge = jnp.einsum("sg,gjc->sjc", pick, all_edge, precision=HIGH).astype(jnp.bfloat16)
    return (mixed, req_state, req_norm, req_edge)


def solution(mesh):
    in_specs = (
        P(("req", "seq"), "tp"),
        P(None, "tp"),
        P(None, "tp"),
        P("tp"),
        P("tp", None),
        P("req"),
        P("req"),
        P("req"),
    )
    out_specs = (
        P(("req", "seq"), "tp"),
        P(("req", "seq"), "tp", None, None),
        P(("req", "seq"), "tp", None),
        P(("req", "seq"), None, "tp"),
    )
    return jax.shard_map(local, mesh=mesh, in_specs=in_specs, out_specs=out_specs, check_vma=False)
```

profile of v0, /device:TPU:24, one launch (start us, length us, event | category | flops | bytes accessed | tf_op | source)
XLA Modules:
  0.0 269.0 jit_solution(10015217603055386801)
XLA Ops:
  7.2 0.0 all-gather.4.cloned.1.call-start
  7.2 0.7 all-gather.4.cloned.1.call-update
  7.9 0.0 all-reduce.4.cloned.1.call-start
  8.0 0.8 reduce-window.7
  8.8 1.3 and_reduce_fusion
  10.8 0.1 convert_reduce_fusion.1
  10.9 0.6 slice.49
  11.5 1.3 dynamic-slice
  12.7 0.8 dynamic-update-slice
  13.5 0.5 copy-done.8
  14.0 0.1 convert_reduce_fusion
  14.1 0.6 broadcast_add_fusion
  14.7 1.4 slice_bitcast_fusion.7
  16.1 1.4 fusion.73
  17.5 73.7 %all-gather.4.cloned.1.call-done = bf16[1024,1792]{0,1:T(8,128)(2,1)} async-done(((bf16[1024,112]{0,1:T(8,128)(2,1)}), bf16[1024,1792]{0,1:T(8,128)(2,1)}) %all-gather.4.cloned.1.call-update) | async-done | bytes 3670032 | tf_op jit(solution)/shard_map/all_gather | solution.py:76
  91.2 3.2 %fusion.7 = bf16[1024,1,256]{0,2,1:T(8,128)(2,1)S(1)} fusion(bf16[1024,1792]{0,1:T(8,128)(2,1)} %all-gather.4.cloned.1.call-done, bf16[1792,256]{1,0:T(8,128)(2,1)S(1)} %copy-done), kind=kOutput, calls=%fused_computation.13 | convolution fusion | flops 939786240 | bytes 5111808 | tf_op jit(solution)/shard_map/dot_general | solution.py:75
  94.4 0.1 slice_bitcast_fusion.4
  94.5 0.1 fusion.59
  94.6 5.8 %fusion.3 = bf16[1024,1024]{1,0:T(8,128)(2,1)} fusion(s32[1024]{0:T(1024)S(1)} %convert_reduce_fusion.1, s32[1024]{0:T(1024)S(1)} %iota_add_fusion.1, bf16[1024,1,256]{0,2,1:T(8,128)(2,1)S(1)} %fusion.7), kind=kOutput, calls=%fused_computation.6 | convolution fusion | flops 210829312 | bytes 2179072 | tf_op jit(solution)/shard_map/thf,shf->hts/dot_general | solution.py:98
  100.4 1.9 collective-permute-start
  102.3 0.1 multiply_multiply_fusion.1
  102.4 0.1 multiply_multiply_fusion.2
  102.5 0.8 fusion.34
  103.3 0.2 copy-done.2
  103.5 3.0 %fusion.13 = bf16[4,273,112]{2,1,0:T(8,128)(2,1)} fusion(f32[1024,4]{0,1:T(4,128)S(1)} %fusion.67, f32[1024,112]{0,1:T(8,128)S(1)} %get-tuple-element.168, f32[1024,1,256]{0,2,1:T(8,128)S(1)} %bitcast.134, f32[1024,1,16]{0,2,1:T(8,128)S(1)} %get-tuple-element.170, f32[273]{0:T(512)S(1)} %pad.8.clone), kind=kOutput, calls=%fused_computation.19 | convolution fusion | flops 1504011776 | bytes 1834948 | tf_op jit(solution)/shard_map/tg,thf,thd->ghfd/dot_general | solution.py:140
  106.5 0.0 reduce-scatter.4.cloned.1.call-start
  106.6 0.8 convolution_convert_fusion.3
  107.4 2.1 fusion.31
  109.5 13.7 %all-gather.1 = bf16[8,273,112]{2,1,0:T(8,128)(2,1)S(1)} all-gather(bf16[1,273,112]{2,1,0:T(8,128)(2,1)S(1)} %fusion.31), channel_id=2, replica_groups=mesh['seq'=8,'tp'=16,'req'=4] {'seq'}, dimensions={0}, use_global_device_ids=true | all-gather | bytes 550368 | tf_op jit(solution)/shard_map/all_gather | solution.py:26
  123.2 15.8 %all-reduce.1 = (bf16[8]{0:T(256)(128)(2,1)}, bf16[4,273]{1,0:T(4,128)(2,1)}, bf16[4,2,112]{2,0,1:T(4,128)(2,1)}) all-reduce(bf16[8]{0:T(256)(128)(2,1)} %copy-done.8, bf16[4,273]{1,0:T(4,128)(2,1)S(1)} %fusion.34, bf16[4,2,112]{2,0,1:T(4,128)(2,1)} %convolution_convert_fusion.3), channel_id=1, replica_groups=mesh['seq'=8,'tp'=16,'req'=4] {'seq'}, use_global_device_ids=true, to_apply=%add | all-reduce | flops 1996 | bytes 7984
  138.9 15.5 %while.14 = (s32[]{:T(128)}, f32[1,273,112]{2,1,0:T(8,128)S(1)}, s32[]{:T(128)}, bf16[8,1,273,112]{3,2,1,0:T(8,128)(2,1)S(1)}, bf16[8]{0:T(256)(128)(2,1)}, /*index=5*/s32[]{:T(128)}, f32[1]{0:T(128)}, s32[]{:T(128)}) while((s32[]{:T(128)}, f32[1,273,112]{2,1,0:T(8,128)S(1)}, s32[]{:T(128)}, ...), condition=%wide.region_4.5_spmd.clone, body=%wide.region_3.4_spmd.clone.sunk | while | flops 152885 | bytes 305899 | solution.py:43
  138.9 1.2 dynamic_slice.27
  140.8 0.1 fusion.103
  140.9 1.2 dynamic_slice.27
  142.7 0.1 fusion.103
  142.8 1.2 dynamic_slice.27
  144.7 0.1 fusion.103
  144.7 1.2 dynamic_slice.27
  146.6 0.1 fusion.103
  146.7 1.2 dynamic_slice.27
  148.6 0.1 fusion.103
  148.6 1.2 dynamic_slice.27
  150.5 0.1 fusion.103
  150.6 1.2 dynamic_slice.27
  152.4 0.1 fusion.103
  152.5 1.2 dynamic_slice.27
  154.4 0.1 fusion.103
  154.5 2.5 convolution_bitcast_fusion.2
  157.0 1.2 multiply_reduce_fusion
  158.3 4.2 %fusion.4 = bf16[1792,1024]{0,1:T(8,128)(2,1)} fusion(bf16[112,1792]{1,0:T(8,128)(2,1)S(1)} %copy-done.9, bf16[1024,112]{0,1:T(8,128)(2,1)S(1)} %get-tuple-element.169, f32[1,112,1024]{2,1,0:T(8,128)S(1)} %get-tuple-element.186, bf16[2,112]{0,1:T(8,128)(2,1)} %collective-permute-done, f32[1024]{0:T(1024)S(1)} %get-tuple-element.176, f32[112]{0:T(128)S(1)} %copy-done.6, ...), kind=kOutput, calls=%fused_computation.8 | convolution fusion | flops 415744000 | bytes 4778176 | tf_op jit(solution)/shard_map/dot_general | solution.py:126
  162.5 6.0 %copy.36 = bf16[1792,1024]{1,0:T(8,128)(2,1)} copy(bf16[1792,1024]{0,1:T(8,128)(2,1)} %fusion.4) | data formatting | bytes 7340032
  168.5 0.0 reduce-scatter.4.cloned.1.call-update
  168.5 0.6 copy-done.4
  169.1 0.1 compare_select_fusion
  169.2 0.6 gather_fusion
  169.8 0.1 and_select_fusion
  169.9 0.2 convolution_convert_fusion.2
  170.1 0.6 copy.35
  170.7 0.2 convolution_bitcast_fusion.3
  170.9 0.6 copy.34
  171.5 7.4 %all-reduce.4.cloned.1.call-done = bf16[4,273,112]{2,1,0:T(8,128)(2,1)} async-done(((bf16[4,273,112]{2,1,0:T(8,128)(2,1)}), bf16[4,273,112]{2,1,0:T(8,128)(2,1)}) %all-reduce.4.cloned.1.call-update) | async-done | bytes 244624 | tf_op jit(solution)/shard_map/psum | solution.py:149
  178.9 1.6 convolution_bitcast_fusion
  180.5 1.4 copy.33
  181.9 80.6 %reduce-scatter.4.cloned.1.call-done = bf16[112,1024]{1,0:T(8,128)(2,1)} async-done(((bf16[1792,1024]{1,0:T(8,128)(2,1)}), bf16[112,1024]{1,0:T(8,128)(2,1)}) %reduce-scatter.4.cloned.1.call-update) | async-done | bytes 229392
  (37 shorter events, 0.2 us)
Async XLA Ops:
  7.2 84.1 %copy-start = (bf16[1792,256]{1,0:T(8,128)(2,1)S(1)}, bf16[1792,256]{1,0:T(8,128)(2,1)}, u32[]{:S(2)}) copy-start(bf16[1792,256]{1,0:T(8,128)(2,1)} %param.11) | copy-start | bytes 2752516
  7.2 84.0 %all-gather.4.cloned.1.call-start = ((), (), s32[]{:S(2)}) async-start(), calls=%async_computation.1 | async-start | bytes 3899392 | tf_op jit(solution)/shard_map/all_gather | solution.py:76
  7.9 170.9 %all-reduce.4.cloned.1.call-start = ((), (), s32[]{:S(2)}) async-start(), calls=%async_computation.2 | async-start | bytes 573440 | tf_op jit(solution)/shard_map/psum | solution.py:149
  13.5 0.5 copy-start.8
  100.4 57.8 %collective-permute-start = (bf16[2,112]{0,1:T(8,128)(2,1)S(1)}, bf16[2,112]{0,1:T(8,128)(2,1)}, u32[]{:S(2)}, u32[]{:S(2)}) collective-permute-start(bf16[2,112]{0,1:T(8,128)(2,1)S(1)} %slice_bitcast_fusion.4), channel_id=1, source_target_pairs={{0,64},{64,128},{128,192},{192,256},{256,320},{320,384},{384,448},... | collective-permute-start | bytes 1352 | tf_op jit(solution)/shard_map/ppermute | solution.py:20
  102.5 1.0 copy-start.2
  106.5 155.9 %reduce-scatter.4.cloned.1.call-start = ((), (), s32[]{:S(2)}) async-start(), calls=%async_computation.3 | async-start | bytes 3899392
  154.5 3.8 %copy-start.5 = (f32[112]{0:T(128)S(1)}, f32[112]{0:T(128)}, u32[]{:S(2)}) copy-start(f32[112]{0:T(128)} %get-tuple-element.180) | copy-start | bytes 1348
  154.5 3.8 %copy-start.6 = (f32[112]{0:T(128)S(1)}, f32[112]{0:T(128)}, u32[]{:S(2)}) copy-start(f32[112]{0:T(128)} %get-tuple-element.181) | copy-start | bytes 1348
  154.5 3.8 %copy-start.7 = (f32[112]{0:T(128)S(1)}, f32[112]{0:T(128)}, u32[]{:S(2)}) copy-start(f32[112]{0:T(128)} %get-tuple-element.182) | copy-start | bytes 1348
  154.5 3.8 %copy-start.9 = (bf16[112,1792]{1,0:T(8,128)(2,1)S(1)}, bf16[112,1792]{1,0:T(8,128)(2,1)}, u32[]{:S(2)}) copy-start(bf16[112,1792]{1,0:T(8,128)(2,1)} %param.14) | copy-start | bytes 1204228
  154.5 3.8 %copy-start.12 = (f32[112]{0:T(128)S(1)}, f32[112]{0:T(128)}, u32[]{:S(2)}) copy-start(f32[112]{0:T(128)} %param.13) | copy-start | bytes 1348
  168.4 0.7 copy-start.4
  168.4 0.7 copy-start.1
  168.4 1.4 copy-start.3
  168.4 1.5 copy-start.11
  168.4 2.2 copy-start.10
Sparse Core Ops, SparseCore 0:
  10.1 81.1 all-gather.3
  106.7 72.1 all-reduce.3
  182.3 80.0 reduce-scatter.3
where the time goes:
time: 270 us; the launch traced here: 269 us
  waiting for transfers between devices  162 us (60%)
  blocking collectives  29.5 us (11%)
  matrix products  25.4 us (9%)
  local copies, waits for them, and re-layouts  24.4 us (9%)
  between operations  14.7 us (5%)
  loops' own time  5.33 us (2%)
  other arithmetic  5.31 us (2%)
    unnamed x4, waiting for transfers between devices  81.3 us
    all_gather x1, waiting for transfers between devices, local(): lax.all_gather(tokens, 'tp', axis=1, tiled=True)  73.7 us
    unnamed x1, blocking collectives  15.8 us
    all_gather x1, blocking collectives, prefix(): lax.all_gather(part.astype(kind), axis)  13.7 us
    unnamed x33, local copies, waits for them, and re-layouts  12 us
    dynamic_slice x8, local copies, waits for them, and re-layouts, step(): part[k].astype(own.dtype)  9.72 us
    psum x1, waiting for transfers between devices, local(): lax.psum(contrib_state.astype(jnp.bfloat16), 'seq').astype(jnp.float32)  7.38 us
    dot_general x1, matrix products, local(): dots = jnp.einsum('thf,shf->hts', qs, ks, precision=HIGH)  5.77 us
  transfers between devices with their start and end apart: 4, of which 3 were waited for; matrix products, arithmetic and copies ran while one was open for 17% of the time, Pallas kernels for 0%

commit v1 on v0

v1 whole, which is shorter than its diff:
```python
import jax
import jax.numpy as jnp
from jax import lax
from jax.sharding import PartitionSpec as P

FEAT = 16
HD = 112
KW = 3
PROMPTS = 4
SLOTS = 4


EPS = 1e-05
HIGH = lax.Precision.HIGHEST


def passed_along(shard, axis, by):
    size = lax.axis_size(axis)
    pairs = [(i, i + by) for i in range(size) if 0 <= i + by < size]
    return lax.ppermute(shard, axis, pairs)


def scan_blocks(parts, axis):
    size, here = (lax.axis_size(axis), lax.axis_index(axis))
    total = [p.astype(jnp.float32) for p in parts]
    before = [jnp.zeros_like(t) for t in total]
    step = 1
    while step < size:
        pairs = [(i, i ^ step) for i in range(size)]
        got = lax.ppermute(tuple(t.astype(jnp.bfloat16) for t in total), axis, pairs)
        got = [g.astype(jnp.float32) for g in got]
        lower = ((here ^ step) < here).astype(jnp.float32)
        before = [b + lower * g for b, g in zip(before, got)]
        total = [t + g for t, g in zip(total, got)]
        step *= 2
    return before, total


def taylor_map(values):
    size = values.shape[-1]
    ones = jnp.ones(values.shape[:-1] + (1,), jnp.float32)
    pairs = (values[..., :, None] * values[..., None, :]).reshape(
        values.shape[:-1] + (size * size,)
    )
    return jnp.concatenate([ones, values, pairs * 0.5**0.5], axis=-1)


def segment_ids(positions, ends):
    return jnp.sum((positions[:, None] >= ends[None, :]).astype(jnp.int32), axis=1)


def local(tokens, w_in, conv_w, head_gain, w_out, prompt_lens, req_group, row_request):
    tok_rows = tokens.shape[0]
    width = 2 * FEAT + 2 * HD
    local_heads = w_in.shape[1] // width
    local_cols = local_heads * HD
    seq_pos = lax.axis_index("seq")
    first_row = seq_pos * tok_rows
    ends = jnp.cumsum(prompt_lens)
    starts = ends - prompt_lens
    positions = first_row + jnp.arange(tok_rows, dtype=jnp.int32)
    seg = segment_ids(positions, ends)
    proj = jnp.dot(
        lax.all_gather(tokens, "tp", axis=1, tiled=True), w_in, preferred_element_type=jnp.float32
    )
    proj = proj.astype(jnp.bfloat16).reshape(tok_rows, local_heads, width)
    gate_pre = proj[:, :, 2 * FEAT + HD :].reshape(tok_rows, local_cols)
    rim = passed_along(gate_pre[tok_rows - (KW - 1) :], "seq", 1)
    extended = jnp.concatenate([rim, gate_pre], 0)
    ext_pos = first_row - (KW - 1) + jnp.arange(tok_rows + KW - 1, dtype=jnp.int32)
    ext_seg = segment_ids(ext_pos, ends)
    gate = jnp.zeros((tok_rows, local_cols), jnp.float32)
    for tap in range(KW):
        low = KW - 1 - tap
        same = (ext_seg[low : low + tok_rows] == seg).astype(jnp.float32)
        gate = (
            gate
            + conv_w[tap][None, :]
            * extended[low : low + tok_rows].astype(jnp.float32)
            * same[:, None]
        )
    qs_b = proj[:, :, :FEAT] * jnp.bfloat16(FEAT ** (-0.25))
    ks_b = proj[:, :, FEAT : 2 * FEAT] * jnp.bfloat16(FEAT ** (-0.25))
    qs = qs_b.astype(jnp.float32)
    ks = ks_b.astype(jnp.float32)
    values = proj[:, :, 2 * FEAT : 2 * FEAT + HD]
    values_f = values.astype(jnp.float32)
    dots = jnp.einsum("thf,shf->hts", qs_b, ks_b, preferred_element_type=jnp.float32)
    visible = (positions[None, :] <= positions[:, None]) & (seg[:, None] == seg[None, :])
    weights = jnp.where(visible[None], 1.0 + dots + 0.5 * dots * dots, 0.0)
    numer = jnp.einsum(
        "hts,shd->thd", weights.astype(jnp.bfloat16), values, preferred_element_type=jnp.float32
    )
    phi_q = taylor_map(qs)
    phi_k = taylor_map(ks)
    fmap = phi_k.shape[-1]
    prompt_index = jnp.arange(PROMPTS, dtype=jnp.int32)
    onehot = (seg[:, None] == prompt_index[None, :]).astype(jnp.float32)
    keyed = (onehot[:, :, None, None] * phi_k[:, None, :, :]).reshape(
        tok_rows, PROMPTS * local_heads * fmap
    )
    contrib_state = lax.dot_general(
        keyed.reshape(tok_rows, PROMPTS, local_heads, fmap),
        values_f,
        (((0,), (0,)), ((2,), (1,))),
        precision=HIGH,
    )
    contrib_norm = jnp.einsum("tg,thf->ghf", onehot, phi_k, precision=HIGH)
    offsets = jnp.arange(KW - 1, dtype=jnp.int32)
    edge_rows = ends[:, None] - (KW - 1) + offsets[None, :]
    edge_valid = edge_rows >= starts[:, None]
    match = ((positions[:, None, None] == edge_rows[None]) & edge_valid[None]).astype(jnp.bfloat16)
    contrib_edge = jnp.einsum("tgj,tc->gjc", match, gate_pre, preferred_element_type=jnp.float32)
    (pre_state, _, _), (all_state, all_norm, all_edge) = scan_blocks(
        (contrib_state, contrib_norm, contrib_edge), "seq"
    )
    seg_before = jnp.sum((first_row - 1 >= ends).astype(jnp.int32))
    carry_state = lax.dynamic_index_in_dim(pre_state, seg_before, axis=1, keepdims=False)
    carried = ((seg == seg_before) & (first_row > 0)).astype(jnp.float32)
    attended = (
        numer
        + jnp.einsum("thf,hfd->thd", phi_q, carry_state, precision=HIGH) * carried[:, None, None]
    )
    inv_rms = lax.rsqrt(jnp.mean(attended * attended, axis=2, keepdims=True) + EPS)
    gain = head_gain.reshape(local_heads, HD)
    hidden = (
        attended * inv_rms * gain[None] * jax.nn.silu(gate.reshape(tok_rows, local_heads, HD))
    ).astype(jnp.bfloat16)
    hidden = hidden.reshape(tok_rows, local_cols)
    product = lax.dot_general(
        w_out, hidden, (((0,), (1,)), ((), ())), preferred_element_type=jnp.float32
    )
    summed = lax.psum_scatter(
        lax.optimization_barrier(product.astype(jnp.bfloat16))
        .astype(jnp.float32)
        .astype(jnp.bfloat16),
        "tp",
        scatter_dimension=0,
        tiled=True,
    ).astype(jnp.float32)
    mixed = summed.T.astype(jnp.bfloat16)
    scale = lax.rsqrt(prompt_lens.astype(jnp.float32))
    my_requests = lax.dynamic_slice_in_dim(row_request, seq_pos * SLOTS, SLOTS)
    my_groups = jnp.take(req_group, my_requests)
    my_scale = jnp.take(scale, my_groups)
    req_state = jnp.take(all_state, my_groups, axis=1).transpose(1, 0, 2, 3) * my_scale[
        :, None, None, None
    ]
    req_norm = jnp.take(all_norm, my_groups, axis=0) * my_scale[:, None, None]
    req_edge = jnp.take(all_edge, my_groups, axis=0).astype(jnp.bfloat16)
    return (mixed, req_state, req_norm, req_edge)


def solution(mesh):
    in_specs = (
        P(("req", "seq"), "tp"),
        P(None, "tp"),
        P(None, "tp"),
        P("tp"),
        P("tp", None),
        P("req"),
        P("req"),
        P("req"),
    )
    out_specs = (
        P(("req", "seq"), "tp"),
        P(("req", "seq"), "tp", None, None),
        P(("req", "seq"), "tp", None),
        P(("req", "seq"), None, "tp"),
    )
    return jax.shard_map(local, mesh=mesh, in_specs=in_specs, out_specs=out_specs, check_vma=False)
```

time: 270 us -> 226 us (0.84)
  blocking collectives: 29.5 us -> 0 us
  starting transfers between devices: 2 us -> 30.1 us
  waiting for transfers between devices: 162 us -> 141 us
  local copies, waits for them, and re-layouts: 24.4 us -> 14.6 us
  matrix products: 25.4 us -> 16.2 us
  loops' own time: 5.33 us -> 0 us
    unnamed x4 -> x3, waiting for transfers between devices: 81.3 us -> 47.3 us
    ppermute x0 -> x9, starting transfers between devices: none -> 27 us  [scan_blocks(): lax.ppermute(tuple((t.astype(jnp.bfloat16) for t in total)), axis, pairs)]
    unnamed x1 -> x0, blocking collectives: 15.8 us -> none
    ppermute x0 -> x9, waiting for transfers between devices: none -> 14.2 us  [scan_blocks(): lax.ppermute(tuple((t.astype(jnp.bfloat16) for t in total)), axis, pairs)]
    all_gather x1 -> x0, blocking collectives: 13.7 us -> none  [prefix(): lax.all_gather(part.astype(kind), axis)]
    dot_general x7 -> x2, matrix products: 13.6 us -> 3.48 us  [the longest x1 2.33 us: local(): lax.dot_general(keyed.reshape(tok_rows, PROMPTS, local_heads, fmap), valu...]
    dynamic_slice x8 -> x0, local copies, waits for them, and re-layouts: 9.72 us -> none  [step(): part[k].astype(own.dtype)]
    psum x1 -> x0, waiting for transfers between devices: 7.38 us -> none  [local(): lax.psum(contrib_state.astype(jnp.bfloat16), 'seq').astype(jnp.float32)]
  transfers between devices with their start and end apart: 4 -> 12, of which waited for: 3 -> 5; matrix products, arithmetic and copies ran while one was open for 17% -> 9% of each run, Pallas kernels for 0% -> 0%
where the time goes in v1:
time: 226 us; the launch traced here: 225 us
  waiting for transfers between devices  141 us (62%)
  starting transfers between devices  30.1 us (13%)
  between operations  16.6 us (7%)
  matrix products  16.2 us (7%)
  local copies, waits for them, and re-layouts  14.6 us (6%)
  other arithmetic  6.73 us (3%)
    all_gather x1, waiting for transfers between devices, local(): lax.all_gather(tokens, 'tp', axis=1, tiled=True)  79 us
    unnamed x3, waiting for transfers between devices  47.3 us
    ppermute x9, starting transfers between devices, scan_blocks(): lax.ppermute(tuple((t.astype(jnp.bfloat16) for t in total)), axis, pairs)  27 us
    ppermute x9, waiting for transfers between devices, scan_blocks(): lax.ppermute(tuple((t.astype(jnp.bfloat16) for t in total)), axis, pairs)  14.2 us
    unnamed x35, local copies, waits for them, and re-layouts  8.61 us
  transfers between devices with their start and end apart: 12, of which 5 were waited for; matrix products, arithmetic and copies ran while one was open for 9% of the time, Pallas kernels for 0%

profile of v1, /device:TPU:24, one launch (start us, length us, event | category | flops | bytes accessed | tf_op | source)
XLA Modules:
  0.0 224.7 jit_solution(10938413765270378709)
XLA Ops:
  7.2 0.0 copy-start
  7.2 0.0 all-gather.2.cloned.1.call-start
  7.2 0.7 all-gather.2.cloned.1.call-update
  7.9 0.0 reduce-scatter.4.cloned.1.call-start
  8.0 0.8 reduce-window.7
  8.8 0.1 convert_reduce_fusion.1
  8.9 0.1 convert_reduce_fusion
  9.0 1.9 bitcast_subtract_fusion
  10.9 1.3 fusion.67
  12.2 79.0 %all-gather.2.cloned.1.call-done = bf16[1024,1792]{0,1:T(8,128)(2,1)} async-done(((bf16[1024,112]{0,1:T(8,128)(2,1)}), bf16[1024,1792]{0,1:T(8,128)(2,1)}) %all-gather.2.cloned.1.call-update) | async-done | bytes 3670032 | tf_op jit(solution)/shard_map/all_gather | solution.py:64
  91.2 3.2 %fusion.9 = bf16[1024,1,256]{0,2,1:T(8,128)(2,1)S(1)} fusion(bf16[1024,1792]{0,1:T(8,128)(2,1)} %all-gather.2.cloned.1.call-done, bf16[1792,256]{1,0:T(8,128)(2,1)S(1)} %copy-done), kind=kOutput, calls=%fused_computation.17 | convolution fusion | flops 939786240 | bytes 5111808 | tf_op jit(solution)/shard_map/dot_general | solution.py:63
  94.4 0.0 copy-start.4
  94.4 0.0 copy-start.7
  94.5 0.7 fusion.55
  95.1 0.1 multiply_multiply_fusion.2
  95.2 0.2 maximum_bitcast_fusion
  95.4 2.3 %fusion = f32[4,273,112]{2,1,0:T(8,128)S(1)} fusion(f32[1024,273]{0,1:T(8,128)S(1)} %maximum_bitcast_fusion, f32[1024,4]{0,1:T(4,128)S(1)} %fusion.59, bf16[1024,1,256]{0,2,1:T(8,128)(2,1)S(1)} %fusion.9), kind=kOutput, calls=%fused_computation.6 | convolution fusion | flops 1503989760 | bytes 1881856 | tf_op jit(solution)/shard_map/dot_general | solution.py:102
  97.8 1.9 collective-permute-start
  99.7 0.6 slice_bitcast_fusion.4
  102.4 1.4 slice_bitcast_fusion.1
  103.8 3.0 %collective-permute-start.3 = (bf16[2,112]{0,1:T(8,128)(2,1)}, bf16[2,112]{0,1:T(8,128)(2,1)}, u32[]{:S(2)}, u32[]{:S(2)}) collective-permute-start(bf16[2,112]{0,1:T(8,128)(2,1)} %slice_bitcast_fusion.1), channel_id=1, source_target_pairs={{0,64},{64,128},{128,192},{192,256},{256,320},{320,384},{384,448},... | collective-permute-start | bytes 1352 | tf_op jit(solution)/shard_map/ppermute | solution.py:20
  106.8 0.0 collective-permute-done
  106.8 0.1 fusion.20
  106.8 2.8 %collective-permute-start.1 = (bf16[1,4,273,112]{3,2,1,0:T(8,128)(2,1)S(1)}, bf16[1,4,273,112]{3,2,1,0:T(8,128)(2,1)S(1)}, u32[]{:S(2)}, u32[]{:S(2)}) collective-permute-start(bf16[1,4,273,112]{3,2,1,0:T(8,128)(2,1)S(1)} %fusion.20), channel_id=1, source_target_pairs={{0,128},{64,192},{128,0},{192,64},{256,384},{320,448},{384,256},{4... | collective-permute-start | bytes 733832 | tf_op jit(solution)/shard_map/ppermute | solution.py:30
  109.6 3.4 %fusion.10 = f32[1,112,1024]{2,1,0:T(8,128)} fusion(s32[1024]{0:T(1024)S(1)} %convert_reduce_fusion.1, s32[1024]{0:T(1024)S(1)} %iota_add_fusion.1, bf16[1024,1,256]{0,2,1:T(8,128)(2,1)} %copy-done.4), kind=kOutput, calls=%fused_computation.18 | convolution fusion | flops 277905408 | bytes 770048 | tf_op jit(solution)/shard_map/hts,shd->thd/dot_general | solution.py:91
  113.1 4.9 %collective-permute-done.1 = bf16[1,4,273,112]{3,2,1,0:T(8,128)(2,1)S(1)} collective-permute-done((bf16[1,4,273,112]{3,2,1,0:T(8,128)(2,1)S(1)}, bf16[1,4,273,112]{3,2,1,0:T(8,128)(2,1)S(1)}, u32[]{:S(2)}, u32[]{:S(2)}) %collective-permute-start.1) | collective-permute-done | bytes 244640 | tf_op jit(solution)/shard_map/ppermute | solution.py:30
  118.0 0.1 fusion.44
  118.1 0.0 copy-start.5
  118.2 0.0 copy-start.14
  118.2 0.0 copy-start.15
  118.2 4.7 %collective-permute-start.2 = (bf16[1,4,273,112]{3,2,1,0:T(8,128)(2,1)S(1)}, bf16[1,4,273,112]{3,2,1,0:T(8,128)(2,1)S(1)}, u32[]{:S(2)}, u32[]{:S(2)}) collective-permute-start(bf16[1,4,273,112]{3,2,1,0:T(8,128)(2,1)S(1)} %fusion.44), channel_id=1, source_target_pairs={{0,256},{64,320},{128,384},{192,448},{256,0},{320,64},{384,128},{4... | collective-permute-start | bytes 733832 | tf_op jit(solution)/shard_map/ppermute | solution.py:30
  122.9 0.1 multiply_multiply_fusion.1
  123.1 1.0 slice_bitcast_fusion
  124.1 6.0 %collective-permute-done.2 = bf16[1,4,273,112]{3,2,1,0:T(8,128)(2,1)S(1)} collective-permute-done((bf16[1,4,273,112]{3,2,1,0:T(8,128)(2,1)S(1)}, bf16[1,4,273,112]{3,2,1,0:T(8,128)(2,1)S(1)}, u32[]{:S(2)}, u32[]{:S(2)}) %collective-permute-start.2) | collective-permute-done | bytes 244640 | tf_op jit(solution)/shard_map/ppermute | solution.py:30
  130.2 1.2 multiply_reduce_fusion
  131.4 0.0 collective-permute-done.3
  131.5 4.1 %fusion.5 = bf16[1792,1024]{0,1:T(8,128)(2,1)} fusion(bf16[112,1792]{1,0:T(8,128)(2,1)S(1)} %copy-done.14, bf16[1024,112]{0,1:T(8,128)(2,1)S(1)} %slice_bitcast_fusion, f32[1,112,1024]{2,1,0:T(8,128)S(1)} %get-tuple-element.37, bf16[2,112]{0,1:T(8,128)(2,1)} %collective-permute-done.3, f32[1024]{0:T(1024)S(1)} %copy-done.6, f32[112]{0:T(128)S(1)} %copy-done.12, ...), kind=kOutput, calls=%fused_computation.12 | convolution fusion | flops 415744000 | bytes 4778176 | tf_op jit(solution)/shard_map/dot_general | solution.py:130
  135.6 5.9 %copy.28 = bf16[1792,1024]{1,0:T(8,128)(2,1)} copy(bf16[1792,1024]{0,1:T(8,128)(2,1)} %fusion.5) | data formatting | bytes 7340032
  141.6 0.0 reduce-scatter.4.cloned.1.call-update
  141.6 0.6 copy-done.1
  142.2 0.6 gather_fusion
  142.9 0.6 gather_fusion.2
  143.6 1.2 fusion.84
  144.7 1.9 collective-permute-start.7
  146.7 0.8 fusion.58
  147.5 2.4 %collective-permute-start.4 = (bf16[4,1,273]{2,0,1:T(4,128)(2,1)S(1)}, bf16[4,1,273]{2,0,1:T(4,128)(2,1)S(1)}, u32[]{:S(2)}, u32[]{:S(2)}) collective-permute-start(bf16[4,1,273]{2,0,1:T(4,128)(2,1)S(1)} %convert_bitcast_fusion.1), channel_id=1, source_target_pairs={{0,64},{64,0},{128,192},{192,128},{256,320},{320,256},{384,448},{4... | collective-permute-start | bytes 6560 | tf_op jit(solution)/shard_map/ppermute | solution.py:30
  149.9 0.0 collective-permute-done.7
  149.9 3.6 %collective-permute-start.8 = (bf16[4,2,112]{2,0,1:T(4,128)(2,1)S(1)}, bf16[4,2,112]{2,0,1:T(4,128)(2,1)S(1)}, u32[]{:S(2)}, u32[]{:S(2)}) collective-permute-start(bf16[4,2,112]{2,0,1:T(4,128)(2,1)S(1)} %fusion.71), channel_id=1, source_target_pairs={{0,128},{64,192},{128,0},{192,64},{256,384},{320,448},{384,256},{4... | collective-permute-start | bytes 5384 | tf_op jit(solution)/shard_map/ppermute | solution.py:30
  153.5 0.0 collective-permute-done.4
  153.6 2.2 collective-permute-start.5
  155.8 4.9 %collective-permute-start.9 = (bf16[4,2,112]{2,0,1:T(4,128)(2,1)S(1)}, bf16[4,2,112]{2,0,1:T(4,128)(2,1)S(1)}, u32[]{:S(2)}, u32[]{:S(2)}) collective-permute-start(bf16[4,2,112]{2,0,1:T(4,128)(2,1)S(1)} %fusion.73), channel_id=1, source_target_pairs={{0,256},{64,320},{128,384},{192,448},{256,0},{320,64},{384,128},{4... | collective-permute-start | bytes 5384 | tf_op jit(solution)/shard_map/ppermute | solution.py:30
  160.7 0.0 collective-permute-done.5
  160.8 2.5 %collective-permute-start.6 = (bf16[4,1,273]{2,0,1:T(4,128)(2,1)S(1)}, bf16[4,1,273]{2,0,1:T(4,128)(2,1)S(1)}, u32[]{:S(2)}, u32[]{:S(2)}) collective-permute-start(bf16[4,1,273]{2,0,1:T(4,128)(2,1)S(1)} %fusion.70), channel_id=1, source_target_pairs={{0,256},{64,320},{128,384},{192,448},{256,0},{320,64},{384,128},{4... | collective-permute-start | bytes 6560 | tf_op jit(solution)/shard_map/ppermute | solution.py:30
  163.3 0.6 gather_fusion.4
  163.8 0.7 select_convert_fusion
  164.5 3.3 %collective-permute-done.6 = bf16[4,1,273]{2,0,1:T(4,128)(2,1)S(1)} collective-permute-done((bf16[4,1,273]{2,0,1:T(4,128)(2,1)S(1)}, bf16[4,1,273]{2,0,1:T(4,128)(2,1)S(1)}, u32[]{:S(2)}, u32[]{:S(2)}) %collective-permute-start.6) | collective-permute-done | bytes 2216 | tf_op jit(solution)/shard_map/ppermute | solution.py:30
  167.8 0.6 gather_fusion.3
  168.3 0.1 fusion.66
  168.4 0.6 copy.27
  169.0 0.1 add_bitcast_fusion
  169.1 0.6 gather_fusion.1
  169.7 0.1 fusion.17
  169.9 1.4 copy.26
  171.2 46.7 %reduce-scatter.4.cloned.1.call-done = bf16[112,1024]{1,0:T(8,128)(2,1)} async-done(((bf16[1792,1024]{1,0:T(8,128)(2,1)}), bf16[112,1024]{1,0:T(8,128)(2,1)}) %reduce-scatter.4.cloned.1.call-update) | async-done | bytes 229392
  (51 shorter events, 0.3 us)
Async XLA Ops:
  7.2 84.1 %copy-start = (bf16[1792,256]{1,0:T(8,128)(2,1)S(1)}, bf16[1792,256]{1,0:T(8,128)(2,1)}, u32[]{:S(2)}) copy-start(bf16[1792,256]{1,0:T(8,128)(2,1)} %param.9) | copy-start | bytes 2752516
  7.2 84.0 %all-gather.2.cloned.1.call-start = ((), (), s32[]{:S(2)}) async-start(), calls=%async_computation.1 | async-start | bytes 3899392 | tf_op jit(solution)/shard_map/all_gather | solution.py:64
  7.9 210.0 %reduce-scatter.4.cloned.1.call-start = ((), (), s32[]{:S(2)}) async-start(), calls=%async_computation.2 | async-start | bytes 3899392
  94.4 5.3 %copy-start.4 = (bf16[1024,1,256]{0,2,1:T(8,128)(2,1)}, bf16[1024,1,256]{0,2,1:T(8,128)(2,1)S(1)}, u32[]{:S(2)}) copy-start(bf16[1024,1,256]{0,2,1:T(8,128)(2,1)S(1)} %fusion.9) | copy-start | bytes 1572868
  94.4 5.3 %copy-start.7 = (f32[3,112]{1,0:T(4,128)S(1)}, f32[3,112]{1,0:T(4,128)}, u32[]{:S(2)}) copy-start(f32[3,112]{1,0:T(4,128)} %param.10) | copy-start | bytes 4036
  97.8 9.0 %collective-permute-start = (bf16[1,4,273,112]{3,2,1,0:T(8,128)(2,1)S(1)}, bf16[1,4,273,112]{3,2,1,0:T(8,128)(2,1)S(1)}, u32[]{:S(2)}, u32[]{:S(2)}) collective-permute-start(bf16[1,4,273,112]{3,2,1,0:T(8,128)(2,1)S(1)} %convert_bitcast_fusion), channel_id=1, source_target_pairs={{0,64},{64,0},{128,192},{192,128},{256,320},{320,256},{384,448},{4... | collective-permute-start | bytes 733832 | tf_op jit(solution)/shard_map/ppermute | solution.py:30
  103.8 27.6 %collective-permute-start.3 = (bf16[2,112]{0,1:T(8,128)(2,1)}, bf16[2,112]{0,1:T(8,128)(2,1)}, u32[]{:S(2)}, u32[]{:S(2)}) collective-permute-start(bf16[2,112]{0,1:T(8,128)(2,1)} %slice_bitcast_fusion.1), channel_id=1, source_target_pairs={{0,64},{64,128},{128,192},{192,256},{256,320},{320,384},{384,448},... | collective-permute-start | bytes 1352 | tf_op jit(solution)/shard_map/ppermute | solution.py:20
  106.8 11.1 %collective-permute-start.1 = (bf16[1,4,273,112]{3,2,1,0:T(8,128)(2,1)S(1)}, bf16[1,4,273,112]{3,2,1,0:T(8,128)(2,1)S(1)}, u32[]{:S(2)}, u32[]{:S(2)}) collective-permute-start(bf16[1,4,273,112]{3,2,1,0:T(8,128)(2,1)S(1)} %fusion.20), channel_id=1, source_target_pairs={{0,128},{64,192},{128,0},{192,64},{256,384},{320,448},{384,256},{4... | collective-permute-start | bytes 733832 | tf_op jit(solution)/shard_map/ppermute | solution.py:30
  113.0 17.1 %copy-start.2 = (f32[1,112,1024]{2,1,0:T(8,128)S(1)}, f32[1,112,1024]{2,1,0:T(8,128)}, u32[]{:S(2)}) copy-start(f32[1,112,1024]{2,1,0:T(8,128)} %fusion.10) | copy-start | bytes 1376260
  113.1 17.1 %copy-start.3 = (f32[1024,1,16]{0,2,1:T(8,128)S(1)}, f32[1024,1,16]{0,2,1:T(8,128)}, u32[]{:S(2)}) copy-start(f32[1024,1,16]{0,2,1:T(8,128)} %get-tuple-element.25) | copy-start | bytes 196612
  118.1 13.3 %copy-start.5 = (f32[1024]{0:T(1024)S(1)}, f32[1024]{0:T(1024)}, u32[]{:S(2)}) copy-start(f32[1024]{0:T(1024)} %get-tuple-element.27) | copy-start | bytes 12292
  118.1 13.3 %copy-start.6 = (f32[1024]{0:T(1024)S(1)}, f32[1024]{0:T(1024)}, u32[]{:S(2)}) copy-start(f32[1024]{0:T(1024)} %get-tuple-element.28) | copy-start | bytes 12292
  118.1 13.3 %copy-start.11 = (f32[112]{0:T(128)S(1)}, f32[112]{0:T(128)}, u32[]{:S(2)}) copy-start(f32[112]{0:T(128)} %get-tuple-element.30) | copy-start | bytes 1348
  118.1 13.3 %copy-start.12 = (f32[112]{0:T(128)S(1)}, f32[112]{0:T(128)}, u32[]{:S(2)}) copy-start(f32[112]{0:T(128)} %get-tuple-element.31) | copy-start | bytes 1348
  118.1 13.3 %copy-start.13 = (f32[112]{0:T(128)S(1)}, f32[112]{0:T(128)}, u32[]{:S(2)}) copy-start(f32[112]{0:T(128)} %get-tuple-element.32) | copy-start | bytes 1348
  118.2 13.3 %copy-start.14 = (bf16[112,1792]{1,0:T(8,128)(2,1)S(1)}, bf16[112,1792]{1,0:T(8,128)(2,1)}, u32[]{:S(2)}) copy-start(bf16[112,1792]{1,0:T(8,128)(2,1)} %param.12) | copy-start | bytes 1204228
  118.2 13.3 %copy-start.15 = (f32[112]{0:T(128)S(1)}, f32[112]{0:T(128)}, u32[]{:S(2)}) copy-start(f32[112]{0:T(128)} %param.11) | copy-start | bytes 1348
  118.2 11.9 %collective-permute-start.2 = (bf16[1,4,273,112]{3,2,1,0:T(8,128)(2,1)S(1)}, bf16[1,4,273,112]{3,2,1,0:T(8,128)(2,1)S(1)}, u32[]{:S(2)}, u32[]{:S(2)}) collective-permute-start(bf16[1,4,273,112]{3,2,1,0:T(8,128)(2,1)S(1)} %fusion.44), channel_id=1, source_target_pairs={{0,256},{64,320},{128,384},{192,448},{256,0},{320,64},{384,128},{4... | collective-permute-start | bytes 733832 | tf_op jit(solution)/shard_map/ppermute | solution.py:30
  141.6 0.7 copy-start.1
  141.6 1.3 copy-start.8
  141.6 2.0 copy-start.10
  141.6 2.0 copy-start.9
  144.7 5.2 %collective-permute-start.7 = (bf16[4,2,112]{2,0,1:T(4,128)(2,1)S(1)}, bf16[4,2,112]{2,0,1:T(4,128)(2,1)S(1)}, u32[]{:S(2)}, u32[]{:S(2)}) collective-permute-start(bf16[4,2,112]{2,0,1:T(4,128)(2,1)S(1)} %get-tuple-element.38), channel_id=1, source_target_pairs={{0,64},{64,0},{128,192},{192,128},{256,320},{320,256},{384,448},{4... | collective-permute-start | bytes 5384 | tf_op jit(solution)/shard_map/ppermute | solution.py:30
  147.5 6.1 %collective-permute-start.4 = (bf16[4,1,273]{2,0,1:T(4,128)(2,1)S(1)}, bf16[4,1,273]{2,0,1:T(4,128)(2,1)S(1)}, u32[]{:S(2)}, u32[]{:S(2)}) collective-permute-start(bf16[4,1,273]{2,0,1:T(4,128)(2,1)S(1)} %convert_bitcast_fusion.1), channel_id=1, source_target_pairs={{0,64},{64,0},{128,192},{192,128},{256,320},{320,256},{384,448},{4... | collective-permute-start | bytes 6560 | tf_op jit(solution)/shard_map/ppermute | solution.py:30
  149.9 5.9 %collective-permute-start.8 = (bf16[4,2,112]{2,0,1:T(4,128)(2,1)S(1)}, bf16[4,2,112]{2,0,1:T(4,128)(2,1)S(1)}, u32[]{:S(2)}, u32[]{:S(2)}) collective-permute-start(bf16[4,2,112]{2,0,1:T(4,128)(2,1)S(1)} %fusion.71), channel_id=1, source_target_pairs={{0,128},{64,192},{128,0},{192,64},{256,384},{320,448},{384,256},{4... | collective-permute-start | bytes 5384 | tf_op jit(solution)/shard_map/ppermute | solution.py:30
  153.6 7.2 %collective-permute-start.5 = (bf16[4,1,273]{2,0,1:T(4,128)(2,1)S(1)}, bf16[4,1,273]{2,0,1:T(4,128)(2,1)S(1)}, u32[]{:S(2)}, u32[]{:S(2)}) collective-permute-start(bf16[4,1,273]{2,0,1:T(4,128)(2,1)S(1)} %fusion.72), channel_id=1, source_target_pairs={{0,128},{64,192},{128,0},{192,64},{256,384},{320,448},{384,256},{4... | collective-permute-start | bytes 6560 | tf_op jit(solution)/shard_map/ppermute | solution.py:30
  155.8 7.4 %collective-permute-start.9 = (bf16[4,2,112]{2,0,1:T(4,128)(2,1)S(1)}, bf16[4,2,112]{2,0,1:T(4,128)(2,1)S(1)}, u32[]{:S(2)}, u32[]{:S(2)}) collective-permute-start(bf16[4,2,112]{2,0,1:T(4,128)(2,1)S(1)} %fusion.73), channel_id=1, source_target_pairs={{0,256},{64,320},{128,384},{192,448},{256,0},{320,64},{384,128},{4... | collective-permute-start | bytes 5384 | tf_op jit(solution)/shard_map/ppermute | solution.py:30
  160.8 7.0 %collective-permute-start.6 = (bf16[4,1,273]{2,0,1:T(4,128)(2,1)S(1)}, bf16[4,1,273]{2,0,1:T(4,128)(2,1)S(1)}, u32[]{:S(2)}, u32[]{:S(2)}) collective-permute-start(bf16[4,1,273]{2,0,1:T(4,128)(2,1)S(1)} %fusion.70), channel_id=1, source_target_pairs={{0,256},{64,320},{128,384},{192,448},{256,0},{320,64},{384,128},{4... | collective-permute-start | bytes 6560 | tf_op jit(solution)/shard_map/ppermute | solution.py:30
Sparse Core Ops, SparseCore 0:
  10.1 81.1 all-gather.1
  141.7 76.1 reduce-scatter.3

commit v2 on v1

--- a/solution.py
+++ b/solution.py
@@ -20,20 +20,37 @@
     return lax.ppermute(shard, axis, pairs)
 
 
-def scan_blocks(parts, axis):
-    size, here = (lax.axis_size(axis), lax.axis_index(axis))
+def psum_doubling(parts, axis):
+    size = lax.axis_size(axis)
     total = [p.astype(jnp.float32) for p in parts]
-    before = [jnp.zeros_like(t) for t in total]
     step = 1
     while step < size:
         pairs = [(i, i ^ step) for i in range(size)]
         got = lax.ppermute(tuple(t.astype(jnp.bfloat16) for t in total), axis, pairs)
-        got = [g.astype(jnp.float32) for g in got]
-        lower = ((here ^ step) < here).astype(jnp.float32)
-        before = [b + lower * g for b, g in zip(before, got)]
-        total = [t + g for t, g in zip(total, got)]
+        total = [t + g.astype(jnp.float32) for t, g in zip(total, got)]
         step *= 2
-    return before, total
+    return total
+
+
+def tail_prefix(tail, tail_seg, axis):
+    size, here = (lax.axis_size(axis), lax.axis_index(axis))
+    seg_before = tail_seg[jnp.maximum(here - 1, 0)]
+    group = tail.astype(jnp.float32)
+    before = jnp.zeros_like(group)
+    step = 1
+    while step < size:
+        pairs = [(i, i ^ step) for i in range(size)]
+        got = lax.ppermute(group.astype(jnp.bfloat16), axis, pairs).astype(jnp.float32)
+        other = here ^ step
+        my_end = (here | (step - 1))
+        other_end = (other | (step - 1))
+        same = (tail_seg[my_end] == tail_seg[other_end]).astype(jnp.float32)
+        earlier = other < here
+        take = (earlier & (tail_seg[other_end] == seg_before)).astype(jnp.float32)
+        before = before + take * got
+        group = jnp.where(earlier, group + same * got, got + same * group)
+        step *= 2
+    return before
 
 
 def taylor_map(values):
@@ -111,11 +128,12 @@
     edge_valid = edge_rows >= starts[:, None]
     match = ((positions[:, None, None] == edge_rows[None]) & edge_valid[None]).astype(jnp.bfloat16)
     contrib_edge = jnp.einsum("tgj,tc->gjc", match, gate_pre, preferred_element_type=jnp.float32)
-    (pre_state, _, _), (all_state, all_norm, all_edge) = scan_blocks(
-        (contrib_state, contrib_norm, contrib_edge), "seq"
-    )
+    block_ends = (jnp.arange(lax.axis_size("seq"), dtype=jnp.int32) + 1) * tok_rows - 1
+    tail_seg = segment_ids(block_ends, ends)
+    seg_last = tail_seg[seq_pos]
+    tail_state = lax.dynamic_index_in_dim(contrib_state, seg_last, axis=1, keepdims=False)
+    carry_state = tail_prefix(tail_state, tail_seg, "seq")
     seg_before = jnp.sum((first_row - 1 >= ends).astype(jnp.int32))
-    carry_state = lax.dynamic_index_in_dim(pre_state, seg_before, axis=1, keepdims=False)
     carried = ((seg == seg_before) & (first_row > 0)).astype(jnp.float32)
     attended = (
         numer
@@ -127,8 +145,11 @@
         attended * inv_rms * gain[None] * jax.nn.silu(gate.reshape(tok_rows, local_heads, HD))
     ).astype(jnp.bfloat16)
     hidden = hidden.reshape(tok_rows, local_cols)
-    product = lax.dot_general(
-        w_out, hidden, (((0,), (1,)), ((), ())), preferred_element_type=jnp.float32
+    product = jnp.einsum(
+        "tk,kgc->gtc",
+        hidden,
+        w_out.reshape(local_cols, lax.axis_size("tp"), -1),
+        preferred_element_type=jnp.float32,
     )
     summed = lax.psum_scatter(
         lax.optimization_barrier(product.astype(jnp.bfloat16))
@@ -137,8 +158,9 @@
         "tp",
         scatter_dimension=0,
         tiled=True,
-    ).astype(jnp.float32)
-    mixed = summed.T.astype(jnp.bfloat16)
+    )
+    mixed = summed.reshape(tok_rows, -1)
+    all_state, all_norm, all_edge = psum_doubling((contrib_state, contrib_norm, contrib_edge), "seq")
     scale = lax.rsqrt(prompt_lens.astype(jnp.float32))
     my_requests = lax.dynamic_slice_in_dim(row_request, seq_pos * SLOTS, SLOTS)
     my_groups = jnp.take(req_group, my_requests)

time: 226 us -> 207 us (0.916)
  waiting for transfers between devices: 141 us -> 113 us
  starting transfers between devices: 30.1 us -> 40.2 us
  between operations: 16.6 us -> 22.9 us
  local copies, waits for them, and re-layouts: 14.6 us -> 8.93 us
  matrix products: 16.2 us -> 12.7 us
    unnamed x3 -> x2, waiting for transfers between devices: 47.3 us -> 0.7 us
    reduce_scatter x0 -> x1, waiting for transfers between devices: none -> 29.4 us  [local(): lax.psum_scatter(lax.optimization_barrier(product.astype(jnp.bfloat16)).a...]
    ppermute x9 -> x12, starting transfers between devices: 27 us -> 38.2 us  [the longest x9 28.1 us: psum_doubling(): lax.ppermute(tuple((t.astype(jnp.bfloat16) for t in total)), axis, pairs)]
    all_gather x1, waiting for transfers between devices: 79 us -> 70.2 us  [local(): lax.all_gather(tokens, 'tp', axis=1, tiled=True)]
    unnamed x35 -> x16, local copies, waits for them, and re-layouts: 8.61 us -> 2.65 us
    dot_general x1 -> x0, matrix products: 4.12 us -> none  [local(): lax.dot_general(w_out, hidden, (((0,), (1,)), ((), ())), preferred_elemen...]
    convert_element_type x11, other arithmetic: 0.38 us -> 2.8 us  [the longest x1 2.39 us: local(): product.astype(jnp.bfloat16)]
    ppermute x9 -> x12, waiting for transfers between devices: 14.2 us -> 13 us  [the longest x9 9.51 us: psum_doubling(): lax.ppermute(tuple((t.astype(jnp.bfloat16) for t in total)), axis, pairs)]
  transfers between devices with their start and end apart: 12 -> 15, of which waited for: 5 -> 7; matrix products, arithmetic and copies ran while one was open for 9% -> 8% of each run, Pallas kernels for 0% -> 0%
where the time goes in v2:
time: 207 us; the launch traced here: 206 us
  waiting for transfers between devices  113 us (55%)
  starting transfers between devices  40.2 us (19%)
  between operations  22.9 us (11%)
  matrix products  12.7 us (6%)
  local copies, waits for them, and re-layouts  8.93 us (4%)
  other arithmetic  7.55 us (4%)
    all_gather x1, waiting for transfers between devices, local(): lax.all_gather(tokens, 'tp', axis=1, tiled=True)  70.2 us
    reduce_scatter x1, waiting for transfers between devices, local(): lax.psum_scatter(lax.optimization_barrier(product.astype(jnp.bfloat16)).a...  29.4 us
    ppermute x9, starting transfers between devices, psum_doubling(): lax.ppermute(tuple((t.astype(jnp.bfloat16) for t in total)), axis, pairs)  28.1 us
    ppermute x3, starting transfers between devices, tail_prefix(): lax.ppermute(group.astype(jnp.bfloat16), axis, pairs).astype(jnp.float32)  10.2 us
    ppermute x9, waiting for transfers between devices, psum_doubling(): lax.ppermute(tuple((t.astype(jnp.bfloat16) for t in total)), axis, pairs)  9.51 us
  transfers between devices with their start and end apart: 15, of which 7 were waited for; matrix products, arithmetic and copies ran while one was open for 8% of the time, Pallas kernels for 0%

profile of v2, /device:TPU:24, one launch (start us, length us, event | category | flops | bytes accessed | tf_op | source)
XLA Modules:
  0.0 205.7 jit_solution(15069101105222260805)
XLA Ops:
  7.2 0.0 copy-start
  7.2 0.0 all-gather.2.cloned.1.call-start
  7.2 0.7 all-gather.2.cloned.1.call-update
  7.9 0.0 reduce-scatter.2.cloned.1.call-start
  8.0 0.8 reduce-window.7
  8.8 0.1 convert_reduce_fusion.2
  8.9 0.7 fusion.89
  18.0 0.1 convert_reduce_fusion.1
  18.1 0.1 convert_reduce_fusion
  18.2 1.3 bitcast_subtract_fusion
  19.5 0.8 slice_bitcast_fusion.4
  20.3 0.7 fusion.73
  21.0 70.2 %all-gather.2.cloned.1.call-done = bf16[1024,1792]{0,1:T(8,128)(2,1)} async-done(((bf16[1024,112]{0,1:T(8,128)(2,1)}), bf16[1024,1792]{0,1:T(8,128)(2,1)}) %all-gather.2.cloned.1.call-update) | async-done | bytes 3670032 | tf_op jit(solution)/shard_map/all_gather | solution.py:81
  91.2 3.2 %fusion.8 = bf16[1024,1,256]{0,2,1:T(8,128)(2,1)S(1)} fusion(bf16[1024,1792]{0,1:T(8,128)(2,1)} %all-gather.2.cloned.1.call-done, bf16[1792,256]{1,0:T(8,128)(2,1)S(1)} %copy-done), kind=kOutput, calls=%fused_computation.16 | convolution fusion | flops 939786240 | bytes 5111808 | tf_op jit(solution)/shard_map/dot_general | solution.py:80
  94.5 1.7 fusion.9
  96.2 0.1 multiply_multiply_fusion.2
  96.3 0.2 maximum_bitcast_fusion
  96.5 3.3 %fusion = f32[4,273,112]{2,1,0:T(8,128)S(1)} fusion(f32[1024,273]{0,1:T(8,128)S(1)} %maximum_bitcast_fusion, f32[1024,4]{0,1:T(4,128)S(1)} %fusion.65, bf16[1024,1,256]{0,2,1:T(8,128)(2,1)} %copy-done.3), kind=kOutput, calls=%fused_computation.6 | convolution fusion | flops 1503989760 | bytes 1853184 | tf_op jit(solution)/shard_map/dot_general | solution.py:119
  99.8 1.9 collective-permute-start
  101.8 1.0 slice_bitcast_fusion
  102.7 0.3 collective-permute-done
  103.0 3.4 %collective-permute-start.1 = (bf16[1,273,112]{2,1,0:T(8,128)(2,1)S(1)}, bf16[1,273,112]{2,1,0:T(8,128)(2,1)S(1)}, u32[]{:S(2)}, u32[]{:S(2)}) collective-permute-start(bf16[1,273,112]{2,1,0:T(8,128)(2,1)S(1)} %fusion.53), channel_id=1, source_target_pairs={{0,128},{64,192},{128,0},{192,64},{256,384},{320,448},{384,256},{4... | collective-permute-start | bytes 183464 | tf_op jit(solution)/shard_map/ppermute | solution.py:43
  106.4 0.8 slice_bitcast_fusion.1
  107.3 1.9 collective-permute-start.3
  109.1 0.2 collective-permute-done.1
  109.3 0.1 fusion.47
  109.4 4.9 %collective-permute-start.2 = (bf16[1,273,112]{2,1,0:T(8,128)(2,1)S(1)}, bf16[1,273,112]{2,1,0:T(8,128)(2,1)S(1)}, u32[]{:S(2)}, u32[]{:S(2)}) collective-permute-start(bf16[1,273,112]{2,1,0:T(8,128)(2,1)S(1)} %fusion.47), channel_id=1, source_target_pairs={{0,256},{64,320},{128,384},{192,448},{256,0},{320,64},{384,128},{4... | collective-permute-start | bytes 183464 | tf_op jit(solution)/shard_map/ppermute | solution.py:43
  114.3 0.1 multiply_multiply_fusion.1
  114.4 3.0 %collective-permute-done.2 = bf16[1,273,112]{2,1,0:T(8,128)(2,1)S(1)} collective-permute-done((bf16[1,273,112]{2,1,0:T(8,128)(2,1)S(1)}, bf16[1,273,112]{2,1,0:T(8,128)(2,1)S(1)}, u32[]{:S(2)}, u32[]{:S(2)}) %collective-permute-start.2) | collective-permute-done | bytes 61184 | tf_op jit(solution)/shard_map/ppermute | solution.py:43
  117.5 1.2 multiply_reduce_fusion
  118.7 1.4 fusion.22
  120.1 2.4 %convert_bitcast_fusion = bf16[16,1024,112]{1,2,0:T(8,128)(2,1)} fusion(f32[1024,16,112]{0,2,1:T(8,128)S(1)} %bitcast.127), kind=kLoop, calls=%fused_computation.11 | loop fusion | flops 1835008 | bytes 11010048 | tf_op jit(solution)/shard_map/convert_element_type | solution.py:155
  122.5 0.0 reduce-scatter.2.cloned.1.call-update
  122.5 0.6 copy-done.5
  123.2 0.1 compare_select_fusion.1
  123.3 0.6 gather_fusion
  123.9 0.1 compare_and_fusion
  124.0 0.6 gather_fusion.2
  124.7 1.2 fusion.90
  125.8 1.9 collective-permute-start.10
  127.8 0.8 fusion.64
  128.5 0.1 convert_bitcast_fusion.1
  128.6 2.4 %collective-permute-start.7 = (bf16[4,1,273]{2,0,1:T(4,128)(2,1)S(1)}, bf16[4,1,273]{2,0,1:T(4,128)(2,1)S(1)}, u32[]{:S(2)}, u32[]{:S(2)}) collective-permute-start(bf16[4,1,273]{2,0,1:T(4,128)(2,1)S(1)} %convert_bitcast_fusion.2), channel_id=1, source_target_pairs={{0,64},{64,0},{128,192},{192,128},{256,320},{320,256},{384,448},{4... | collective-permute-start | bytes 6560 | tf_op jit(solution)/shard_map/ppermute | solution.py:29
  131.1 1.9 collective-permute-start.4
  133.0 3.7 %collective-permute-start.11 = (bf16[4,2,112]{2,0,1:T(4,128)(2,1)S(1)}, bf16[4,2,112]{2,0,1:T(4,128)(2,1)S(1)}, u32[]{:S(2)}, u32[]{:S(2)}) collective-permute-start(bf16[4,2,112]{2,0,1:T(4,128)(2,1)S(1)} %fusion.77), channel_id=1, source_target_pairs={{0,128},{64,192},{128,0},{192,64},{256,384},{320,448},{384,256},{4... | collective-permute-start | bytes 5384 | tf_op jit(solution)/shard_map/ppermute | solution.py:29
  136.8 2.1 %collective-permute-start.8 = (bf16[4,1,273]{2,0,1:T(4,128)(2,1)S(1)}, bf16[4,1,273]{2,0,1:T(4,128)(2,1)S(1)}, u32[]{:S(2)}, u32[]{:S(2)}) collective-permute-start(bf16[4,1,273]{2,0,1:T(4,128)(2,1)S(1)} %fusion.78), channel_id=1, source_target_pairs={{0,128},{64,192},{128,0},{192,64},{256,384},{320,448},{384,256},{4... | collective-permute-start | bytes 6560 | tf_op jit(solution)/shard_map/ppermute | solution.py:29
  138.9 4.9 %collective-permute-start.12 = (bf16[4,2,112]{2,0,1:T(4,128)(2,1)S(1)}, bf16[4,2,112]{2,0,1:T(4,128)(2,1)S(1)}, u32[]{:S(2)}, u32[]{:S(2)}) collective-permute-start(bf16[4,2,112]{2,0,1:T(4,128)(2,1)S(1)} %fusion.79), channel_id=1, source_target_pairs={{0,256},{64,320},{128,384},{192,448},{256,0},{320,64},{384,128},{4... | collective-permute-start | bytes 5384 | tf_op jit(solution)/shard_map/ppermute | solution.py:29
  143.8 2.5 %collective-permute-start.9 = (bf16[4,1,273]{2,0,1:T(4,128)(2,1)S(1)}, bf16[4,1,273]{2,0,1:T(4,128)(2,1)S(1)}, u32[]{:S(2)}, u32[]{:S(2)}) collective-permute-start(bf16[4,1,273]{2,0,1:T(4,128)(2,1)S(1)} %fusion.76), channel_id=1, source_target_pairs={{0,256},{64,320},{128,384},{192,448},{256,0},{320,64},{384,128},{4... | collective-permute-start | bytes 6560 | tf_op jit(solution)/shard_map/ppermute | solution.py:29
  146.3 0.1 fusion.35
  146.4 3.7 %collective-permute-start.5 = (bf16[1,4,273,112]{3,2,1,0:T(8,128)(2,1)S(1)}, bf16[1,4,273,112]{3,2,1,0:T(8,128)(2,1)S(1)}, u32[]{:S(2)}, u32[]{:S(2)}) collective-permute-start(bf16[1,4,273,112]{3,2,1,0:T(8,128)(2,1)S(1)} %fusion.35), channel_id=1, source_target_pairs={{0,128},{64,192},{128,0},{192,64},{256,384},{320,448},{384,256},{4... | collective-permute-start | bytes 733832 | tf_op jit(solution)/shard_map/ppermute | solution.py:29
  150.1 0.6 gather_fusion.4
  150.7 0.7 select_convert_fusion
  151.4 5.0 %collective-permute-done.5 = bf16[1,4,273,112]{3,2,1,0:T(8,128)(2,1)S(1)} collective-permute-done((bf16[1,4,273,112]{3,2,1,0:T(8,128)(2,1)S(1)}, bf16[1,4,273,112]{3,2,1,0:T(8,128)(2,1)S(1)}, u32[]{:S(2)}, u32[]{:S(2)}) %collective-permute-start.5) | collective-permute-done | bytes 244640 | tf_op jit(solution)/shard_map/ppermute | solution.py:29
  156.4 0.1 fusion.18
  156.5 4.9 %collective-permute-start.6 = (bf16[1,4,273,112]{3,2,1,0:T(8,128)(2,1)S(1)}, bf16[1,4,273,112]{3,2,1,0:T(8,128)(2,1)S(1)}, u32[]{:S(2)}, u32[]{:S(2)}) collective-permute-start(bf16[1,4,273,112]{3,2,1,0:T(8,128)(2,1)S(1)} %fusion.18), channel_id=1, source_target_pairs={{0,256},{64,320},{128,384},{192,448},{256,0},{320,64},{384,128},{4... | collective-permute-start | bytes 733832 | tf_op jit(solution)/shard_map/ppermute | solution.py:29
  161.4 0.6 gather_fusion.3
  162.0 0.1 fusion.72
  162.1 0.6 copy.23
  162.7 4.5 %collective-permute-done.6 = bf16[1,4,273,112]{3,2,1,0:T(8,128)(2,1)S(1)} collective-permute-done((bf16[1,4,273,112]{3,2,1,0:T(8,128)(2,1)S(1)}, bf16[1,4,273,112]{3,2,1,0:T(8,128)(2,1)S(1)}, u32[]{:S(2)}, u32[]{:S(2)}) %collective-permute-start.6) | collective-permute-done | bytes 244640 | tf_op jit(solution)/shard_map/ppermute | solution.py:29
  167.2 0.1 add_bitcast_fusion
  167.3 0.6 gather_fusion.1
  167.9 0.1 fusion.16
  168.0 1.4 copy.22
  169.4 29.4 %reduce-scatter.2.cloned.1.call-done = bf16[1,1024,112]{1,2,0:T(8,128)(2,1)} async-done(((bf16[16,1024,112]{1,2,0:T(8,128)(2,1)}), bf16[1,1024,112]{1,2,0:T(8,128)(2,1)}) %reduce-scatter.2.cloned.1.call-update) | async-done | bytes 229392 | tf_op jit(solution)/shard_map/reduce_scatter | solution.py:154
  (43 shorter events, 0.3 us)
Async XLA Ops:
  7.2 84.1 %copy-start = (bf16[1792,256]{1,0:T(8,128)(2,1)S(1)}, bf16[1792,256]{1,0:T(8,128)(2,1)}, u32[]{:S(2)}) copy-start(bf16[1792,256]{1,0:T(8,128)(2,1)} %param.9) | copy-start | bytes 2752516
  7.2 84.0 %all-gather.2.cloned.1.call-start = ((), (), s32[]{:S(2)}) async-start(), calls=%async_computation.1 | async-start | bytes 3899392 | tf_op jit(solution)/shard_map/all_gather | solution.py:81
  7.9 190.9 %reduce-scatter.2.cloned.1.call-start = ((), (), s32[]{:S(2)}) async-start(), calls=%async_computation.2 | async-start | bytes 3899392 | tf_op jit(solution)/shard_map/reduce_scatter | solution.py:154
  94.4 1.7 copy-start.3
  96.5 22.3 %copy-start.2 = (bf16[112,1792]{1,0:T(8,128)(2,1)S(1)}, bf16[112,1792]{1,0:T(8,128)(2,1)}, u32[]{:S(2)}) copy-start(bf16[112,1792]{1,0:T(8,128)(2,1)} %param.12) | copy-start | bytes 1204228
  96.5 22.3 %copy-start.4 = (f32[112]{0:T(128)S(1)}, f32[112]{0:T(128)}, u32[]{:S(2)}) copy-start(f32[112]{0:T(128)} %param.11) | copy-start | bytes 1348
  99.8 3.2 %collective-permute-start = (bf16[1,273,112]{2,1,0:T(8,128)(2,1)S(1)}, bf16[1,273,112]{2,1,0:T(8,128)(2,1)S(1)}, u32[]{:S(2)}, u32[]{:S(2)}) collective-permute-start(bf16[1,273,112]{2,1,0:T(8,128)(2,1)S(1)} %dynamic-slice_convert_fusion), channel_id=1, source_target_pairs={{0,64},{64,0},{128,192},{192,128},{256,320},{320,256},{384,448},{4... | collective-permute-start | bytes 183464 | tf_op jit(solution)/shard_map/ppermute | solution.py:43
  103.0 6.3 %collective-permute-start.1 = (bf16[1,273,112]{2,1,0:T(8,128)(2,1)S(1)}, bf16[1,273,112]{2,1,0:T(8,128)(2,1)S(1)}, u32[]{:S(2)}, u32[]{:S(2)}) collective-permute-start(bf16[1,273,112]{2,1,0:T(8,128)(2,1)S(1)} %fusion.53), channel_id=1, source_target_pairs={{0,128},{64,192},{128,0},{192,64},{256,384},{320,448},{384,256},{4... | collective-permute-start | bytes 183464 | tf_op jit(solution)/shard_map/ppermute | solution.py:43
  107.3 11.5 %collective-permute-start.3 = (bf16[2,112]{0,1:T(8,128)(2,1)S(1)}, bf16[2,112]{0,1:T(8,128)(2,1)S(1)}, u32[]{:S(2)}, u32[]{:S(2)}) collective-permute-start(bf16[2,112]{0,1:T(8,128)(2,1)S(1)} %slice_bitcast_fusion.1), channel_id=1, source_target_pairs={{0,64},{64,128},{128,192},{192,256},{256,320},{320,384},{384,448},... | collective-permute-start | bytes 1352 | tf_op jit(solution)/shard_map/ppermute | solution.py:20
  109.4 8.1 %collective-permute-start.2 = (bf16[1,273,112]{2,1,0:T(8,128)(2,1)S(1)}, bf16[1,273,112]{2,1,0:T(8,128)(2,1)S(1)}, u32[]{:S(2)}, u32[]{:S(2)}) collective-permute-start(bf16[1,273,112]{2,1,0:T(8,128)(2,1)S(1)} %fusion.47), channel_id=1, source_target_pairs={{0,256},{64,320},{128,384},{192,448},{256,0},{320,64},{384,128},{4... | collective-permute-start | bytes 183464 | tf_op jit(solution)/shard_map/ppermute | solution.py:43
  122.5 0.7 copy-start.5
  122.5 0.7 copy-start.1
  122.5 1.5 copy-start.6
  125.8 7.1 %collective-permute-start.10 = (bf16[4,2,112]{2,0,1:T(4,128)(2,1)S(1)}, bf16[4,2,112]{2,0,1:T(4,128)(2,1)S(1)}, u32[]{:S(2)}, u32[]{:S(2)}) collective-permute-start(bf16[4,2,112]{2,0,1:T(4,128)(2,1)S(1)} %get-tuple-element.40), channel_id=1, source_target_pairs={{0,64},{64,0},{128,192},{192,128},{256,320},{320,256},{384,448},{4... | collective-permute-start | bytes 5384 | tf_op jit(solution)/shard_map/ppermute | solution.py:29
  128.6 8.1 %collective-permute-start.7 = (bf16[4,1,273]{2,0,1:T(4,128)(2,1)S(1)}, bf16[4,1,273]{2,0,1:T(4,128)(2,1)S(1)}, u32[]{:S(2)}, u32[]{:S(2)}) collective-permute-start(bf16[4,1,273]{2,0,1:T(4,128)(2,1)S(1)} %convert_bitcast_fusion.2), channel_id=1, source_target_pairs={{0,64},{64,0},{128,192},{192,128},{256,320},{320,256},{384,448},{4... | collective-permute-start | bytes 6560 | tf_op jit(solution)/shard_map/ppermute | solution.py:29
  131.1 15.2 %collective-permute-start.4 = (bf16[1,4,273,112]{3,2,1,0:T(8,128)(2,1)S(1)}, bf16[1,4,273,112]{3,2,1,0:T(8,128)(2,1)S(1)}, u32[]{:S(2)}, u32[]{:S(2)}) collective-permute-start(bf16[1,4,273,112]{3,2,1,0:T(8,128)(2,1)S(1)} %convert_bitcast_fusion.1), channel_id=1, source_target_pairs={{0,64},{64,0},{128,192},{192,128},{256,320},{320,256},{384,448},{4... | collective-permute-start | bytes 733832 | tf_op jit(solution)/shard_map/ppermute | solution.py:29
  133.0 5.9 %collective-permute-start.11 = (bf16[4,2,112]{2,0,1:T(4,128)(2,1)S(1)}, bf16[4,2,112]{2,0,1:T(4,128)(2,1)S(1)}, u32[]{:S(2)}, u32[]{:S(2)}) collective-permute-start(bf16[4,2,112]{2,0,1:T(4,128)(2,1)S(1)} %fusion.77), channel_id=1, source_target_pairs={{0,128},{64,192},{128,0},{192,64},{256,384},{320,448},{384,256},{4... | collective-permute-start | bytes 5384 | tf_op jit(solution)/shard_map/ppermute | solution.py:29
  136.8 7.1 %collective-permute-start.8 = (bf16[4,1,273]{2,0,1:T(4,128)(2,1)S(1)}, bf16[4,1,273]{2,0,1:T(4,128)(2,1)S(1)}, u32[]{:S(2)}, u32[]{:S(2)}) collective-permute-start(bf16[4,1,273]{2,0,1:T(4,128)(2,1)S(1)} %fusion.78), channel_id=1, source_target_pairs={{0,128},{64,192},{128,0},{192,64},{256,384},{320,448},{384,256},{4... | collective-permute-start | bytes 6560 | tf_op jit(solution)/shard_map/ppermute | solution.py:29
  138.9 11.2 %collective-permute-start.12 = (bf16[4,2,112]{2,0,1:T(4,128)(2,1)S(1)}, bf16[4,2,112]{2,0,1:T(4,128)(2,1)S(1)}, u32[]{:S(2)}, u32[]{:S(2)}) collective-permute-start(bf16[4,2,112]{2,0,1:T(4,128)(2,1)S(1)} %fusion.79), channel_id=1, source_target_pairs={{0,256},{64,320},{128,384},{192,448},{256,0},{320,64},{384,128},{4... | collective-permute-start | bytes 5384 | tf_op jit(solution)/shard_map/ppermute | solution.py:29
  143.8 17.6 %collective-permute-start.9 = (bf16[4,1,273]{2,0,1:T(4,128)(2,1)S(1)}, bf16[4,1,273]{2,0,1:T(4,128)(2,1)S(1)}, u32[]{:S(2)}, u32[]{:S(2)}) collective-permute-start(bf16[4,1,273]{2,0,1:T(4,128)(2,1)S(1)} %fusion.76), channel_id=1, source_target_pairs={{0,256},{64,320},{128,384},{192,448},{256,0},{320,64},{384,128},{4... | collective-permute-start | bytes 6560 | tf_op jit(solution)/shard_map/ppermute | solution.py:29
  146.4 10.0 %collective-permute-start.5 = (bf16[1,4,273,112]{3,2,1,0:T(8,128)(2,1)S(1)}, bf16[1,4,273,112]{3,2,1,0:T(8,128)(2,1)S(1)}, u32[]{:S(2)}, u32[]{:S(2)}) collective-permute-start(bf16[1,4,273,112]{3,2,1,0:T(8,128)(2,1)S(1)} %fusion.35), channel_id=1, source_target_pairs={{0,128},{64,192},{128,0},{192,64},{256,384},{320,448},{384,256},{4... | collective-permute-start | bytes 733832 | tf_op jit(solution)/shard_map/ppermute | solution.py:29
  156.5 10.7 %collective-permute-start.6 = (bf16[1,4,273,112]{3,2,1,0:T(8,128)(2,1)S(1)}, bf16[1,4,273,112]{3,2,1,0:T(8,128)(2,1)S(1)}, u32[]{:S(2)}, u32[]{:S(2)}) collective-permute-start(bf16[1,4,273,112]{3,2,1,0:T(8,128)(2,1)S(1)} %fusion.18), channel_id=1, source_target_pairs={{0,256},{64,320},{128,384},{192,448},{256,0},{320,64},{384,128},{4... | collective-permute-start | bytes 733832 | tf_op jit(solution)/shard_map/ppermute | solution.py:29
Sparse Core Ops, SparseCore 0:
  10.1 81.1 all-gather.1
  122.7 76.1 reduce-scatter.1

commit v3 on v2

--- a/solution.py
+++ b/solution.py
@@ -132,8 +132,11 @@
     tail_seg = segment_ids(block_ends, ends)
     seg_last = tail_seg[seq_pos]
     tail_state = lax.dynamic_index_in_dim(contrib_state, seg_last, axis=1, keepdims=False)
-    carry_state = tail_prefix(tail_state, tail_seg, "seq")
     seg_before = jnp.sum((first_row - 1 >= ends).astype(jnp.int32))
+    tails = lax.all_gather(tail_state.astype(jnp.bfloat16), "seq").astype(jnp.float32)
+    block_index = jnp.arange(lax.axis_size("seq"), dtype=jnp.int32)
+    chained = ((block_index < seq_pos) & (tail_seg == seg_before)).astype(jnp.float32)
+    carry_state = jnp.sum(chained.reshape((-1,) + (1,) * (tails.ndim - 1)) * tails, axis=0)
     carried = ((seg == seg_before) & (first_row > 0)).astype(jnp.float32)
     attended = (
         numer

time: 207 us -> 204 us (0.986)
  blocking collectives: 0 us -> 14.3 us
  starting transfers between devices: 40.2 us -> 27.9 us
  between operations: 22.9 us -> 16.4 us
  waiting for transfers between devices: 113 us -> 117 us
    all_gather x0 -> x1, blocking collectives: none -> 14.3 us  [local(): lax.all_gather(tail_state.astype(jnp.bfloat16), 'seq').astype(jnp.float32)]
    ppermute x3 -> x0, starting transfers between devices: 10.2 us -> none  [tail_prefix(): lax.ppermute(group.astype(jnp.bfloat16), axis, pairs).astype(jnp.float32)]
    all_gather x1, waiting for transfers between devices: 70.2 us -> 76.1 us  [local(): lax.all_gather(tokens, 'tp', axis=1, tiled=True)]
    ppermute x3 -> x0, waiting for transfers between devices: 3.5 us -> none  [tail_prefix(): lax.ppermute(group.astype(jnp.bfloat16), axis, pairs).astype(jnp.float32)]
  transfers between devices with their start and end apart: 15 -> 12, of which waited for: 7 -> 4; matrix products, arithmetic and copies ran while one was open for 8% -> 9% of each run, Pallas kernels for 0% -> 0%
where the time goes in v3:
time: 204 us; the launch traced here: 203 us
  waiting for transfers between devices  117 us (57%)
  starting transfers between devices  27.9 us (14%)
  between operations  16.4 us (8%)
  blocking collectives  14.3 us (7%)
  matrix products  12.7 us (6%)
  other arithmetic  8.29 us (4%)
  local copies, waits for them, and re-layouts  7.16 us (4%)
    all_gather x1, waiting for transfers between devices, local(): lax.all_gather(tokens, 'tp', axis=1, tiled=True)  76.1 us
    reduce_scatter x1, waiting for transfers between devices, local(): lax.psum_scatter(lax.optimization_barrier(product.astype(jnp.bfloat16)).a...  29 us
    ppermute x9, starting transfers between devices, psum_doubling(): lax.ppermute(tuple((t.astype(jnp.bfloat16) for t in total)), axis, pairs)  26.6 us
    all_gather x1, blocking collectives, local(): lax.all_gather(tail_state.astype(jnp.bfloat16), 'seq').astype(jnp.float32)  14.3 us
    ppermute x9, waiting for transfers between devices, psum_doubling(): lax.ppermute(tuple((t.astype(jnp.bfloat16) for t in total)), axis, pairs)  10.7 us
  transfers between devices with their start and end apart: 12, of which 4 were waited for; matrix products, arithmetic and copies ran while one was open for 9% of the time, Pallas kernels for 0%

profile of v3, /device:TPU:24, one launch (start us, length us, event | category | flops | bytes accessed | tf_op | source)
XLA Modules:
  0.0 203.3 jit_solution(10032742969712793396)
XLA Ops:
  7.2 0.0 copy-start
  7.2 0.0 all-gather.3.cloned.1.call-start
  7.2 0.7 all-gather.3.cloned.1.call-update
  7.9 0.0 reduce-scatter.2.cloned.1.call-start
  8.0 0.8 reduce-window.7
  8.8 0.1 convert_reduce_fusion.2
  8.9 0.6 dynamic_slice.8
  11.5 0.1 convert_reduce_fusion.1
  11.5 0.1 convert_reduce_fusion
  11.6 1.3 bitcast_subtract_fusion
  12.9 0.6 and_convert_fusion.1
  13.6 0.8 slice_bitcast_fusion.4
  14.4 0.7 fusion.59
  15.1 76.1 %all-gather.3.cloned.1.call-done = bf16[1024,1792]{0,1:T(8,128)(2,1)} async-done(((bf16[1024,112]{0,1:T(8,128)(2,1)}), bf16[1024,1792]{0,1:T(8,128)(2,1)}) %all-gather.3.cloned.1.call-update) | async-done | bytes 3670032 | tf_op jit(solution)/shard_map/all_gather | solution.py:81
  91.2 3.2 %fusion.8 = bf16[1024,1,256]{0,2,1:T(8,128)(2,1)S(1)} fusion(bf16[1024,1792]{0,1:T(8,128)(2,1)} %all-gather.3.cloned.1.call-done, bf16[1792,256]{1,0:T(8,128)(2,1)S(1)} %copy-done), kind=kOutput, calls=%fused_computation.16 | convolution fusion | flops 939786240 | bytes 5111808 | tf_op jit(solution)/shard_map/dot_general | solution.py:80
  94.4 0.0 copy-start.3
  94.4 0.1 slice_bitcast_fusion.1
  94.6 1.7 fusion.9
  96.3 1.3 collective-permute-start
  97.6 0.1 multiply_multiply_fusion.1
  97.7 0.1 multiply_multiply_fusion.2
  97.9 0.0 copy-start.2
  97.9 0.0 copy-start.4
  97.9 0.2 maximum_bitcast_fusion
  98.0 3.3 %fusion = f32[4,273,112]{2,1,0:T(8,128)S(1)} fusion(f32[1024,273]{0,1:T(8,128)S(1)} %maximum_bitcast_fusion, f32[1024,4]{0,1:T(4,128)S(1)} %fusion.51, bf16[1024,1,256]{0,2,1:T(8,128)(2,1)} %copy-done.3), kind=kOutput, calls=%fused_computation.6 | convolution fusion | flops 1503989760 | bytes 1853184 | tf_op jit(solution)/shard_map/dot_general | solution.py:119
  101.3 14.3 %all-gather = bf16[8,273,112]{2,1,0:T(8,128)(2,1)S(1)} all-gather(bf16[1,273,112]{2,1,0:T(8,128)(2,1)S(1)} %dynamic-slice_convert_fusion), channel_id=2, replica_groups=mesh['seq'=8,'tp'=16,'req'=4] {'seq'}, dimensions={0}, use_global_device_ids=true | all-gather | bytes 550368 | tf_op jit(solution)/shard_map/all_gather | solution.py:136
  115.6 0.2 fusion.15
  115.8 1.2 multiply_reduce_fusion
  117.1 1.4 fusion.23
  118.5 2.4 %convert_bitcast_fusion = bf16[16,1024,112]{1,2,0:T(8,128)(2,1)} fusion(f32[1024,16,112]{0,2,1:T(8,128)S(1)} %bitcast.121), kind=kLoop, calls=%fused_computation.11 | loop fusion | flops 1835008 | bytes 11010048 | tf_op jit(solution)/shard_map/convert_element_type | solution.py:158
  120.9 0.0 reduce-scatter.2.cloned.1.call-update
  120.9 0.6 copy-done.5
  121.5 0.1 compare_select_fusion.1
  121.6 0.6 gather_fusion
  122.2 0.1 compare_and_fusion
  122.4 0.6 gather_fusion.2
  123.0 1.2 fusion.75
  124.2 2.3 %collective-permute-start.7 = (bf16[4,2,112]{2,0,1:T(4,128)(2,1)S(1)}, bf16[4,2,112]{2,0,1:T(4,128)(2,1)S(1)}, u32[]{:S(2)}, u32[]{:S(2)}) collective-permute-start(bf16[4,2,112]{2,0,1:T(4,128)(2,1)S(1)} %get-tuple-element.38), channel_id=1, source_target_pairs={{0,64},{64,0},{128,192},{192,128},{256,320},{320,256},{384,448},{4... | collective-permute-start | bytes 5384 | tf_op jit(solution)/shard_map/ppermute | solution.py:29
  126.5 0.8 fusion.50
  127.2 0.1 convert_bitcast_fusion.1
  127.3 2.1 %collective-permute-start.4 = (bf16[4,1,273]{2,0,1:T(4,128)(2,1)S(1)}, bf16[4,1,273]{2,0,1:T(4,128)(2,1)S(1)}, u32[]{:S(2)}, u32[]{:S(2)}) collective-permute-start(bf16[4,1,273]{2,0,1:T(4,128)(2,1)S(1)} %convert_bitcast_fusion.2), channel_id=1, source_target_pairs={{0,64},{64,0},{128,192},{192,128},{256,320},{320,256},{384,448},{4... | collective-permute-start | bytes 6560 | tf_op jit(solution)/shard_map/ppermute | solution.py:29
  129.4 2.3 %collective-permute-start.1 = (bf16[1,4,273,112]{3,2,1,0:T(8,128)(2,1)S(1)}, bf16[1,4,273,112]{3,2,1,0:T(8,128)(2,1)S(1)}, u32[]{:S(2)}, u32[]{:S(2)}) collective-permute-start(bf16[1,4,273,112]{3,2,1,0:T(8,128)(2,1)S(1)} %convert_bitcast_fusion.1), channel_id=1, source_target_pairs={{0,64},{64,0},{128,192},{192,128},{256,320},{320,256},{384,448},{4... | collective-permute-start | bytes 733832 | tf_op jit(solution)/shard_map/ppermute | solution.py:29
  131.7 0.0 collective-permute-done.7
  131.7 2.9 %collective-permute-start.8 = (bf16[4,2,112]{2,0,1:T(4,128)(2,1)S(1)}, bf16[4,2,112]{2,0,1:T(4,128)(2,1)S(1)}, u32[]{:S(2)}, u32[]{:S(2)}) collective-permute-start(bf16[4,2,112]{2,0,1:T(4,128)(2,1)S(1)} %fusion.63), channel_id=1, source_target_pairs={{0,128},{64,192},{128,0},{192,64},{256,384},{320,448},{384,256},{4... | collective-permute-start | bytes 5384 | tf_op jit(solution)/shard_map/ppermute | solution.py:29
  134.6 0.0 collective-permute-done.4
  134.6 2.9 %collective-permute-start.5 = (bf16[4,1,273]{2,0,1:T(4,128)(2,1)S(1)}, bf16[4,1,273]{2,0,1:T(4,128)(2,1)S(1)}, u32[]{:S(2)}, u32[]{:S(2)}) collective-permute-start(bf16[4,1,273]{2,0,1:T(4,128)(2,1)S(1)} %fusion.64), channel_id=1, source_target_pairs={{0,128},{64,192},{128,0},{192,64},{256,384},{320,448},{384,256},{4... | collective-permute-start | bytes 6560 | tf_op jit(solution)/shard_map/ppermute | solution.py:29
  137.6 3.6 %collective-permute-start.9 = (bf16[4,2,112]{2,0,1:T(4,128)(2,1)S(1)}, bf16[4,2,112]{2,0,1:T(4,128)(2,1)S(1)}, u32[]{:S(2)}, u32[]{:S(2)}) collective-permute-start(bf16[4,2,112]{2,0,1:T(4,128)(2,1)S(1)} %fusion.65), channel_id=1, source_target_pairs={{0,256},{64,320},{128,384},{192,448},{256,0},{320,64},{384,128},{4... | collective-permute-start | bytes 5384 | tf_op jit(solution)/shard_map/ppermute | solution.py:29
  141.2 3.8 %collective-permute-start.6 = (bf16[4,1,273]{2,0,1:T(4,128)(2,1)S(1)}, bf16[4,1,273]{2,0,1:T(4,128)(2,1)S(1)}, u32[]{:S(2)}, u32[]{:S(2)}) collective-permute-start(bf16[4,1,273]{2,0,1:T(4,128)(2,1)S(1)} %fusion.62), channel_id=1, source_target_pairs={{0,256},{64,320},{128,384},{192,448},{256,0},{320,64},{384,128},{4... | collective-permute-start | bytes 6560 | tf_op jit(solution)/shard_map/ppermute | solution.py:29
  145.0 0.1 fusion.36
  145.1 2.9 %collective-permute-start.2 = (bf16[1,4,273,112]{3,2,1,0:T(8,128)(2,1)S(1)}, bf16[1,4,273,112]{3,2,1,0:T(8,128)(2,1)S(1)}, u32[]{:S(2)}, u32[]{:S(2)}) collective-permute-start(bf16[1,4,273,112]{3,2,1,0:T(8,128)(2,1)S(1)} %fusion.36), channel_id=1, source_target_pairs={{0,128},{64,192},{128,0},{192,64},{256,384},{320,448},{384,256},{4... | collective-permute-start | bytes 733832 | tf_op jit(solution)/shard_map/ppermute | solution.py:29
  148.0 0.6 gather_fusion.4
  148.6 0.7 select_convert_fusion
  149.3 5.5 %collective-permute-done.2 = bf16[1,4,273,112]{3,2,1,0:T(8,128)(2,1)S(1)} collective-permute-done((bf16[1,4,273,112]{3,2,1,0:T(8,128)(2,1)S(1)}, bf16[1,4,273,112]{3,2,1,0:T(8,128)(2,1)S(1)}, u32[]{:S(2)}, u32[]{:S(2)}) %collective-permute-start.2) | collective-permute-done | bytes 244640 | tf_op jit(solution)/shard_map/ppermute | solution.py:29
  154.7 0.1 fusion.19
  154.9 3.9 %collective-permute-start.3 = (bf16[1,4,273,112]{3,2,1,0:T(8,128)(2,1)S(1)}, bf16[1,4,273,112]{3,2,1,0:T(8,128)(2,1)S(1)}, u32[]{:S(2)}, u32[]{:S(2)}) collective-permute-start(bf16[1,4,273,112]{3,2,1,0:T(8,128)(2,1)S(1)} %fusion.19), channel_id=1, source_target_pairs={{0,256},{64,320},{128,384},{192,448},{256,0},{320,64},{384,128},{4... | collective-permute-start | bytes 733832 | tf_op jit(solution)/shard_map/ppermute | solution.py:29
  158.7 0.6 gather_fusion.3
  159.3 0.1 fusion.58
  159.4 0.6 copy.27
  160.0 5.2 %collective-permute-done.3 = bf16[1,4,273,112]{3,2,1,0:T(8,128)(2,1)S(1)} collective-permute-done((bf16[1,4,273,112]{3,2,1,0:T(8,128)(2,1)S(1)}, bf16[1,4,273,112]{3,2,1,0:T(8,128)(2,1)S(1)}, u32[]{:S(2)}, u32[]{:S(2)}) %collective-permute-start.3) | collective-permute-done | bytes 244640 | tf_op jit(solution)/shard_map/ppermute | solution.py:29
  165.2 0.1 add_bitcast_fusion
  165.3 0.6 gather_fusion.1
  165.9 0.1 fusion.17
  166.0 1.4 copy.26
  167.4 29.0 %reduce-scatter.2.cloned.1.call-done = bf16[1,1024,112]{1,2,0:T(8,128)(2,1)} async-done(((bf16[16,1024,112]{1,2,0:T(8,128)(2,1)}), bf16[1,1024,112]{1,2,0:T(8,128)(2,1)}) %reduce-scatter.2.cloned.1.call-update) | async-done | bytes 229392 | tf_op jit(solution)/shard_map/reduce_scatter | solution.py:157
  (38 shorter events, 0.2 us)
Async XLA Ops:
  7.2 84.1 %copy-start = (bf16[1792,256]{1,0:T(8,128)(2,1)S(1)}, bf16[1792,256]{1,0:T(8,128)(2,1)}, u32[]{:S(2)}) copy-start(bf16[1792,256]{1,0:T(8,128)(2,1)} %param.9) | copy-start | bytes 2752516
  7.2 84.0 %all-gather.3.cloned.1.call-start = ((), (), s32[]{:S(2)}) async-start(), calls=%async_computation.1 | async-start | bytes 3899392 | tf_op jit(solution)/shard_map/all_gather | solution.py:81
  7.9 188.5 %reduce-scatter.2.cloned.1.call-start = ((), (), s32[]{:S(2)}) async-start(), calls=%async_computation.2 | async-start | bytes 3899392 | tf_op jit(solution)/shard_map/reduce_scatter | solution.py:157
  94.4 1.8 copy-start.3
  96.3 20.8 %collective-permute-start = (bf16[2,112]{0,1:T(8,128)(2,1)S(1)}, bf16[2,112]{0,1:T(8,128)(2,1)S(1)}, u32[]{:S(2)}, u32[]{:S(2)}) collective-permute-start(bf16[2,112]{0,1:T(8,128)(2,1)S(1)} %slice_bitcast_fusion.1), channel_id=1, source_target_pairs={{0,64},{64,128},{128,192},{192,256},{256,320},{320,384},{384,448},... | collective-permute-start | bytes 1352 | tf_op jit(solution)/shard_map/ppermute | solution.py:20
  97.9 19.2 %copy-start.2 = (bf16[112,1792]{1,0:T(8,128)(2,1)S(1)}, bf16[112,1792]{1,0:T(8,128)(2,1)}, u32[]{:S(2)}) copy-start(bf16[112,1792]{1,0:T(8,128)(2,1)} %param.12) | copy-start | bytes 1204228
  97.9 19.2 %copy-start.4 = (f32[112]{0:T(128)S(1)}, f32[112]{0:T(128)}, u32[]{:S(2)}) copy-start(f32[112]{0:T(128)} %param.11) | copy-start | bytes 1348
  120.9 0.7 copy-start.5
  120.9 0.7 copy-start.1
  120.9 1.5 copy-start.6
  124.2 7.5 %collective-permute-start.7 = (bf16[4,2,112]{2,0,1:T(4,128)(2,1)S(1)}, bf16[4,2,112]{2,0,1:T(4,128)(2,1)S(1)}, u32[]{:S(2)}, u32[]{:S(2)}) collective-permute-start(bf16[4,2,112]{2,0,1:T(4,128)(2,1)S(1)} %get-tuple-element.38), channel_id=1, source_target_pairs={{0,64},{64,0},{128,192},{192,128},{256,320},{320,256},{384,448},{4... | collective-permute-start | bytes 5384 | tf_op jit(solution)/shard_map/ppermute | solution.py:29
  127.3 7.3 %collective-permute-start.4 = (bf16[4,1,273]{2,0,1:T(4,128)(2,1)S(1)}, bf16[4,1,273]{2,0,1:T(4,128)(2,1)S(1)}, u32[]{:S(2)}, u32[]{:S(2)}) collective-permute-start(bf16[4,1,273]{2,0,1:T(4,128)(2,1)S(1)} %convert_bitcast_fusion.2), channel_id=1, source_target_pairs={{0,64},{64,0},{128,192},{192,128},{256,320},{320,256},{384,448},{4... | collective-permute-start | bytes 6560 | tf_op jit(solution)/shard_map/ppermute | solution.py:29
  129.4 15.6 %collective-permute-start.1 = (bf16[1,4,273,112]{3,2,1,0:T(8,128)(2,1)S(1)}, bf16[1,4,273,112]{3,2,1,0:T(8,128)(2,1)S(1)}, u32[]{:S(2)}, u32[]{:S(2)}) collective-permute-start(bf16[1,4,273,112]{3,2,1,0:T(8,128)(2,1)S(1)} %convert_bitcast_fusion.1), channel_id=1, source_target_pairs={{0,64},{64,0},{128,192},{192,128},{256,320},{320,256},{384,448},{4... | collective-permute-start | bytes 733832 | tf_op jit(solution)/shard_map/ppermute | solution.py:29
  131.7 5.9 %collective-permute-start.8 = (bf16[4,2,112]{2,0,1:T(4,128)(2,1)S(1)}, bf16[4,2,112]{2,0,1:T(4,128)(2,1)S(1)}, u32[]{:S(2)}, u32[]{:S(2)}) collective-permute-start(bf16[4,2,112]{2,0,1:T(4,128)(2,1)S(1)} %fusion.63), channel_id=1, source_target_pairs={{0,128},{64,192},{128,0},{192,64},{256,384},{320,448},{384,256},{4... | collective-permute-start | bytes 5384 | tf_op jit(solution)/shard_map/ppermute | solution.py:29
  134.6 6.5 %collective-permute-start.5 = (bf16[4,1,273]{2,0,1:T(4,128)(2,1)S(1)}, bf16[4,1,273]{2,0,1:T(4,128)(2,1)S(1)}, u32[]{:S(2)}, u32[]{:S(2)}) collective-permute-start(bf16[4,1,273]{2,0,1:T(4,128)(2,1)S(1)} %fusion.64), channel_id=1, source_target_pairs={{0,128},{64,192},{128,0},{192,64},{256,384},{320,448},{384,256},{4... | collective-permute-start | bytes 6560 | tf_op jit(solution)/shard_map/ppermute | solution.py:29
  137.6 10.4 %collective-permute-start.9 = (bf16[4,2,112]{2,0,1:T(4,128)(2,1)S(1)}, bf16[4,2,112]{2,0,1:T(4,128)(2,1)S(1)}, u32[]{:S(2)}, u32[]{:S(2)}) collective-permute-start(bf16[4,2,112]{2,0,1:T(4,128)(2,1)S(1)} %fusion.65), channel_id=1, source_target_pairs={{0,256},{64,320},{128,384},{192,448},{256,0},{320,64},{384,128},{4... | collective-permute-start | bytes 5384 | tf_op jit(solution)/shard_map/ppermute | solution.py:29
  141.2 17.5 %collective-permute-start.6 = (bf16[4,1,273]{2,0,1:T(4,128)(2,1)S(1)}, bf16[4,1,273]{2,0,1:T(4,128)(2,1)S(1)}, u32[]{:S(2)}, u32[]{:S(2)}) collective-permute-start(bf16[4,1,273]{2,0,1:T(4,128)(2,1)S(1)} %fusion.62), channel_id=1, source_target_pairs={{0,256},{64,320},{128,384},{192,448},{256,0},{320,64},{384,128},{4... | collective-permute-start | bytes 6560 | tf_op jit(solution)/shard_map/ppermute | solution.py:29
  145.1 9.7 %collective-permute-start.2 = (bf16[1,4,273,112]{3,2,1,0:T(8,128)(2,1)S(1)}, bf16[1,4,273,112]{3,2,1,0:T(8,128)(2,1)S(1)}, u32[]{:S(2)}, u32[]{:S(2)}) collective-permute-start(bf16[1,4,273,112]{3,2,1,0:T(8,128)(2,1)S(1)} %fusion.36), channel_id=1, source_target_pairs={{0,128},{64,192},{128,0},{192,64},{256,384},{320,448},{384,256},{4... | collective-permute-start | bytes 733832 | tf_op jit(solution)/shard_map/ppermute | solution.py:29
  154.9 10.3 %collective-permute-start.3 = (bf16[1,4,273,112]{3,2,1,0:T(8,128)(2,1)S(1)}, bf16[1,4,273,112]{3,2,1,0:T(8,128)(2,1)S(1)}, u32[]{:S(2)}, u32[]{:S(2)}) collective-permute-start(bf16[1,4,273,112]{3,2,1,0:T(8,128)(2,1)S(1)} %fusion.19), channel_id=1, source_target_pairs={{0,256},{64,320},{128,384},{192,448},{256,0},{320,64},{384,128},{4... | collective-permute-start | bytes 733832 | tf_op jit(solution)/shard_map/ppermute | solution.py:29
Sparse Core Ops, SparseCore 0:
  10.1 81.1 all-gather.2
  121.0 75.3 reduce-scatter.1

commit v4 on v3

--- a/solution.py
+++ b/solution.py
@@ -131,7 +131,10 @@
     block_ends = (jnp.arange(lax.axis_size("seq"), dtype=jnp.int32) + 1) * tok_rows - 1
     tail_seg = segment_ids(block_ends, ends)
     seg_last = tail_seg[seq_pos]
-    tail_state = lax.dynamic_index_in_dim(contrib_state, seg_last, axis=1, keepdims=False)
+    in_tail = (seg == seg_last).astype(jnp.float32)
+    tail_state = jnp.einsum(
+        "thf,thd->hfd", phi_k * in_tail[:, None, None], values_f, precision=HIGH
+    )
     seg_before = jnp.sum((first_row - 1 >= ends).astype(jnp.int32))
     tails = lax.all_gather(tail_state.astype(jnp.bfloat16), "seq").astype(jnp.float32)
     block_index = jnp.arange(lax.axis_size("seq"), dtype=jnp.int32)
@@ -152,12 +155,10 @@
         "tk,kgc->gtc",
         hidden,
         w_out.reshape(local_cols, lax.axis_size("tp"), -1),
-        preferred_element_type=jnp.float32,
+        preferred_element_type=jnp.bfloat16,
     )
     summed = lax.psum_scatter(
-        lax.optimization_barrier(product.astype(jnp.bfloat16))
-        .astype(jnp.float32)
-        .astype(jnp.bfloat16),
+        product,
         "tp",
         scatter_dimension=0,
         tiled=True,

time: 204 us -> 201 us (0.985)
    convert_element_type x2 -> x1, other arithmetic: 2.39 us -> 0.03 us  [local(): ks = ks_b.astype(jnp.float32)]
where the time goes in v4:
time: 201 us; the launch traced here: 200 us
  waiting for transfers between devices  116 us (58%)
  starting transfers between devices  28 us (14%)
  between operations  14.5 us (7%)
  blocking collectives  14.3 us (7%)
  matrix products  13.4 us (7%)
  local copies, waits for them, and re-layouts  7.13 us (4%)
  other arithmetic  6.52 us (3%)
    all_gather x1, waiting for transfers between devices, local(): lax.all_gather(tokens, 'tp', axis=1, tiled=True)  77.4 us
    reduce_scatter x1, waiting for transfers between devices, local(): summed = lax.psum_scatter(product, 'tp', scatter_dimension=0, tiled=True)  27.5 us
    ppermute x9, starting transfers between devices, psum_doubling(): lax.ppermute(tuple((t.astype(jnp.bfloat16) for t in total)), axis, pairs)  26.6 us
    all_gather x1, blocking collectives, local(): lax.all_gather(tail_state.astype(jnp.bfloat16), 'seq').astype(jnp.float32)  14.3 us
    ppermute x9, waiting for transfers between devices, psum_doubling(): lax.ppermute(tuple((t.astype(jnp.bfloat16) for t in total)), axis, pairs)  10.8 us
  transfers between devices with their start and end apart: 12, of which 4 were waited for; matrix products, arithmetic and copies ran while one was open for 9% of the time, Pallas kernels for 0%

profile of v4, /device:TPU:24, one launch (start us, length us, event | category | flops | bytes accessed | tf_op | source)
XLA Modules:
  0.0 200.2 jit_solution(5603790079659906955)
XLA Ops:
  7.2 0.0 copy-start
  7.2 0.0 all-gather.4.cloned.1.call-start
  7.2 0.7 all-gather.4.cloned.1.call-update
  7.9 0.0 reduce-scatter.2.cloned.1.call-start
  8.0 0.8 reduce-window.7
  8.8 0.1 convert_reduce_fusion.2
  8.9 0.6 dynamic_slice.6
  9.5 0.1 convert_reduce_fusion.1
  9.6 0.1 convert_reduce_fusion
  9.7 1.3 bitcast_subtract_fusion
  11.0 0.6 and_convert_fusion.1
  11.6 0.8 slice_bitcast_fusion.4
  12.4 1.4 fusion.74
  13.8 77.4 %all-gather.4.cloned.1.call-done = bf16[1024,1792]{0,1:T(8,128)(2,1)} async-done(((bf16[1024,112]{0,1:T(8,128)(2,1)}), bf16[1024,1792]{0,1:T(8,128)(2,1)}) %all-gather.4.cloned.1.call-update) | async-done | bytes 3670032 | tf_op jit(solution)/shard_map/all_gather | solution.py:81
  91.2 3.2 %fusion.8 = bf16[1024,1,256]{0,2,1:T(8,128)(2,1)S(1)} fusion(bf16[1024,1792]{0,1:T(8,128)(2,1)} %all-gather.4.cloned.1.call-done, bf16[1792,256]{1,0:T(8,128)(2,1)S(1)} %copy-done), kind=kOutput, calls=%fused_computation.15 | convolution fusion | flops 939786240 | bytes 5111808 | tf_op jit(solution)/shard_map/dot_general | solution.py:80
  94.4 0.1 slice_bitcast_fusion.1
  94.6 1.7 fusion.9
  96.3 1.3 collective-permute-start
  97.6 0.1 multiply_multiply_fusion.1
  97.7 0.1 multiply_multiply_fusion.2
  97.8 0.8 fusion.25
  98.7 14.3 %all-gather.1 = bf16[8,273,112]{2,1,0:T(8,128)(2,1)S(1)} all-gather(bf16[1,273,112]{2,1,0:T(8,128)(2,1)S(1)} %fusion.25), channel_id=2, replica_groups=mesh['seq'=8,'tp'=16,'req'=4] {'seq'}, dimensions={0}, use_global_device_ids=true | all-gather | bytes 550368 | tf_op jit(solution)/shard_map/all_gather | solution.py:139
  112.9 0.2 fusion.21
  113.2 0.0 copy-start.2
  113.2 0.0 copy-start.3
  113.2 1.2 multiply_reduce_fusion
  114.4 0.0 collective-permute-done
  114.5 3.2 %fusion.38 = bf16[1024,1792]{0,1} fusion(bf16[112,1792]{1,0:T(8,128)(2,1)S(1)} %copy-done.2, bf16[1024,112]{0,1:T(8,128)(2,1)S(1)} %slice_bitcast_fusion, f32[1,112,1024]{2,1,0:T(8,128)S(1)} %get-tuple-element.39, bf16[2,112]{0,1:T(8,128)(2,1)S(1)} %collective-permute-done, f32[1024]{0:T(1024)S(1)} %get-tuple-element.28, f32[112]{0:T(128)S(1)} %get-tuple-element.33, ...), kind=kOutput, calls=%fused_computation.57 | convolution fusion | flops 413908992 | bytes 4778176
  117.6 0.0 reduce-scatter.2.cloned.1.call-update
  117.7 0.6 copy-done.4
  118.3 0.1 compare_select_fusion.1
  118.4 0.6 gather_fusion
  119.0 0.1 compare_and_fusion
  119.1 0.6 gather_fusion.2
  119.8 0.2 fusion.91
  120.0 2.3 %collective-permute-start.7 = (bf16[4,2,112]{2,0,1:T(4,128)(2,1)S(1)}, bf16[4,2,112]{2,0,1:T(4,128)(2,1)S(1)}, u32[]{:S(2)}, u32[]{:S(2)}) collective-permute-start(bf16[4,2,112]{2,0,1:T(4,128)(2,1)S(1)} %get-tuple-element.40), channel_id=1, source_target_pairs={{0,64},{64,0},{128,192},{192,128},{256,320},{320,256},{384,448},{4... | collective-permute-start | bytes 5384 | tf_op jit(solution)/shard_map/ppermute | solution.py:29
  122.3 0.8 fusion.65
  123.1 2.1 %collective-permute-start.4 = (bf16[4,1,273]{2,0,1:T(4,128)(2,1)S(1)}, bf16[4,1,273]{2,0,1:T(4,128)(2,1)S(1)}, u32[]{:S(2)}, u32[]{:S(2)}) collective-permute-start(bf16[4,1,273]{2,0,1:T(4,128)(2,1)S(1)} %convert_bitcast_fusion.3), channel_id=1, source_target_pairs={{0,64},{64,0},{128,192},{192,128},{256,320},{320,256},{384,448},{4... | collective-permute-start | bytes 6560 | tf_op jit(solution)/shard_map/ppermute | solution.py:29
  125.2 0.2 maximum_bitcast_fusion.2
  125.3 2.3 %fusion = f32[4,273,112]{2,1,0:T(8,128)S(1)} fusion(f32[1024,273]{0,1:T(8,128)S(1)} %maximum_bitcast_fusion.2, f32[1024,4]{0,1:T(4,128)S(1)} %fusion.66, bf16[1024,1,256]{0,2,1:T(8,128)(2,1)S(1)} %fusion.8), kind=kOutput, calls=%fused_computation.6 | convolution fusion | flops 1503989760 | bytes 1881856 | tf_op jit(solution)/shard_map/dot_general | solution.py:119
  127.7 2.3 %collective-permute-start.1 = (bf16[1,4,273,112]{3,2,1,0:T(8,128)(2,1)S(1)}, bf16[1,4,273,112]{3,2,1,0:T(8,128)(2,1)S(1)}, u32[]{:S(2)}, u32[]{:S(2)}) collective-permute-start(bf16[1,4,273,112]{3,2,1,0:T(8,128)(2,1)S(1)} %convert_bitcast_fusion), channel_id=1, source_target_pairs={{0,64},{64,0},{128,192},{192,128},{256,320},{320,256},{384,448},{4... | collective-permute-start | bytes 733832 | tf_op jit(solution)/shard_map/ppermute | solution.py:29
  130.0 0.0 collective-permute-done.7
  130.0 2.9 %collective-permute-start.8 = (bf16[4,2,112]{2,0,1:T(4,128)(2,1)S(1)}, bf16[4,2,112]{2,0,1:T(4,128)(2,1)S(1)}, u32[]{:S(2)}, u32[]{:S(2)}) collective-permute-start(bf16[4,2,112]{2,0,1:T(4,128)(2,1)S(1)} %fusion.78), channel_id=1, source_target_pairs={{0,128},{64,192},{128,0},{192,64},{256,384},{320,448},{384,256},{4... | collective-permute-start | bytes 5384 | tf_op jit(solution)/shard_map/ppermute | solution.py:29
  133.0 2.9 %collective-permute-start.5 = (bf16[4,1,273]{2,0,1:T(4,128)(2,1)S(1)}, bf16[4,1,273]{2,0,1:T(4,128)(2,1)S(1)}, u32[]{:S(2)}, u32[]{:S(2)}) collective-permute-start(bf16[4,1,273]{2,0,1:T(4,128)(2,1)S(1)} %fusion.79), channel_id=1, source_target_pairs={{0,128},{64,192},{128,0},{192,64},{256,384},{320,448},{384,256},{4... | collective-permute-start | bytes 6560 | tf_op jit(solution)/shard_map/ppermute | solution.py:29
  135.9 3.6 %collective-permute-start.9 = (bf16[4,2,112]{2,0,1:T(4,128)(2,1)S(1)}, bf16[4,2,112]{2,0,1:T(4,128)(2,1)S(1)}, u32[]{:S(2)}, u32[]{:S(2)}) collective-permute-start(bf16[4,2,112]{2,0,1:T(4,128)(2,1)S(1)} %fusion.80), channel_id=1, source_target_pairs={{0,256},{64,320},{128,384},{192,448},{256,0},{320,64},{384,128},{4... | collective-permute-start | bytes 5384 | tf_op jit(solution)/shard_map/ppermute | solution.py:29
  139.5 0.0 collective-permute-done.5
  139.5 3.8 %collective-permute-start.6 = (bf16[4,1,273]{2,0,1:T(4,128)(2,1)S(1)}, bf16[4,1,273]{2,0,1:T(4,128)(2,1)S(1)}, u32[]{:S(2)}, u32[]{:S(2)}) collective-permute-start(bf16[4,1,273]{2,0,1:T(4,128)(2,1)S(1)} %fusion.77), channel_id=1, source_target_pairs={{0,256},{64,320},{128,384},{192,448},{256,0},{320,64},{384,128},{4... | collective-permute-start | bytes 6560 | tf_op jit(solution)/shard_map/ppermute | solution.py:29
  143.3 0.1 fusion.51
  143.4 2.9 %collective-permute-start.2 = (bf16[1,4,273,112]{3,2,1,0:T(8,128)(2,1)S(1)}, bf16[1,4,273,112]{3,2,1,0:T(8,128)(2,1)S(1)}, u32[]{:S(2)}, u32[]{:S(2)}) collective-permute-start(bf16[1,4,273,112]{3,2,1,0:T(8,128)(2,1)S(1)} %fusion.51), channel_id=1, source_target_pairs={{0,128},{64,192},{128,0},{192,64},{256,384},{320,448},{384,256},{4... | collective-permute-start | bytes 733832 | tf_op jit(solution)/shard_map/ppermute | solution.py:29
  146.3 0.0 collective-permute-done.9
  146.4 0.6 gather_fusion.4
  146.9 0.7 select_convert_fusion
  147.6 5.5 %collective-permute-done.2 = bf16[1,4,273,112]{3,2,1,0:T(8,128)(2,1)S(1)} collective-permute-done((bf16[1,4,273,112]{3,2,1,0:T(8,128)(2,1)S(1)}, bf16[1,4,273,112]{3,2,1,0:T(8,128)(2,1)S(1)}, u32[]{:S(2)}, u32[]{:S(2)}) %collective-permute-start.2) | collective-permute-done | bytes 244640 | tf_op jit(solution)/shard_map/ppermute | solution.py:29
  153.1 0.1 fusion.33
  153.2 3.9 %collective-permute-start.3 = (bf16[1,4,273,112]{3,2,1,0:T(8,128)(2,1)S(1)}, bf16[1,4,273,112]{3,2,1,0:T(8,128)(2,1)S(1)}, u32[]{:S(2)}, u32[]{:S(2)}) collective-permute-start(bf16[1,4,273,112]{3,2,1,0:T(8,128)(2,1)S(1)} %fusion.33), channel_id=1, source_target_pairs={{0,256},{64,320},{128,384},{192,448},{256,0},{320,64},{384,128},{4... | collective-permute-start | bytes 733832 | tf_op jit(solution)/shard_map/ppermute | solution.py:29
  157.1 0.6 gather_fusion.3
  157.7 0.1 fusion.73
  157.7 0.6 copy.27
  158.3 5.3 %collective-permute-done.3 = bf16[1,4,273,112]{3,2,1,0:T(8,128)(2,1)S(1)} collective-permute-done((bf16[1,4,273,112]{3,2,1,0:T(8,128)(2,1)S(1)}, bf16[1,4,273,112]{3,2,1,0:T(8,128)(2,1)S(1)}, u32[]{:S(2)}, u32[]{:S(2)}) %collective-permute-start.3) | collective-permute-done | bytes 244640 | tf_op jit(solution)/shard_map/ppermute | solution.py:29
  163.6 0.1 add_bitcast_fusion
  163.8 0.6 gather_fusion.1
  164.4 0.1 fusion.30
  164.5 1.4 copy.26
  165.9 27.5 %reduce-scatter.2.cloned.1.call-done = bf16[1,1024,112]{1,2,0:T(8,128)(2,1)} async-done(((bf16[16,1024,112]{1,2,0:T(8,128)(2,1)}), bf16[1,1024,112]{1,2,0:T(8,128)(2,1)}) %reduce-scatter.2.cloned.1.call-update) | async-done | bytes 229392 | tf_op jit(solution)/shard_map/reduce_scatter | solution.py:160
  (35 shorter events, 0.2 us)
Async XLA Ops:
  7.2 84.1 %copy-start = (bf16[1792,256]{1,0:T(8,128)(2,1)S(1)}, bf16[1792,256]{1,0:T(8,128)(2,1)}, u32[]{:S(2)}) copy-start(bf16[1792,256]{1,0:T(8,128)(2,1)} %param.9) | copy-start | bytes 2752516
  7.2 84.0 %all-gather.4.cloned.1.call-start = ((), (), s32[]{:S(2)}) async-start(), calls=%async_computation.1 | async-start | bytes 3899392 | tf_op jit(solution)/shard_map/all_gather | solution.py:81
  7.9 185.4 %reduce-scatter.2.cloned.1.call-start = ((), (), s32[]{:S(2)}) async-start(), calls=%async_computation.2 | async-start | bytes 3899392 | tf_op jit(solution)/shard_map/reduce_scatter | solution.py:160
  96.3 18.2 %collective-permute-start = (bf16[2,112]{0,1:T(8,128)(2,1)S(1)}, bf16[2,112]{0,1:T(8,128)(2,1)S(1)}, u32[]{:S(2)}, u32[]{:S(2)}) collective-permute-start(bf16[2,112]{0,1:T(8,128)(2,1)S(1)} %slice_bitcast_fusion.1), channel_id=1, source_target_pairs={{0,64},{64,128},{128,192},{192,256},{256,320},{320,384},{384,448},... | collective-permute-start | bytes 1352 | tf_op jit(solution)/shard_map/ppermute | solution.py:20
  113.2 1.3 copy-start.2
  113.2 1.3 copy-start.3
  117.6 0.7 copy-start.4
  117.6 0.7 copy-start.1
  117.6 1.5 copy-start.5
  120.0 10.0 %collective-permute-start.7 = (bf16[4,2,112]{2,0,1:T(4,128)(2,1)S(1)}, bf16[4,2,112]{2,0,1:T(4,128)(2,1)S(1)}, u32[]{:S(2)}, u32[]{:S(2)}) collective-permute-start(bf16[4,2,112]{2,0,1:T(4,128)(2,1)S(1)} %get-tuple-element.40), channel_id=1, source_target_pairs={{0,64},{64,0},{128,192},{192,128},{256,320},{320,256},{384,448},{4... | collective-permute-start | bytes 5384 | tf_op jit(solution)/shard_map/ppermute | solution.py:29
  123.1 9.9 %collective-permute-start.4 = (bf16[4,1,273]{2,0,1:T(4,128)(2,1)S(1)}, bf16[4,1,273]{2,0,1:T(4,128)(2,1)S(1)}, u32[]{:S(2)}, u32[]{:S(2)}) collective-permute-start(bf16[4,1,273]{2,0,1:T(4,128)(2,1)S(1)} %convert_bitcast_fusion.3), channel_id=1, source_target_pairs={{0,64},{64,0},{128,192},{192,128},{256,320},{320,256},{384,448},{4... | collective-permute-start | bytes 6560 | tf_op jit(solution)/shard_map/ppermute | solution.py:29
  127.7 15.6 %collective-permute-start.1 = (bf16[1,4,273,112]{3,2,1,0:T(8,128)(2,1)S(1)}, bf16[1,4,273,112]{3,2,1,0:T(8,128)(2,1)S(1)}, u32[]{:S(2)}, u32[]{:S(2)}) collective-permute-start(bf16[1,4,273,112]{3,2,1,0:T(8,128)(2,1)S(1)} %convert_bitcast_fusion), channel_id=1, source_target_pairs={{0,64},{64,0},{128,192},{192,128},{256,320},{320,256},{384,448},{4... | collective-permute-start | bytes 733832 | tf_op jit(solution)/shard_map/ppermute | solution.py:29
  130.0 5.9 %collective-permute-start.8 = (bf16[4,2,112]{2,0,1:T(4,128)(2,1)S(1)}, bf16[4,2,112]{2,0,1:T(4,128)(2,1)S(1)}, u32[]{:S(2)}, u32[]{:S(2)}) collective-permute-start(bf16[4,2,112]{2,0,1:T(4,128)(2,1)S(1)} %fusion.78), channel_id=1, source_target_pairs={{0,128},{64,192},{128,0},{192,64},{256,384},{320,448},{384,256},{4... | collective-permute-start | bytes 5384 | tf_op jit(solution)/shard_map/ppermute | solution.py:29
  133.0 6.5 %collective-permute-start.5 = (bf16[4,1,273]{2,0,1:T(4,128)(2,1)S(1)}, bf16[4,1,273]{2,0,1:T(4,128)(2,1)S(1)}, u32[]{:S(2)}, u32[]{:S(2)}) collective-permute-start(bf16[4,1,273]{2,0,1:T(4,128)(2,1)S(1)} %fusion.79), channel_id=1, source_target_pairs={{0,128},{64,192},{128,0},{192,64},{256,384},{320,448},{384,256},{4... | collective-permute-start | bytes 6560 | tf_op jit(solution)/shard_map/ppermute | solution.py:29
  135.9 10.4 %collective-permute-start.9 = (bf16[4,2,112]{2,0,1:T(4,128)(2,1)S(1)}, bf16[4,2,112]{2,0,1:T(4,128)(2,1)S(1)}, u32[]{:S(2)}, u32[]{:S(2)}) collective-permute-start(bf16[4,2,112]{2,0,1:T(4,128)(2,1)S(1)} %fusion.80), channel_id=1, source_target_pairs={{0,256},{64,320},{128,384},{192,448},{256,0},{320,64},{384,128},{4... | collective-permute-start | bytes 5384 | tf_op jit(solution)/shard_map/ppermute | solution.py:29
  139.5 17.5 %collective-permute-start.6 = (bf16[4,1,273]{2,0,1:T(4,128)(2,1)S(1)}, bf16[4,1,273]{2,0,1:T(4,128)(2,1)S(1)}, u32[]{:S(2)}, u32[]{:S(2)}) collective-permute-start(bf16[4,1,273]{2,0,1:T(4,128)(2,1)S(1)} %fusion.77), channel_id=1, source_target_pairs={{0,256},{64,320},{128,384},{192,448},{256,0},{320,64},{384,128},{4... | collective-permute-start | bytes 6560 | tf_op jit(solution)/shard_map/ppermute | solution.py:29
  143.4 9.7 %collective-permute-start.2 = (bf16[1,4,273,112]{3,2,1,0:T(8,128)(2,1)S(1)}, bf16[1,4,273,112]{3,2,1,0:T(8,128)(2,1)S(1)}, u32[]{:S(2)}, u32[]{:S(2)}) collective-permute-start(bf16[1,4,273,112]{3,2,1,0:T(8,128)(2,1)S(1)} %fusion.51), channel_id=1, source_target_pairs={{0,128},{64,192},{128,0},{192,64},{256,384},{320,448},{384,256},{4... | collective-permute-start | bytes 733832 | tf_op jit(solution)/shard_map/ppermute | solution.py:29
  153.2 10.4 %collective-permute-start.3 = (bf16[1,4,273,112]{3,2,1,0:T(8,128)(2,1)S(1)}, bf16[1,4,273,112]{3,2,1,0:T(8,128)(2,1)S(1)}, u32[]{:S(2)}, u32[]{:S(2)}) collective-permute-start(bf16[1,4,273,112]{3,2,1,0:T(8,128)(2,1)S(1)} %fusion.33), channel_id=1, source_target_pairs={{0,256},{64,320},{128,384},{192,448},{256,0},{320,64},{384,128},{4... | collective-permute-start | bytes 733832 | tf_op jit(solution)/shard_map/ppermute | solution.py:29
Sparse Core Ops, SparseCore 0:
  10.1 81.1 all-gather.3
  117.8 75.5 reduce-scatter.1

commit v5 on v4

--- a/solution.py
+++ b/solution.py
@@ -77,10 +77,16 @@
     starts = ends - prompt_lens
     positions = first_row + jnp.arange(tok_rows, dtype=jnp.int32)
     seg = segment_ids(positions, ends)
-    proj = jnp.dot(
-        lax.all_gather(tokens, "tp", axis=1, tiled=True), w_in, preferred_element_type=jnp.float32
-    )
-    proj = proj.astype(jnp.bfloat16).reshape(tok_rows, local_heads, width)
+    half = tok_rows // 2
+    proj_halves = [
+        jnp.dot(
+            lax.all_gather(part, "tp", axis=1, tiled=True), w_in, preferred_element_type=jnp.float32
+        )
+        .astype(jnp.bfloat16)
+        .reshape(half, local_heads, width)
+        for part in (tokens[:half], tokens[half:])
+    ]
+    proj = jnp.concatenate(proj_halves, axis=0)
     gate_pre = proj[:, :, 2 * FEAT + HD :].reshape(tok_rows, local_cols)
     rim = passed_along(gate_pre[tok_rows - (KW - 1) :], "seq", 1)
     extended = jnp.concatenate([rim, gate_pre], 0)
@@ -102,12 +108,24 @@
     ks = ks_b.astype(jnp.float32)
     values = proj[:, :, 2 * FEAT : 2 * FEAT + HD]
     values_f = values.astype(jnp.float32)
-    dots = jnp.einsum("thf,shf->hts", qs_b, ks_b, preferred_element_type=jnp.float32)
-    visible = (positions[None, :] <= positions[:, None]) & (seg[:, None] == seg[None, :])
-    weights = jnp.where(visible[None], 1.0 + dots + 0.5 * dots * dots, 0.0)
-    numer = jnp.einsum(
-        "hts,shd->thd", weights.astype(jnp.bfloat16), values, preferred_element_type=jnp.float32
-    )
+    numer_halves = []
+    for lo, hi in ((0, half), (half, tok_rows)):
+        dots = jnp.einsum(
+            "thf,shf->hts", qs_b[lo:hi], ks_b[:hi], preferred_element_type=jnp.float32
+        )
+        visible = (positions[None, :hi] <= positions[lo:hi, None]) & (
+            seg[lo:hi, None] == seg[None, :hi]
+        )
+        weights = jnp.where(visible[None], 1.0 + dots + 0.5 * dots * dots, 0.0)
+        numer_halves.append(
+            jnp.einsum(
+                "hts,shd->thd",
+                weights.astype(jnp.bfloat16),
+                values[:hi],
+                preferred_element_type=jnp.float32,
+            )
+        )
+    numer = jnp.concatenate(numer_halves, axis=0)
     phi_q = taylor_map(qs)
     phi_k = taylor_map(ks)
     fmap = phi_k.shape[-1]
@@ -132,8 +150,14 @@
     tail_seg = segment_ids(block_ends, ends)
     seg_last = tail_seg[seq_pos]
     in_tail = (seg == seg_last).astype(jnp.float32)
-    tail_state = jnp.einsum(
-        "thf,thd->hfd", phi_k * in_tail[:, None, None], values_f, precision=HIGH
+    tail_state = sum(
+        jnp.einsum(
+            "thf,thd->hfd",
+            taylor_map(ks[lo:hi]) * in_tail[lo:hi, None, None],
+            values_f[lo:hi],
+            precision=HIGH,
+        )
+        for lo, hi in ((0, half), (half, tok_rows))
     )
     seg_before = jnp.sum((first_row - 1 >= ends).astype(jnp.int32))
     tails = lax.all_gather(tail_state.astype(jnp.bfloat16), "seq").astype(jnp.float32)

time: 201 us -> 270 us (1.34)
  waiting for transfers between devices: 116 us -> 173 us
  matrix products: 13.4 us -> 18.6 us
  local copies, waits for them, and re-layouts: 7.13 us -> 11.3 us
    all_gather x1 -> x2, waiting for transfers between devices: 77.4 us -> 135 us  [local(): lax.all_gather(part, 'tp', axis=1, tiled=True)]
    dot_general x3 -> x6, matrix products: 5.71 us -> 9.12 us  [the longest x2 4.36 us: local(): jnp.dot(lax.all_gather(part, 'tp', axis=1, tiled=True), w_in, preferred_e...]
    slice x0 -> x4, local copies, waits for them, and re-layouts: none -> 2.91 us  [the longest x1 1.72 us: local(): tokens[:half]]
  transfers between devices with their start and end apart: 12 -> 13, of which waited for: 4 -> 5; matrix products, arithmetic and copies ran while one was open for 9% -> 12% of each run, Pallas kernels for 0% -> 0%
where the time goes in v5:
time: 270 us; the launch traced here: 269 us
  waiting for transfers between devices  173 us (64%)
  starting transfers between devices  28.9 us (11%)
  matrix products  18.6 us (7%)
  between operations  14.4 us (5%)
  blocking collectives  13.5 us (5%)
  local copies, waits for them, and re-layouts  11.3 us (4%)
  other arithmetic  9.19 us (3%)
    all_gather x2, waiting for transfers between devices, local(): lax.all_gather(part, 'tp', axis=1, tiled=True)  135 us
    reduce_scatter x1, waiting for transfers between devices, local(): summed = lax.psum_scatter(product, 'tp', scatter_dimension=0, tiled=True)  27.3 us
    ppermute x9, starting transfers between devices, psum_doubling(): lax.ppermute(tuple((t.astype(jnp.bfloat16) for t in total)), axis, pairs)  26.9 us
    all_gather x1, blocking collectives, local(): lax.all_gather(tail_state.astype(jnp.bfloat16), 'seq').astype(jnp.float32)  13.5 us
    ppermute x9, waiting for transfers between devices, psum_doubling(): lax.ppermute(tuple((t.astype(jnp.bfloat16) for t in total)), axis, pairs)  10.5 us
  transfers between devices with their start and end apart: 13, of which 5 were waited for; matrix products, arithmetic and copies ran while one was open for 12% of the time, Pallas kernels for 0%

profile of v5, /device:TPU:24, one launch (start us, length us, event | category | flops | bytes accessed | tf_op | source)
XLA Modules:
  0.0 269.1 jit_solution(1293546007089729475)
XLA Ops:
  7.2 1.7 fusion.108
  9.0 0.0 all-gather.5.cloned.1.call-start
  9.0 0.7 all-gather.5.cloned.1.call-update
  9.7 0.0 reduce-scatter.2.cloned.1.call-start
  9.8 0.8 reduce-window.7
  10.6 0.1 convert_reduce_fusion.2
  10.7 0.7 dynamic_slice.6
  11.4 0.1 convert_reduce_fusion.1
  11.5 0.1 convert_reduce_fusion
  11.6 1.9 bitcast_subtract_fusion
  13.5 1.2 and_convert_fusion.1
  14.7 1.4 slice_bitcast_fusion.21
  16.1 0.6 fusion.109
  16.6 0.6 fusion.110
  17.2 2.0 fusion.84
  19.2 67.9 %all-gather.7.cloned.1.call-done = bf16[512,1792]{0,1:T(8,128)(2,1)} async-done(((bf16[512,112]{0,1:T(8,128)(2,1)}), bf16[512,1792]{0,1:T(8,128)(2,1)}) %all-gather.7.cloned.1.call-update) | async-done | bytes 1835024 | tf_op jit(solution)/shard_map/all_gather | solution.py:83
  87.1 2.2 fusion.12
  89.3 0.7 slice_bitcast_fusion.9
  90.0 1.9 collective-permute-start
  91.9 66.9 %all-gather.5.cloned.1.call-done = bf16[512,1792]{0,1:T(8,128)(2,1)} async-done(((bf16[512,112]{0,1:T(8,128)(2,1)}), bf16[512,1792]{0,1:T(8,128)(2,1)}) %all-gather.5.cloned.1.call-update) | async-done | bytes 1835024 | tf_op jit(solution)/shard_map/all_gather | solution.py:83
  158.8 2.2 fusion.11
  161.1 0.1 multiply_multiply_fusion.3
  161.2 0.1 multiply_multiply_fusion.4
  161.3 0.5 fusion.32
  161.9 0.5 fusion.19
  162.4 13.5 %all-gather.1 = bf16[8,273,112]{2,1,0:T(8,128)(2,1)S(1)} all-gather(bf16[1,273,112]{2,1,0:T(8,128)(2,1)S(1)} %fusion.19), channel_id=2, replica_groups=mesh['seq'=8,'tp'=16,'req'=4] {'seq'}, dimensions={0}, use_global_device_ids=true | all-gather | bytes 550368 | tf_op jit(solution)/shard_map/all_gather | solution.py:163
  175.8 1.7 fusion.13
  177.5 2.1 convolution_bitcast_fusion.1
  179.7 1.0 fusion.17
  180.6 2.2 multiply_reduce_fusion
  182.9 4.0 %fusion.60 = bf16[1024,1792]{0,1} fusion(bf16[112,1792]{1,0:T(8,128)(2,1)S(1)} %copy-done.2, bf16[1024,112]{0,1:T(8,128)(2,1)S(1)} %fusion.92, f32[1024,1,112]{0,2,1:T(8,128)S(1)} %get-tuple-element.52, bf16[2,112]{0,1:T(8,128)(2,1)} %collective-permute-done, f32[1024]{0:T(1024)S(1)} %copy-done.10, f32[112]{0:T(128)S(1)} %copy-done.13, ...), kind=kOutput, calls=%fused_computation.91 | convolution fusion | flops 413908992 | bytes 4778176
  187.0 0.6 copy-done.16
  187.6 0.1 compare_select_fusion.1
  187.7 0.6 gather_fusion
  188.3 0.1 compare_and_fusion
  188.4 0.6 gather_fusion.2
  189.1 0.2 fusion.112
  189.3 2.3 collective-permute-start.7
  191.6 0.1 multiply_multiply_fusion.2
  191.8 0.8 fusion.79
  192.5 2.1 collective-permute-start.4
  194.6 0.2 maximum_bitcast_fusion.2
  194.8 2.3 fusion
  197.2 2.3 collective-permute-start.1
  199.4 3.1 %collective-permute-start.8 = (bf16[4,2,112]{2,0,1:T(4,128)(2,1)S(1)}, bf16[4,2,112]{2,0,1:T(4,128)(2,1)S(1)}, u32[]{:S(2)}, u32[]{:S(2)}) collective-permute-start(bf16[4,2,112]{2,0,1:T(4,128)(2,1)S(1)} %fusion.88), channel_id=1, source_target_pairs={{0,128},{64,192},{128,0},{192,64},{256,384},{320,448},{384,256},{4... | collective-permute-start | bytes 5384 | tf_op jit(solution)/shard_map/ppermute | solution.py:29
  202.6 2.8 %collective-permute-start.5 = (bf16[4,1,273]{2,0,1:T(4,128)(2,1)S(1)}, bf16[4,1,273]{2,0,1:T(4,128)(2,1)S(1)}, u32[]{:S(2)}, u32[]{:S(2)}) collective-permute-start(bf16[4,1,273]{2,0,1:T(4,128)(2,1)S(1)} %fusion.89), channel_id=1, source_target_pairs={{0,128},{64,192},{128,0},{192,64},{256,384},{320,448},{384,256},{4... | collective-permute-start | bytes 6560 | tf_op jit(solution)/shard_map/ppermute | solution.py:29
  205.4 3.7 %collective-permute-start.9 = (bf16[4,2,112]{2,0,1:T(4,128)(2,1)S(1)}, bf16[4,2,112]{2,0,1:T(4,128)(2,1)S(1)}, u32[]{:S(2)}, u32[]{:S(2)}) collective-permute-start(bf16[4,2,112]{2,0,1:T(4,128)(2,1)S(1)} %fusion.90), channel_id=1, source_target_pairs={{0,256},{64,320},{128,384},{192,448},{256,0},{320,64},{384,128},{4... | collective-permute-start | bytes 5384 | tf_op jit(solution)/shard_map/ppermute | solution.py:29
  209.1 3.6 %collective-permute-start.6 = (bf16[4,1,273]{2,0,1:T(4,128)(2,1)S(1)}, bf16[4,1,273]{2,0,1:T(4,128)(2,1)S(1)}, u32[]{:S(2)}, u32[]{:S(2)}) collective-permute-start(bf16[4,1,273]{2,0,1:T(4,128)(2,1)S(1)} %fusion.87), channel_id=1, source_target_pairs={{0,256},{64,320},{128,384},{192,448},{256,0},{320,64},{384,128},{4... | collective-permute-start | bytes 6560 | tf_op jit(solution)/shard_map/ppermute | solution.py:29
  212.8 0.1 fusion.72
  212.8 3.1 %collective-permute-start.2 = (bf16[1,4,273,112]{3,2,1,0:T(8,128)(2,1)S(1)}, bf16[1,4,273,112]{3,2,1,0:T(8,128)(2,1)S(1)}, u32[]{:S(2)}, u32[]{:S(2)}) collective-permute-start(bf16[1,4,273,112]{3,2,1,0:T(8,128)(2,1)S(1)} %fusion.72), channel_id=1, source_target_pairs={{0,128},{64,192},{128,0},{192,64},{256,384},{320,448},{384,256},{4... | collective-permute-start | bytes 733832 | tf_op jit(solution)/shard_map/ppermute | solution.py:29
  216.0 0.6 gather_fusion.4
  216.5 0.7 select_convert_fusion
  217.2 5.3 %collective-permute-done.2 = bf16[1,4,273,112]{3,2,1,0:T(8,128)(2,1)S(1)} collective-permute-done((bf16[1,4,273,112]{3,2,1,0:T(8,128)(2,1)S(1)}, bf16[1,4,273,112]{3,2,1,0:T(8,128)(2,1)S(1)}, u32[]{:S(2)}, u32[]{:S(2)}) %collective-permute-start.2) | collective-permute-done | bytes 244640 | tf_op jit(solution)/shard_map/ppermute | solution.py:29
  222.5 0.1 fusion.51
  222.6 4.0 %collective-permute-start.3 = (bf16[1,4,273,112]{3,2,1,0:T(8,128)(2,1)S(1)}, bf16[1,4,273,112]{3,2,1,0:T(8,128)(2,1)S(1)}, u32[]{:S(2)}, u32[]{:S(2)}) collective-permute-start(bf16[1,4,273,112]{3,2,1,0:T(8,128)(2,1)S(1)} %fusion.51), channel_id=1, source_target_pairs={{0,256},{64,320},{128,384},{192,448},{256,0},{320,64},{384,128},{4... | collective-permute-start | bytes 733832 | tf_op jit(solution)/shard_map/ppermute | solution.py:29
  226.6 0.6 gather_fusion.3
  227.2 0.1 fusion.83
  227.3 0.6 copy.39
  227.9 5.1 %collective-permute-done.3 = bf16[1,4,273,112]{3,2,1,0:T(8,128)(2,1)S(1)} collective-permute-done((bf16[1,4,273,112]{3,2,1,0:T(8,128)(2,1)S(1)}, bf16[1,4,273,112]{3,2,1,0:T(8,128)(2,1)S(1)}, u32[]{:S(2)}, u32[]{:S(2)}) %collective-permute-start.3) | collective-permute-done | bytes 244640 | tf_op jit(solution)/shard_map/ppermute | solution.py:29
  233.0 0.1 add_bitcast_fusion
  233.2 0.6 gather_fusion.1
  233.8 0.1 fusion.42
  233.9 1.4 copy.38
  235.3 27.3 %reduce-scatter.2.cloned.1.call-done = bf16[1,1024,112]{1,2,0:T(8,128)(2,1)} async-done(((bf16[16,1024,112]{1,2,0:T(8,128)(2,1)}), bf16[1,1024,112]{1,2,0:T(8,128)(2,1)}) %reduce-scatter.2.cloned.1.call-update) | async-done | bytes 229392 | tf_op jit(solution)/shard_map/reduce_scatter | solution.py:184
  (77 shorter events, 0.4 us)
Async XLA Ops:
  7.2 80.0 %copy-start = (bf16[1792,256]{1,0:T(8,128)(2,1)S(1)}, bf16[1792,256]{1,0:T(8,128)(2,1)}, u32[]{:S(2)}) copy-start(bf16[1792,256]{1,0:T(8,128)(2,1)} %param.9) | copy-start | bytes 2752516
  7.2 79.9 %all-gather.7.cloned.1.call-start = ((), (), s32[]{:S(2)}) async-start(), calls=%async_computation.2 | async-start | bytes 1949696 | tf_op jit(solution)/shard_map/all_gather | solution.py:83
  9.0 149.8 %all-gather.5.cloned.1.call-start = ((), (), s32[]{:S(2)}) async-start(), calls=%async_computation.1 | async-start | bytes 1949696 | tf_op jit(solution)/shard_map/all_gather | solution.py:83
  9.7 252.8 %reduce-scatter.2.cloned.1.call-start = ((), (), s32[]{:S(2)}) async-start(), calls=%async_computation.3 | async-start | bytes 3899392 | tf_op jit(solution)/shard_map/reduce_scatter | solution.py:184
  11.4 150.5 %copy-start.7 = (f32[273]{0:T(512)}, f32[273]{0:T(512)S(1)}, u32[]{:S(2)}) copy-start(f32[273]{0:T(512)S(1)} %pad.11.clone) | copy-start | bytes 3280
  11.4 4.7 %copy-start.3 = (s32[1024]{0:T(1024)}, s32[1024]{0:T(1024)S(1)}, u32[]{:S(2)}) copy-start(s32[1024]{0:T(1024)S(1)} %iota_add_fusion.1) | copy-start | bytes 12292
  11.5 5.8 %copy-start.5 = (s32[1024]{0:T(1024)}, s32[1024]{0:T(1024)S(1)}, u32[]{:S(2)}) copy-start(s32[1024]{0:T(1024)S(1)} %convert_reduce_fusion.1) | copy-start | bytes 12292
  90.0 92.8 %collective-permute-start = (bf16[2,112]{0,1:T(8,128)(2,1)}, bf16[2,112]{0,1:T(8,128)(2,1)}, u32[]{:S(2)}, u32[]{:S(2)}) collective-permute-start(bf16[2,112]{0,1:T(8,128)(2,1)} %slice_bitcast_fusion.9), channel_id=1, source_target_pairs={{0,64},{64,128},{128,192},{192,256},{256,320},{320,384},{384,448},... | collective-permute-start | bytes 1352 | tf_op jit(solution)/shard_map/ppermute | solution.py:20
  179.6 3.2 %copy-start.2 = (bf16[112,1792]{1,0:T(8,128)(2,1)S(1)}, bf16[112,1792]{1,0:T(8,128)(2,1)}, u32[]{:S(2)}) copy-start(bf16[112,1792]{1,0:T(8,128)(2,1)} %param.12) | copy-start | bytes 1204228
  179.6 3.3 %copy-start.9 = (f32[1024]{0:T(1024)S(1)}, f32[1024]{0:T(1024)}, u32[]{:S(2)}) copy-start(f32[1024]{0:T(1024)} %get-tuple-element.34) | copy-start | bytes 12292
  179.6 3.3 %copy-start.10 = (f32[1024]{0:T(1024)S(1)}, f32[1024]{0:T(1024)}, u32[]{:S(2)}) copy-start(f32[1024]{0:T(1024)} %get-tuple-element.35) | copy-start | bytes 12292
  179.6 3.3 %copy-start.11 = (f32[1024]{0:T(1024)S(1)}, f32[1024]{0:T(1024)}, u32[]{:S(2)}) copy-start(f32[1024]{0:T(1024)} %get-tuple-element.36) | copy-start | bytes 12292
  179.6 3.3 %copy-start.12 = (f32[112]{0:T(128)S(1)}, f32[112]{0:T(128)}, u32[]{:S(2)}) copy-start(f32[112]{0:T(128)} %get-tuple-element.45) | copy-start | bytes 1348
  179.6 3.3 %copy-start.13 = (f32[112]{0:T(128)S(1)}, f32[112]{0:T(128)}, u32[]{:S(2)}) copy-start(f32[112]{0:T(128)} %get-tuple-element.46) | copy-start | bytes 1348
  179.6 3.3 %copy-start.14 = (f32[112]{0:T(128)S(1)}, f32[112]{0:T(128)}, u32[]{:S(2)}) copy-start(f32[112]{0:T(128)} %get-tuple-element.47) | copy-start | bytes 1348
  179.6 3.3 %copy-start.15 = (f32[112]{0:T(128)S(1)}, f32[112]{0:T(128)}, u32[]{:S(2)}) copy-start(f32[112]{0:T(128)} %param.11) | copy-start | bytes 1348
  186.9 0.7 copy-start.16
  186.9 0.7 copy-start.1
  186.9 1.5 copy-start.17
  186.9 2.1 copy-start.19
  186.9 2.1 copy-start.18
  186.9 2.2 copy-start.6
  186.9 2.2 copy-start.4
  187.0 4.8 %copy-start.8 = (f32[273]{0:T(512)S(1)}, f32[273]{0:T(512)}, u32[]{:S(2)}) copy-start(f32[273]{0:T(512)} %copy-done.7) | copy-start | bytes 3280
  189.3 10.1 %collective-permute-start.7 = (bf16[4,2,112]{2,0,1:T(4,128)(2,1)S(1)}, bf16[4,2,112]{2,0,1:T(4,128)(2,1)S(1)}, u32[]{:S(2)}, u32[]{:S(2)}) collective-permute-start(bf16[4,2,112]{2,0,1:T(4,128)(2,1)S(1)} %get-tuple-element.53), channel_id=1, source_target_pairs={{0,64},{64,0},{128,192},{192,128},{256,320},{320,256},{384,448},{4... | collective-permute-start | bytes 5384 | tf_op jit(solution)/shard_map/ppermute | solution.py:29
  192.5 10.0 %collective-permute-start.4 = (bf16[4,1,273]{2,0,1:T(4,128)(2,1)S(1)}, bf16[4,1,273]{2,0,1:T(4,128)(2,1)S(1)}, u32[]{:S(2)}, u32[]{:S(2)}) collective-permute-start(bf16[4,1,273]{2,0,1:T(4,128)(2,1)S(1)} %convert_bitcast_fusion.3), channel_id=1, source_target_pairs={{0,64},{64,0},{128,192},{192,128},{256,320},{320,256},{384,448},{4... | collective-permute-start | bytes 6560 | tf_op jit(solution)/shard_map/ppermute | solution.py:29
  197.2 15.6 %collective-permute-start.1 = (bf16[1,4,273,112]{3,2,1,0:T(8,128)(2,1)S(1)}, bf16[1,4,273,112]{3,2,1,0:T(8,128)(2,1)S(1)}, u32[]{:S(2)}, u32[]{:S(2)}) collective-permute-start(bf16[1,4,273,112]{3,2,1,0:T(8,128)(2,1)S(1)} %convert_bitcast_fusion), channel_id=1, source_target_pairs={{0,64},{64,0},{128,192},{192,128},{256,320},{320,256},{384,448},{4... | collective-permute-start | bytes 733832 | tf_op jit(solution)/shard_map/ppermute | solution.py:29
  199.4 5.9 %collective-permute-start.8 = (bf16[4,2,112]{2,0,1:T(4,128)(2,1)S(1)}, bf16[4,2,112]{2,0,1:T(4,128)(2,1)S(1)}, u32[]{:S(2)}, u32[]{:S(2)}) collective-permute-start(bf16[4,2,112]{2,0,1:T(4,128)(2,1)S(1)} %fusion.88), channel_id=1, source_target_pairs={{0,128},{64,192},{128,0},{192,64},{256,384},{320,448},{384,256},{4... | collective-permute-start | bytes 5384 | tf_op jit(solution)/shard_map/ppermute | solution.py:29
  202.6 6.5 %collective-permute-start.5 = (bf16[4,1,273]{2,0,1:T(4,128)(2,1)S(1)}, bf16[4,1,273]{2,0,1:T(4,128)(2,1)S(1)}, u32[]{:S(2)}, u32[]{:S(2)}) collective-permute-start(bf16[4,1,273]{2,0,1:T(4,128)(2,1)S(1)} %fusion.89), channel_id=1, source_target_pairs={{0,128},{64,192},{128,0},{192,64},{256,384},{320,448},{384,256},{4... | collective-permute-start | bytes 6560 | tf_op jit(solution)/shard_map/ppermute | solution.py:29
  205.4 10.6 %collective-permute-start.9 = (bf16[4,2,112]{2,0,1:T(4,128)(2,1)S(1)}, bf16[4,2,112]{2,0,1:T(4,128)(2,1)S(1)}, u32[]{:S(2)}, u32[]{:S(2)}) collective-permute-start(bf16[4,2,112]{2,0,1:T(4,128)(2,1)S(1)} %fusion.90), channel_id=1, source_target_pairs={{0,256},{64,320},{128,384},{192,448},{256,0},{320,64},{384,128},{4... | collective-permute-start | bytes 5384 | tf_op jit(solution)/shard_map/ppermute | solution.py:29
  209.1 17.5 %collective-permute-start.6 = (bf16[4,1,273]{2,0,1:T(4,128)(2,1)S(1)}, bf16[4,1,273]{2,0,1:T(4,128)(2,1)S(1)}, u32[]{:S(2)}, u32[]{:S(2)}) collective-permute-start(bf16[4,1,273]{2,0,1:T(4,128)(2,1)S(1)} %fusion.87), channel_id=1, source_target_pairs={{0,256},{64,320},{128,384},{192,448},{256,0},{320,64},{384,128},{4... | collective-permute-start | bytes 6560 | tf_op jit(solution)/shard_map/ppermute | solution.py:29
  212.8 9.7 %collective-permute-start.2 = (bf16[1,4,273,112]{3,2,1,0:T(8,128)(2,1)S(1)}, bf16[1,4,273,112]{3,2,1,0:T(8,128)(2,1)S(1)}, u32[]{:S(2)}, u32[]{:S(2)}) collective-permute-start(bf16[1,4,273,112]{3,2,1,0:T(8,128)(2,1)S(1)} %fusion.72), channel_id=1, source_target_pairs={{0,128},{64,192},{128,0},{192,64},{256,384},{320,448},{384,256},{4... | collective-permute-start | bytes 733832 | tf_op jit(solution)/shard_map/ppermute | solution.py:29
  222.6 10.4 %collective-permute-start.3 = (bf16[1,4,273,112]{3,2,1,0:T(8,128)(2,1)S(1)}, bf16[1,4,273,112]{3,2,1,0:T(8,128)(2,1)S(1)}, u32[]{:S(2)}, u32[]{:S(2)}) collective-permute-start(bf16[1,4,273,112]{3,2,1,0:T(8,128)(2,1)S(1)} %fusion.51), channel_id=1, source_target_pairs={{0,256},{64,320},{128,384},{192,448},{256,0},{320,64},{384,128},{4... | collective-permute-start | bytes 733832 | tf_op jit(solution)/shard_map/ppermute | solution.py:29
Sparse Core Ops, SparseCore 0:
  10.6 76.4 all-gather.6
  89.8 68.9 all-gather.4
  187.1 75.4 reduce-scatter.1

commit v6 on v4

--- a/solution.py
+++ b/solution.py
@@ -151,19 +151,15 @@
         attended * inv_rms * gain[None] * jax.nn.silu(gate.reshape(tok_rows, local_heads, HD))
     ).astype(jnp.bfloat16)
     hidden = hidden.reshape(tok_rows, local_cols)
-    product = jnp.einsum(
-        "tk,kgc->gtc",
-        hidden,
-        w_out.reshape(local_cols, lax.axis_size("tp"), -1),
-        preferred_element_type=jnp.bfloat16,
+    n_tp = lax.axis_size("tp")
+    w_cols = lax.all_to_all(
+        w_out.reshape(local_cols, n_tp, -1), "tp", split_axis=1, concat_axis=0, tiled=True
+    ).reshape(n_tp, local_cols, -1)
+    hidden_all = lax.all_gather(hidden, "tp", axis=1, tiled=True).reshape(tok_rows, n_tp, local_cols)
+    partial = jnp.einsum(
+        "tgk,gkc->gtc", hidden_all, w_cols, preferred_element_type=jnp.bfloat16
     )
-    summed = lax.psum_scatter(
-        product,
-        "tp",
-        scatter_dimension=0,
-        tiled=True,
-    )
-    mixed = summed.reshape(tok_rows, -1)
+    mixed = jnp.sum(partial.astype(jnp.float32), axis=0).astype(jnp.bfloat16)
     all_state, all_norm, all_edge = psum_doubling((contrib_state, contrib_norm, contrib_edge), "seq")
     scale = lax.rsqrt(prompt_lens.astype(jnp.float32))
     my_requests = lax.dynamic_slice_in_dim(row_request, seq_pos * SLOTS, SLOTS)

time: 201 us -> 215 us (1.070)
  starting transfers between devices: 28 us -> 35.5 us
  waiting for transfers between devices: 116 us -> 121 us
    all_gather x0 -> x1, waiting for transfers between devices: none -> 31.4 us  [local(): lax.all_gather(hidden, 'tp', axis=1, tiled=True)]
    reduce_scatter x1 -> x0, waiting for transfers between devices: 27.5 us -> none  [local(): summed = lax.psum_scatter(product, 'tp', scatter_dimension=0, tiled=True)]
    all_to_all x0 -> x1, starting transfers between devices: none -> 7.91 us  [local(): lax.all_to_all(w_out.reshape(local_cols, n_tp, -1), 'tp', split_axis=1, c...]
    dot_general x0 -> x1, matrix products: none -> 3.47 us  [local(): jnp.einsum('tgk,gkc->gtc', hidden_all, w_cols, preferred_element_type=jnp...]
    unnamed x1 -> x0, matrix products: 3.18 us -> none
  transfers between devices with their start and end apart: 12 -> 13, of which waited for: 4 -> 4; matrix products, arithmetic and copies ran while one was open for 9% -> 9% of each run, Pallas kernels for 0% -> 0%
where the time goes in v6:
time: 215 us; the launch traced here: 214 us
  waiting for transfers between devices  121 us (56%)
  starting transfers between devices  35.5 us (17%)
  between operations  14.5 us (7%)
  blocking collectives  14.3 us (7%)
  matrix products  13.7 us (6%)
  other arithmetic  7.7 us (4%)
  local copies, waits for them, and re-layouts  7.49 us (3%)
    all_gather x1, waiting for transfers between devices, local(): lax.all_gather(tokens, 'tp', axis=1, tiled=True)  77.4 us
    all_gather x1, waiting for transfers between devices, local(): lax.all_gather(hidden, 'tp', axis=1, tiled=True)  31.4 us
    ppermute x9, starting transfers between devices, psum_doubling(): lax.ppermute(tuple((t.astype(jnp.bfloat16) for t in total)), axis, pairs)  26.3 us
    all_gather x1, blocking collectives, local(): lax.all_gather(tail_state.astype(jnp.bfloat16), 'seq').astype(jnp.float32)  14.3 us
    ppermute x9, waiting for transfers between devices, psum_doubling(): lax.ppermute(tuple((t.astype(jnp.bfloat16) for t in total)), axis, pairs)  11.4 us
    all_to_all x1, starting transfers between devices, local(): lax.all_to_all(w_out.reshape(local_cols, n_tp, -1), 'tp', split_axis=1, c...  7.91 us
  transfers between devices with their start and end apart: 13, of which 4 were waited for; matrix products, arithmetic and copies ran while one was open for 9% of the time, Pallas kernels for 0%

profile of v6, /device:TPU:24, one launch (start us, length us, event | category | flops | bytes accessed | tf_op | source)
XLA Modules:
  0.0 214.1 jit_solution(943063682857224133)
XLA Ops:
  7.2 0.0 copy-start
  7.2 0.0 all-gather.6.cloned.1.call-start
  7.2 0.7 all-gather.6.cloned.1.call-update
  7.9 0.0 all-gather.8.cloned.1.call-start
  8.0 0.8 reduce-window.7
  8.8 0.1 convert_reduce_fusion.2
  8.9 0.6 dynamic_slice.6
  9.5 0.1 convert_reduce_fusion.1
  9.6 0.1 convert_reduce_fusion
  9.7 1.3 bitcast_subtract_fusion
  11.0 0.6 and_convert_fusion.1
  11.6 0.8 slice_bitcast_fusion.4
  12.4 1.4 fusion.64
  13.8 77.4 %all-gather.6.cloned.1.call-done = bf16[1024,1792]{0,1:T(8,128)(2,1)} async-done(((bf16[1024,112]{0,1:T(8,128)(2,1)}), bf16[1024,1792]{0,1:T(8,128)(2,1)}) %all-gather.6.cloned.1.call-update) | async-done | bytes 3670032 | tf_op jit(solution)/shard_map/all_gather | solution.py:81
  91.2 3.2 %fusion.8 = bf16[1024,1,256]{0,2,1:T(8,128)(2,1)S(1)} fusion(bf16[1024,1792]{0,1:T(8,128)(2,1)} %all-gather.6.cloned.1.call-done, bf16[1792,256]{1,0:T(8,128)(2,1)S(1)} %copy-done), kind=kOutput, calls=%fused_computation.15 | convolution fusion | flops 939786240 | bytes 5111808 | tf_op jit(solution)/shard_map/dot_general | solution.py:80
  94.4 0.1 slice_bitcast_fusion.1
  94.6 1.7 fusion.9
  96.3 1.3 collective-permute-start
  97.6 0.1 multiply_multiply_fusion.1
  97.7 0.1 multiply_multiply_fusion.2
  97.8 0.8 fusion.25
  98.7 14.3 %all-gather.2 = bf16[8,273,112]{2,1,0:T(8,128)(2,1)S(1)} all-gather(bf16[1,273,112]{2,1,0:T(8,128)(2,1)S(1)} %fusion.25), channel_id=2, replica_groups=mesh['seq'=8,'tp'=16,'req'=4] {'seq'}, dimensions={0}, use_global_device_ids=true | all-gather | bytes 550368 | tf_op jit(solution)/shard_map/all_gather | solution.py:139
  112.9 0.2 fusion.21
  113.2 0.0 copy-start.3
  113.2 1.2 multiply_reduce_fusion
  114.4 0.0 copy-start.2
  114.4 1.2 fusion.33
  115.6 0.0 all-gather.8.cloned.1.call-update
  115.7 0.0 copy-start.5
  115.7 1.0 copy.24
  116.6 7.9 %all-to-all-start = ((bf16[112,16,112]{0,2,1:T(8,128)(2,1)}), bf16[112,16,112]{0,2,1:T(8,128)(2,1)S(1)}, u32[]{:S(2)}, u32[]{:S(2)}) async-start(bf16[112,16,112]{0,2,1:T(8,128)(2,1)} %bitcast.26), calls=%async_computation | async-start | bytes 917504 | tf_op jit(solution)/shard_map/all_to_all | solution.py:155
  124.6 0.1 compare_select_fusion.1
  124.7 0.6 gather_fusion
  125.3 0.1 compare_and_fusion
  125.4 0.6 gather_fusion.2
  126.1 0.2 fusion.79
  126.3 2.0 collective-permute-start.7
  128.3 0.8 fusion.55
  129.1 2.4 %collective-permute-start.4 = (bf16[4,1,273]{2,0,1:T(4,128)(2,1)S(1)}, bf16[4,1,273]{2,0,1:T(4,128)(2,1)S(1)}, u32[]{:S(2)}, u32[]{:S(2)}) collective-permute-start(bf16[4,1,273]{2,0,1:T(4,128)(2,1)S(1)} %convert_bitcast_fusion.3), channel_id=1, source_target_pairs={{0,64},{64,0},{128,192},{192,128},{256,320},{320,256},{384,448},{4... | collective-permute-start | bytes 6560 | tf_op jit(solution)/shard_map/ppermute | solution.py:29
  131.5 0.2 maximum_bitcast_fusion.2
  131.6 2.3 %fusion = f32[4,273,112]{2,1,0:T(8,128)S(1)} fusion(f32[1024,273]{0,1:T(8,128)S(1)} %maximum_bitcast_fusion.2, f32[1024,4]{0,1:T(4,128)S(1)} %fusion.56, bf16[1024,1,256]{0,2,1:T(8,128)(2,1)S(1)} %fusion.8), kind=kOutput, calls=%fused_computation.6 | convolution fusion | flops 1503989760 | bytes 1881856 | tf_op jit(solution)/shard_map/dot_general | solution.py:119
  134.0 2.0 collective-permute-start.1
  136.0 0.0 collective-permute-done.7
  136.0 2.9 %collective-permute-start.8 = (bf16[4,2,112]{2,0,1:T(4,128)(2,1)S(1)}, bf16[4,2,112]{2,0,1:T(4,128)(2,1)S(1)}, u32[]{:S(2)}, u32[]{:S(2)}) collective-permute-start(bf16[4,2,112]{2,0,1:T(4,128)(2,1)S(1)} %fusion.68), channel_id=1, source_target_pairs={{0,128},{64,192},{128,0},{192,64},{256,384},{320,448},{384,256},{4... | collective-permute-start | bytes 5384 | tf_op jit(solution)/shard_map/ppermute | solution.py:29
  138.9 2.9 %collective-permute-start.5 = (bf16[4,1,273]{2,0,1:T(4,128)(2,1)S(1)}, bf16[4,1,273]{2,0,1:T(4,128)(2,1)S(1)}, u32[]{:S(2)}, u32[]{:S(2)}) collective-permute-start(bf16[4,1,273]{2,0,1:T(4,128)(2,1)S(1)} %fusion.69), channel_id=1, source_target_pairs={{0,128},{64,192},{128,0},{192,64},{256,384},{320,448},{384,256},{4... | collective-permute-start | bytes 6560 | tf_op jit(solution)/shard_map/ppermute | solution.py:29
  141.9 3.6 %collective-permute-start.9 = (bf16[4,2,112]{2,0,1:T(4,128)(2,1)S(1)}, bf16[4,2,112]{2,0,1:T(4,128)(2,1)S(1)}, u32[]{:S(2)}, u32[]{:S(2)}) collective-permute-start(bf16[4,2,112]{2,0,1:T(4,128)(2,1)S(1)} %fusion.70), channel_id=1, source_target_pairs={{0,256},{64,320},{128,384},{192,448},{256,0},{320,64},{384,128},{4... | collective-permute-start | bytes 5384 | tf_op jit(solution)/shard_map/ppermute | solution.py:29
  145.5 3.8 %collective-permute-start.6 = (bf16[4,1,273]{2,0,1:T(4,128)(2,1)S(1)}, bf16[4,1,273]{2,0,1:T(4,128)(2,1)S(1)}, u32[]{:S(2)}, u32[]{:S(2)}) collective-permute-start(bf16[4,1,273]{2,0,1:T(4,128)(2,1)S(1)} %fusion.67), channel_id=1, source_target_pairs={{0,256},{64,320},{128,384},{192,448},{256,0},{320,64},{384,128},{4... | collective-permute-start | bytes 6560 | tf_op jit(solution)/shard_map/ppermute | solution.py:29
  149.3 0.1 fusion.41
  149.4 2.9 %collective-permute-start.2 = (bf16[1,4,273,112]{3,2,1,0:T(8,128)(2,1)S(1)}, bf16[1,4,273,112]{3,2,1,0:T(8,128)(2,1)S(1)}, u32[]{:S(2)}, u32[]{:S(2)}) collective-permute-start(bf16[1,4,273,112]{3,2,1,0:T(8,128)(2,1)S(1)} %fusion.41), channel_id=1, source_target_pairs={{0,128},{64,192},{128,0},{192,64},{256,384},{320,448},{384,256},{4... | collective-permute-start | bytes 733832 | tf_op jit(solution)/shard_map/ppermute | solution.py:29
  152.3 0.6 gather_fusion.4
  152.9 0.7 select_convert_fusion
  153.6 5.8 %collective-permute-done.2 = bf16[1,4,273,112]{3,2,1,0:T(8,128)(2,1)S(1)} collective-permute-done((bf16[1,4,273,112]{3,2,1,0:T(8,128)(2,1)S(1)}, bf16[1,4,273,112]{3,2,1,0:T(8,128)(2,1)S(1)}, u32[]{:S(2)}, u32[]{:S(2)}) %collective-permute-start.2) | collective-permute-done | bytes 244640 | tf_op jit(solution)/shard_map/ppermute | solution.py:29
  159.4 0.1 fusion.34
  159.5 3.8 %collective-permute-start.3 = (bf16[1,4,273,112]{3,2,1,0:T(8,128)(2,1)S(1)}, bf16[1,4,273,112]{3,2,1,0:T(8,128)(2,1)S(1)}, u32[]{:S(2)}, u32[]{:S(2)}) collective-permute-start(bf16[1,4,273,112]{3,2,1,0:T(8,128)(2,1)S(1)} %fusion.34), channel_id=1, source_target_pairs={{0,256},{64,320},{128,384},{192,448},{256,0},{320,64},{384,128},{4... | collective-permute-start | bytes 733832 | tf_op jit(solution)/shard_map/ppermute | solution.py:29
  163.3 0.6 gather_fusion.3
  163.9 0.1 fusion.63
  164.0 0.6 copy.27
  164.6 5.6 %collective-permute-done.3 = bf16[1,4,273,112]{3,2,1,0:T(8,128)(2,1)S(1)} collective-permute-done((bf16[1,4,273,112]{3,2,1,0:T(8,128)(2,1)S(1)}, bf16[1,4,273,112]{3,2,1,0:T(8,128)(2,1)S(1)}, u32[]{:S(2)}, u32[]{:S(2)}) %collective-permute-start.3) | collective-permute-done | bytes 244640 | tf_op jit(solution)/shard_map/ppermute | solution.py:29
  170.2 0.1 add_bitcast_fusion
  170.3 0.6 gather_fusion.1
  170.9 0.1 fusion.30
  171.0 1.4 copy.26
  172.4 31.4 %all-gather.8.cloned.1.call-done = bf16[1024,1,1792]{0,2,1:T(8,128)(2,1)} async-done(((bf16[1024,1,112]{0,2,1:T(8,128)(2,1)}), bf16[1024,1,1792]{0,2,1:T(8,128)(2,1)}) %all-gather.8.cloned.1.call-update) | async-done | bytes 3670032 | tf_op jit(solution)/shard_map/all_gather | solution.py:158
  203.8 3.5 %convolution_bitcast_fusion.1 = bf16[1024,112]{0,1:T(8,128)(2,1)} fusion(bf16[1024,16,112]{0,2,1:T(8,128)(2,1)} %bitcast.135, bf16[112,16,112]{0,2,1:T(8,128)(2,1)S(1)} %all-to-all-done), kind=kOutput, calls=%fused_computation.20 | convolution fusion | flops 411041792 | bytes 4300800 | tf_op jit(solution)/shard_map/tgk,gkc->gtc/dot_general | solution.py:159
  (39 shorter events, 0.2 us)
Async XLA Ops:
  7.2 84.1 %copy-start = (bf16[1792,256]{1,0:T(8,128)(2,1)S(1)}, bf16[1792,256]{1,0:T(8,128)(2,1)}, u32[]{:S(2)}) copy-start(bf16[1792,256]{1,0:T(8,128)(2,1)} %param.9) | copy-start | bytes 2752516
  7.2 84.0 %all-gather.6.cloned.1.call-start = ((), (), s32[]{:S(2)}) async-start(), calls=%async_computation.1 | async-start | bytes 3899392 | tf_op jit(solution)/shard_map/all_gather | solution.py:81
  7.9 195.9 %all-gather.8.cloned.1.call-start = ((), (), s32[]{:S(2)}) async-start(), calls=%async_computation.2 | async-start | bytes 3899392 | tf_op jit(solution)/shard_map/all_gather | solution.py:158
  96.3 18.2 %collective-permute-start = (bf16[2,112]{0,1:T(8,128)(2,1)S(1)}, bf16[2,112]{0,1:T(8,128)(2,1)S(1)}, u32[]{:S(2)}, u32[]{:S(2)}) collective-permute-start(bf16[2,112]{0,1:T(8,128)(2,1)S(1)} %slice_bitcast_fusion.1), channel_id=1, source_target_pairs={{0,64},{64,128},{128,192},{192,256},{256,320},{320,384},{384,448},... | collective-permute-start | bytes 1352 | tf_op jit(solution)/shard_map/ppermute | solution.py:20
  113.2 1.3 copy-start.3
  114.4 1.2 copy-start.2
  115.6 9.0 %copy-start.4 = (s32[32]{0:T(128)S(1)}, s32[32]{0:T(128)}, u32[]{:S(2)}) copy-start(s32[32]{0:T(128)} %param.15) | copy-start | bytes 388
  115.6 9.1 %copy-start.1 = (s32[32]{0:T(128)S(1)}, s32[32]{0:T(128)}, u32[]{:S(2)}) copy-start(s32[32]{0:T(128)} %param.14) | copy-start | bytes 388
  115.7 9.8 %copy-start.5 = (s32[4]{0:T(128)S(1)}, s32[4]{0:T(128)}, u32[]{:S(2)}) copy-start(s32[4]{0:T(128)} %param.13) | copy-start | bytes 52
  116.6 55.7 %all-to-all-start = ((bf16[112,16,112]{0,2,1:T(8,128)(2,1)}), bf16[112,16,112]{0,2,1:T(8,128)(2,1)S(1)}, u32[]{:S(2)}, u32[]{:S(2)}) async-start(bf16[112,16,112]{0,2,1:T(8,128)(2,1)} %bitcast.26), calls=%async_computation | async-start | bytes 917504 | tf_op jit(solution)/shard_map/all_to_all | solution.py:155
  126.3 9.7 %collective-permute-start.7 = (bf16[4,2,112]{2,0,1:T(4,128)(2,1)S(1)}, bf16[4,2,112]{2,0,1:T(4,128)(2,1)S(1)}, u32[]{:S(2)}, u32[]{:S(2)}) collective-permute-start(bf16[4,2,112]{2,0,1:T(4,128)(2,1)S(1)} %get-tuple-element.40), channel_id=1, source_target_pairs={{0,64},{64,0},{128,192},{192,128},{256,320},{320,256},{384,448},{4... | collective-permute-start | bytes 5384 | tf_op jit(solution)/shard_map/ppermute | solution.py:29
  129.1 9.9 %collective-permute-start.4 = (bf16[4,1,273]{2,0,1:T(4,128)(2,1)S(1)}, bf16[4,1,273]{2,0,1:T(4,128)(2,1)S(1)}, u32[]{:S(2)}, u32[]{:S(2)}) collective-permute-start(bf16[4,1,273]{2,0,1:T(4,128)(2,1)S(1)} %convert_bitcast_fusion.3), channel_id=1, source_target_pairs={{0,64},{64,0},{128,192},{192,128},{256,320},{320,256},{384,448},{4... | collective-permute-start | bytes 6560 | tf_op jit(solution)/shard_map/ppermute | solution.py:29
  134.0 15.3 %collective-permute-start.1 = (bf16[1,4,273,112]{3,2,1,0:T(8,128)(2,1)S(1)}, bf16[1,4,273,112]{3,2,1,0:T(8,128)(2,1)S(1)}, u32[]{:S(2)}, u32[]{:S(2)}) collective-permute-start(bf16[1,4,273,112]{3,2,1,0:T(8,128)(2,1)S(1)} %convert_bitcast_fusion), channel_id=1, source_target_pairs={{0,64},{64,0},{128,192},{192,128},{256,320},{320,256},{384,448},{4... | collective-permute-start | bytes 733832 | tf_op jit(solution)/shard_map/ppermute | solution.py:29
  136.0 5.9 %collective-permute-start.8 = (bf16[4,2,112]{2,0,1:T(4,128)(2,1)S(1)}, bf16[4,2,112]{2,0,1:T(4,128)(2,1)S(1)}, u32[]{:S(2)}, u32[]{:S(2)}) collective-permute-start(bf16[4,2,112]{2,0,1:T(4,128)(2,1)S(1)} %fusion.68), channel_id=1, source_target_pairs={{0,128},{64,192},{128,0},{192,64},{256,384},{320,448},{384,256},{4... | collective-permute-start | bytes 5384 | tf_op jit(solution)/shard_map/ppermute | solution.py:29
  138.9 6.5 %collective-permute-start.5 = (bf16[4,1,273]{2,0,1:T(4,128)(2,1)S(1)}, bf16[4,1,273]{2,0,1:T(4,128)(2,1)S(1)}, u32[]{:S(2)}, u32[]{:S(2)}) collective-permute-start(bf16[4,1,273]{2,0,1:T(4,128)(2,1)S(1)} %fusion.69), channel_id=1, source_target_pairs={{0,128},{64,192},{128,0},{192,64},{256,384},{320,448},{384,256},{4... | collective-permute-start | bytes 6560 | tf_op jit(solution)/shard_map/ppermute | solution.py:29
  141.9 10.4 %collective-permute-start.9 = (bf16[4,2,112]{2,0,1:T(4,128)(2,1)S(1)}, bf16[4,2,112]{2,0,1:T(4,128)(2,1)S(1)}, u32[]{:S(2)}, u32[]{:S(2)}) collective-permute-start(bf16[4,2,112]{2,0,1:T(4,128)(2,1)S(1)} %fusion.70), channel_id=1, source_target_pairs={{0,256},{64,320},{128,384},{192,448},{256,0},{320,64},{384,128},{4... | collective-permute-start | bytes 5384 | tf_op jit(solution)/shard_map/ppermute | solution.py:29
  145.5 17.8 %collective-permute-start.6 = (bf16[4,1,273]{2,0,1:T(4,128)(2,1)S(1)}, bf16[4,1,273]{2,0,1:T(4,128)(2,1)S(1)}, u32[]{:S(2)}, u32[]{:S(2)}) collective-permute-start(bf16[4,1,273]{2,0,1:T(4,128)(2,1)S(1)} %fusion.67), channel_id=1, source_target_pairs={{0,256},{64,320},{128,384},{192,448},{256,0},{320,64},{384,128},{4... | collective-permute-start | bytes 6560 | tf_op jit(solution)/shard_map/ppermute | solution.py:29
  149.4 10.0 %collective-permute-start.2 = (bf16[1,4,273,112]{3,2,1,0:T(8,128)(2,1)S(1)}, bf16[1,4,273,112]{3,2,1,0:T(8,128)(2,1)S(1)}, u32[]{:S(2)}, u32[]{:S(2)}) collective-permute-start(bf16[1,4,273,112]{3,2,1,0:T(8,128)(2,1)S(1)} %fusion.41), channel_id=1, source_target_pairs={{0,128},{64,192},{128,0},{192,64},{256,384},{320,448},{384,256},{4... | collective-permute-start | bytes 733832 | tf_op jit(solution)/shard_map/ppermute | solution.py:29
  159.5 10.7 %collective-permute-start.3 = (bf16[1,4,273,112]{3,2,1,0:T(8,128)(2,1)S(1)}, bf16[1,4,273,112]{3,2,1,0:T(8,128)(2,1)S(1)}, u32[]{:S(2)}, u32[]{:S(2)}) collective-permute-start(bf16[1,4,273,112]{3,2,1,0:T(8,128)(2,1)S(1)} %fusion.34), channel_id=1, source_target_pairs={{0,256},{64,320},{128,384},{192,448},{256,0},{320,64},{384,128},{4... | collective-permute-start | bytes 733832 | tf_op jit(solution)/shard_map/ppermute | solution.py:29
Sparse Core Ops, SparseCore 0:
  10.1 81.1 all-gather.5
  115.8 87.9 all-gather.7

commit v7 on v4

--- a/solution.py
+++ b/solution.py
@@ -82,7 +82,58 @@
     )
     proj = proj.astype(jnp.bfloat16).reshape(tok_rows, local_heads, width)
     gate_pre = proj[:, :, 2 * FEAT + HD :].reshape(tok_rows, local_cols)
-    rim = passed_along(gate_pre[tok_rows - (KW - 1) :], "seq", 1)
+    own_rim = gate_pre[tok_rows - (KW - 1) :]
+    qs_b = proj[:, :, :FEAT] * jnp.bfloat16(FEAT ** (-0.25))
+    ks_b = proj[:, :, FEAT : 2 * FEAT] * jnp.bfloat16(FEAT ** (-0.25))
+    qs = qs_b.astype(jnp.float32)
+    ks = ks_b.astype(jnp.float32)
+    values = proj[:, :, 2 * FEAT : 2 * FEAT + HD]
+    values_f = values.astype(jnp.float32)
+    dots = jnp.einsum("thf,shf->hts", qs_b, ks_b, preferred_element_type=jnp.float32)
+    visible = (positions[None, :] <= positions[:, None]) & (seg[:, None] == seg[None, :])
+    weights = jnp.where(visible[None], 1.0 + dots + 0.5 * dots * dots, 0.0)
+    numer = jnp.einsum(
+        "hts,shd->thd", weights.astype(jnp.bfloat16), values, preferred_element_type=jnp.float32
+    )
+    phi_q = taylor_map(qs)
+    phi_k = taylor_map(ks)
+    fmap = phi_k.shape[-1]
+    prompt_index = jnp.arange(PROMPTS, dtype=jnp.int32)
+    onehot = (seg[:, None] == prompt_index[None, :]).astype(jnp.float32)
+    keyed = (onehot[:, :, None, None] * phi_k[:, None, :, :]).reshape(
+        tok_rows, PROMPTS * local_heads * fmap
+    )
+    contrib_state = lax.dot_general(
+        keyed.reshape(tok_rows, PROMPTS, local_heads, fmap),
+        values_f,
+        (((0,), (0,)), ((2,), (1,))),
+        precision=HIGH,
+    )
+    contrib_norm = jnp.einsum("tg,thf->ghf", onehot, phi_k, precision=HIGH)
+    offsets = jnp.arange(KW - 1, dtype=jnp.int32)
+    edge_rows = ends[:, None] - (KW - 1) + offsets[None, :]
+    edge_valid = edge_rows >= starts[:, None]
+    match = ((positions[:, None, None] == edge_rows[None]) & edge_valid[None]).astype(jnp.bfloat16)
+    contrib_edge = jnp.einsum("tgj,tc->gjc", match, gate_pre, preferred_element_type=jnp.float32)
+    block_ends = (jnp.arange(lax.axis_size("seq"), dtype=jnp.int32) + 1) * tok_rows - 1
+    tail_seg = segment_ids(block_ends, ends)
+    seg_last = tail_seg[seq_pos]
+    in_tail = (seg == seg_last).astype(jnp.float32)
+    tail_state = jnp.einsum(
+        "thf,thd->hfd", phi_k * in_tail[:, None, None], values_f, precision=HIGH
+    )
+    seg_before = jnp.sum((first_row - 1 >= ends).astype(jnp.int32))
+    fmap_rows = tail_state.shape[1]
+    shared = lax.all_gather(
+        jnp.concatenate(
+            [tail_state.astype(jnp.bfloat16), own_rim.reshape(1, KW - 1, -1)], axis=1
+        ),
+        "seq",
+    )
+    tails = shared[:, :, :fmap_rows].astype(jnp.float32)
+    rim = lax.dynamic_index_in_dim(
+        shared[:, 0, fmap_rows:], jnp.maximum(seq_pos - 1, 0), axis=0, keepdims=False
+    ) * (seq_pos > 0).astype(jnp.bfloat16)
     extended = jnp.concatenate([rim, gate_pre], 0)
     ext_pos = first_row - (KW - 1) + jnp.arange(tok_rows + KW - 1, dtype=jnp.int32)
     ext_seg = segment_ids(ext_pos, ends)
@@ -96,47 +147,6 @@
             * extended[low : low + tok_rows].astype(jnp.float32)
             * same[:, None]
         )
-    qs_b = proj[:, :, :FEAT] * jnp.bfloat16(FEAT ** (-0.25))
-    ks_b = proj[:, :, FEAT : 2 * FEAT] * jnp.bfloat16(FEAT ** (-0.25))
-    qs = qs_b.astype(jnp.float32)
-    ks = ks_b.astype(jnp.float32)
-    values = proj[:, :, 2 * FEAT : 2 * FEAT + HD]
-    values_f = values.astype(jnp.float32)
-    dots = jnp.einsum("thf,shf->hts", qs_b, ks_b, preferred_element_type=jnp.float32)
-    visible = (positions[None, :] <= positions[:, None]) & (seg[:, None] == seg[None, :])
-    weights = jnp.where(visible[None], 1.0 + dots + 0.5 * dots * dots, 0.0)
-    numer = jnp.einsum(
-        "hts,shd->thd", weights.astype(jnp.bfloat16), values, preferred_element_type=jnp.float32
-    )
-    phi_q = taylor_map(qs)
-    phi_k = taylor_map(ks)
-    fmap = phi_k.shape[-1]
-    prompt_index = jnp.arange(PROMPTS, dtype=jnp.int32)
-    onehot = (seg[:, None] == prompt_index[None, :]).astype(jnp.float32)
-    keyed = (onehot[:, :, None, None] * phi_k[:, None, :, :]).reshape(
-        tok_rows, PROMPTS * local_heads * fmap
-    )
-    contrib_state = lax.dot_general(
-        keyed.reshape(tok_rows, PROMPTS, local_heads, fmap),
-        values_f,
-        (((0,), (0,)), ((2,), (1,))),
-        precision=HIGH,
-    )
-    contrib_norm = jnp.einsum("tg,thf->ghf", onehot, phi_k, precision=HIGH)
-    offsets = jnp.arange(KW - 1, dtype=jnp.int32)
-    edge_rows = ends[:, None] - (KW - 1) + offsets[None, :]
-    edge_valid = edge_rows >= starts[:, None]
-    match = ((positions[:, None, None] == edge_rows[None]) & edge_valid[None]).astype(jnp.bfloat16)
-    contrib_edge = jnp.einsum("tgj,tc->gjc", match, gate_pre, preferred_element_type=jnp.float32)
-    block_ends = (jnp.arange(lax.axis_size("seq"), dtype=jnp.int32) + 1) * tok_rows - 1
-    tail_seg = segment_ids(block_ends, ends)
-    seg_last = tail_seg[seq_pos]
-    in_tail = (seg == seg_last).astype(jnp.float32)
-    tail_state = jnp.einsum(
-        "thf,thd->hfd", phi_k * in_tail[:, None, None], values_f, precision=HIGH
-    )
-    seg_before = jnp.sum((first_row - 1 >= ends).astype(jnp.int32))
-    tails = lax.all_gather(tail_state.astype(jnp.bfloat16), "seq").astype(jnp.float32)
     block_index = jnp.arange(lax.axis_size("seq"), dtype=jnp.int32)
     chained = ((block_index < seq_pos) & (tail_seg == seg_before)).astype(jnp.float32)
     carry_state = jnp.sum(chained.reshape((-1,) + (1,) * (tails.ndim - 1)) * tails, axis=0)

time: 201 us -> 207 us (1.030)
  local copies, waits for them, and re-layouts: 7.13 us -> 10.5 us
  other arithmetic: 6.52 us -> 8.8 us
    all_gather x0 -> x1, local copies, waits for them, and re-layouts: none -> 2.18 us  [local(): lax.all_gather(jnp.concatenate([tail_state.astype(jnp.bfloat16), own_rim....]
  transfers between devices with their start and end apart: 12 -> 11, of which waited for: 4 -> 4; matrix products, arithmetic and copies ran while one was open for 9% -> 8% of each run, Pallas kernels for 0% -> 0%
where the time goes in v7:
time: 207 us; the launch traced here: 206 us
  waiting for transfers between devices  115 us (56%)
  starting transfers between devices  27 us (13%)
  matrix products  15.1 us (7%)
  blocking collectives  14.6 us (7%)
  between operations  14.5 us (7%)
  local copies, waits for them, and re-layouts  10.5 us (5%)
  other arithmetic  8.8 us (4%)
    all_gather x1, waiting for transfers between devices, local(): lax.all_gather(tokens, 'tp', axis=1, tiled=True)  76.4 us
    reduce_scatter x1, waiting for transfers between devices, local(): summed = lax.psum_scatter(product, 'tp', scatter_dimension=0, tiled=True)  27.5 us
    ppermute x9, starting transfers between devices, psum_doubling(): lax.ppermute(tuple((t.astype(jnp.bfloat16) for t in total)), axis, pairs)  26.9 us
    all_gather x1, blocking collectives, local(): lax.all_gather(jnp.concatenate([tail_state.astype(jnp.bfloat16), own_rim....  14.6 us
    ppermute x9, waiting for transfers between devices, psum_doubling(): lax.ppermute(tuple((t.astype(jnp.bfloat16) for t in total)), axis, pairs)  10.5 us
  transfers between devices with their start and end apart: 11, of which 4 were waited for; matrix products, arithmetic and copies ran while one was open for 8% of the time, Pallas kernels for 0%

profile of v7, /device:TPU:24, one launch (start us, length us, event | category | flops | bytes accessed | tf_op | source)
XLA Modules:
  0.0 205.6 jit_solution(16955415257671343951)
XLA Ops:
  7.2 0.0 copy-start
  7.2 0.0 all-gather.3.cloned.1.call-start
  7.2 0.7 all-gather.3.cloned.1.call-update
  7.9 0.0 reduce-scatter.2.cloned.1.call-start
  8.0 0.8 reduce-window.7
  8.8 0.1 convert_reduce_fusion.2
  8.9 0.6 dynamic_slice.10
  9.5 0.1 convert_reduce_fusion.1
  9.6 0.1 convert_reduce_fusion
  9.7 1.8 bitcast_subtract_fusion
  11.5 1.2 and_convert_fusion.1
  12.7 0.8 slice_bitcast_fusion.4
  13.5 1.4 fusion.73
  14.8 76.4 %all-gather.3.cloned.1.call-done = bf16[1024,1792]{0,1:T(8,128)(2,1)} async-done(((bf16[1024,112]{0,1:T(8,128)(2,1)}), bf16[1024,1792]{0,1:T(8,128)(2,1)}) %all-gather.3.cloned.1.call-update) | async-done | bytes 3670032 | tf_op jit(solution)/shard_map/all_gather | solution.py:81
  91.2 3.2 %fusion.8 = bf16[1024,1,256]{0,2,1:T(8,128)(2,1)S(1)} fusion(bf16[1024,1792]{0,1:T(8,128)(2,1)} %all-gather.3.cloned.1.call-done, bf16[1792,256]{1,0:T(8,128)(2,1)S(1)} %copy-done), kind=kOutput, calls=%fused_computation.16 | convolution fusion | flops 939786240 | bytes 5111808 | tf_op jit(solution)/shard_map/dot_general | solution.py:80
  94.4 0.0 copy-start.4
  94.4 0.1 slice_bitcast_fusion.1
  94.6 2.5 %fusion.9 = f32[1,112,1024]{2,1,0:T(8,128)} fusion(s32[1024]{0:T(1024)S(1)} %convert_reduce_fusion.1, s32[1024]{0:T(1024)S(1)} %iota_add_fusion.1, bf16[1024,1,256]{0,2,1:T(8,128)(2,1)S(1)} %fusion.8), kind=kOutput, calls=%fused_computation.17 | convolution fusion | flops 277905408 | bytes 770048 | tf_op jit(solution)/shard_map/hts,shd->thd/dot_general | solution.py:95
  97.1 0.1 copy.28
  97.1 0.1 multiply_multiply_fusion.1
  97.3 0.1 multiply_multiply_fusion.2
  97.4 1.8 fusion.24
  99.2 14.6 %all-gather = bf16[8,275,112]{2,1,0:T(8,128)(2,1)} all-gather(bf16[1,275,112]{2,1,0:T(8,128)(2,1)S(1)} %pad_maximum_fusion.1), channel_id=2, replica_groups=mesh['seq'=8,'tp'=16,'req'=4] {'seq'}, dimensions={0}, use_global_device_ids=true | all-gather | bytes 554400 | tf_op jit(solution)/shard_map/all_gather | solution.py:127
  113.8 2.2 %copy.29 = bf16[8,275,112]{1,2,0:T(8,128)(2,1)} copy(bf16[8,275,112]{2,1,0:T(8,128)(2,1)} %all-gather) | data formatting | bytes 985600 | tf_op jit(solution)/shard_map/all_gather | solution.py:127
  116.0 1.1 slice.79
  117.1 0.0 copy-start.2
  117.1 0.0 copy-start.7
  117.1 1.4 multiply_reduce_fusion
  118.5 1.1 multiply_reduce_fusion.1
  119.7 3.2 %fusion.37 = bf16[1024,1792]{0,1} fusion(bf16[112,1792]{1,0:T(8,128)(2,1)S(1)} %copy-done.2, bf16[1024,112]{0,1:T(8,128)(2,1)S(1)} %slice_bitcast_fusion, f32[1,112,1024]{2,1,0:T(8,128)S(1)} %get-tuple-element.39, bf16[2,112]{0,1:T(8,128)(2,1)S(1)} %multiply_bitcast_fusion, f32[1024]{0:T(1024)S(1)} %get-tuple-element.28, f32[112]{0:T(128)S(1)} %get-tuple-element.33, ...), kind=kOutput, calls=%fused_computation.56 | convolution fusion | flops 413908992 | bytes 4778176
  122.9 0.0 copy-start.10
  123.0 0.0 reduce-scatter.2.cloned.1.call-update
  123.0 0.6 copy-done.8
  123.6 0.1 compare_select_fusion.1
  123.7 0.6 gather_fusion
  124.3 0.1 compare_and_fusion
  124.4 0.6 gather_fusion.2
  125.1 0.2 fusion.90
  125.4 2.3 %collective-permute-start.6 = (bf16[4,2,112]{2,0,1:T(4,128)(2,1)S(1)}, bf16[4,2,112]{2,0,1:T(4,128)(2,1)S(1)}, u32[]{:S(2)}, u32[]{:S(2)}) collective-permute-start(bf16[4,2,112]{2,0,1:T(4,128)(2,1)S(1)} %get-tuple-element.40), channel_id=1, source_target_pairs={{0,64},{64,0},{128,192},{192,128},{256,320},{320,256},{384,448},{4... | collective-permute-start | bytes 5384 | tf_op jit(solution)/shard_map/ppermute | solution.py:29
  127.6 0.8 fusion.64
  128.4 2.1 %collective-permute-start.3 = (bf16[4,1,273]{2,0,1:T(4,128)(2,1)S(1)}, bf16[4,1,273]{2,0,1:T(4,128)(2,1)S(1)}, u32[]{:S(2)}, u32[]{:S(2)}) collective-permute-start(bf16[4,1,273]{2,0,1:T(4,128)(2,1)S(1)} %convert_bitcast_fusion.3), channel_id=1, source_target_pairs={{0,64},{64,0},{128,192},{192,128},{256,320},{320,256},{384,448},{4... | collective-permute-start | bytes 6560 | tf_op jit(solution)/shard_map/ppermute | solution.py:29
  130.5 0.2 maximum_bitcast_fusion.2
  130.7 2.3 %fusion = f32[4,273,112]{2,1,0:T(8,128)S(1)} fusion(f32[1024,273]{0,1:T(8,128)S(1)} %maximum_bitcast_fusion.2, f32[1024,4]{0,1:T(4,128)S(1)} %fusion.65, bf16[1024,1,256]{0,2,1:T(8,128)(2,1)S(1)} %copy-done.5), kind=kOutput, calls=%fused_computation.6 | convolution fusion | flops 1503989760 | bytes 1881856 | tf_op jit(solution)/shard_map/dot_general | solution.py:106
  133.1 2.3 %collective-permute-start = (bf16[1,4,273,112]{3,2,1,0:T(8,128)(2,1)S(1)}, bf16[1,4,273,112]{3,2,1,0:T(8,128)(2,1)S(1)}, u32[]{:S(2)}, u32[]{:S(2)}) collective-permute-start(bf16[1,4,273,112]{3,2,1,0:T(8,128)(2,1)S(1)} %convert_bitcast_fusion), channel_id=1, source_target_pairs={{0,64},{64,0},{128,192},{192,128},{256,320},{320,256},{384,448},{4... | collective-permute-start | bytes 733832 | tf_op jit(solution)/shard_map/ppermute | solution.py:29
  135.3 3.1 %collective-permute-start.7 = (bf16[4,2,112]{2,0,1:T(4,128)(2,1)S(1)}, bf16[4,2,112]{2,0,1:T(4,128)(2,1)S(1)}, u32[]{:S(2)}, u32[]{:S(2)}) collective-permute-start(bf16[4,2,112]{2,0,1:T(4,128)(2,1)S(1)} %fusion.77), channel_id=1, source_target_pairs={{0,128},{64,192},{128,0},{192,64},{256,384},{320,448},{384,256},{4... | collective-permute-start | bytes 5384 | tf_op jit(solution)/shard_map/ppermute | solution.py:29
  138.4 2.8 %collective-permute-start.4 = (bf16[4,1,273]{2,0,1:T(4,128)(2,1)S(1)}, bf16[4,1,273]{2,0,1:T(4,128)(2,1)S(1)}, u32[]{:S(2)}, u32[]{:S(2)}) collective-permute-start(bf16[4,1,273]{2,0,1:T(4,128)(2,1)S(1)} %fusion.78), channel_id=1, source_target_pairs={{0,128},{64,192},{128,0},{192,64},{256,384},{320,448},{384,256},{4... | collective-permute-start | bytes 6560 | tf_op jit(solution)/shard_map/ppermute | solution.py:29
  141.2 3.7 %collective-permute-start.8 = (bf16[4,2,112]{2,0,1:T(4,128)(2,1)S(1)}, bf16[4,2,112]{2,0,1:T(4,128)(2,1)S(1)}, u32[]{:S(2)}, u32[]{:S(2)}) collective-permute-start(bf16[4,2,112]{2,0,1:T(4,128)(2,1)S(1)} %fusion.79), channel_id=1, source_target_pairs={{0,256},{64,320},{128,384},{192,448},{256,0},{320,64},{384,128},{4... | collective-permute-start | bytes 5384 | tf_op jit(solution)/shard_map/ppermute | solution.py:29
  145.0 3.6 %collective-permute-start.5 = (bf16[4,1,273]{2,0,1:T(4,128)(2,1)S(1)}, bf16[4,1,273]{2,0,1:T(4,128)(2,1)S(1)}, u32[]{:S(2)}, u32[]{:S(2)}) collective-permute-start(bf16[4,1,273]{2,0,1:T(4,128)(2,1)S(1)} %fusion.76), channel_id=1, source_target_pairs={{0,256},{64,320},{128,384},{192,448},{256,0},{320,64},{384,128},{4... | collective-permute-start | bytes 6560 | tf_op jit(solution)/shard_map/ppermute | solution.py:29
  148.6 0.1 fusion.50
  148.7 3.1 %collective-permute-start.1 = (bf16[1,4,273,112]{3,2,1,0:T(8,128)(2,1)S(1)}, bf16[1,4,273,112]{3,2,1,0:T(8,128)(2,1)S(1)}, u32[]{:S(2)}, u32[]{:S(2)}) collective-permute-start(bf16[1,4,273,112]{3,2,1,0:T(8,128)(2,1)S(1)} %fusion.50), channel_id=1, source_target_pairs={{0,128},{64,192},{128,0},{192,64},{256,384},{320,448},{384,256},{4... | collective-permute-start | bytes 733832 | tf_op jit(solution)/shard_map/ppermute | solution.py:29
  151.8 0.6 gather_fusion.4
  152.4 0.7 select_convert_fusion
  153.1 5.3 %collective-permute-done.1 = bf16[1,4,273,112]{3,2,1,0:T(8,128)(2,1)S(1)} collective-permute-done((bf16[1,4,273,112]{3,2,1,0:T(8,128)(2,1)S(1)}, bf16[1,4,273,112]{3,2,1,0:T(8,128)(2,1)S(1)}, u32[]{:S(2)}, u32[]{:S(2)}) %collective-permute-start.1) | collective-permute-done | bytes 244640 | tf_op jit(solution)/shard_map/ppermute | solution.py:29
  158.4 0.1 fusion.32
  158.5 4.0 %collective-permute-start.2 = (bf16[1,4,273,112]{3,2,1,0:T(8,128)(2,1)S(1)}, bf16[1,4,273,112]{3,2,1,0:T(8,128)(2,1)S(1)}, u32[]{:S(2)}, u32[]{:S(2)}) collective-permute-start(bf16[1,4,273,112]{3,2,1,0:T(8,128)(2,1)S(1)} %fusion.32), channel_id=1, source_target_pairs={{0,256},{64,320},{128,384},{192,448},{256,0},{320,64},{384,128},{4... | collective-permute-start | bytes 733832 | tf_op jit(solution)/shard_map/ppermute | solution.py:29
  162.6 0.6 gather_fusion.3
  163.1 0.1 fusion.72
  163.2 0.6 copy.33
  163.8 5.1 %collective-permute-done.2 = bf16[1,4,273,112]{3,2,1,0:T(8,128)(2,1)S(1)} collective-permute-done((bf16[1,4,273,112]{3,2,1,0:T(8,128)(2,1)S(1)}, bf16[1,4,273,112]{3,2,1,0:T(8,128)(2,1)S(1)}, u32[]{:S(2)}, u32[]{:S(2)}) %collective-permute-start.2) | collective-permute-done | bytes 244640 | tf_op jit(solution)/shard_map/ppermute | solution.py:29
  168.9 0.1 add_bitcast_fusion
  169.1 0.6 gather_fusion.1
  169.7 0.1 fusion.29
  169.8 1.4 copy.32
  171.2 27.5 %reduce-scatter.2.cloned.1.call-done = bf16[1,1024,112]{1,2,0:T(8,128)(2,1)} async-done(((bf16[16,1024,112]{1,2,0:T(8,128)(2,1)}), bf16[1,1024,112]{1,2,0:T(8,128)(2,1)}) %reduce-scatter.2.cloned.1.call-update) | async-done | bytes 229392 | tf_op jit(solution)/shard_map/reduce_scatter | solution.py:170
  (50 shorter events, 0.3 us)
Async XLA Ops:
  7.2 84.1 %copy-start = (bf16[1792,256]{1,0:T(8,128)(2,1)S(1)}, bf16[1792,256]{1,0:T(8,128)(2,1)}, u32[]{:S(2)}) copy-start(bf16[1792,256]{1,0:T(8,128)(2,1)} %param.9) | copy-start | bytes 2752516
  7.2 84.0 %all-gather.3.cloned.1.call-start = ((), (), s32[]{:S(2)}) async-start(), calls=%async_computation.1 | async-start | bytes 3899392 | tf_op jit(solution)/shard_map/all_gather | solution.py:81
  7.9 190.8 %reduce-scatter.2.cloned.1.call-start = ((), (), s32[]{:S(2)}) async-start(), calls=%async_computation.2 | async-start | bytes 3899392 | tf_op jit(solution)/shard_map/reduce_scatter | solution.py:170
  94.4 2.6 %copy-start.4 = (bf16[1024,1,256]{0,2,1:T(8,128)(2,1)}, bf16[1024,1,256]{0,2,1:T(8,128)(2,1)S(1)}, u32[]{:S(2)}) copy-start(bf16[1024,1,256]{0,2,1:T(8,128)(2,1)S(1)} %fusion.8) | copy-start | bytes 1572868
  99.2 17.9 %copy-start.6 = (f32[8]{0:T(128)S(1)}, f32[8]{0:T(128)}, u32[]{:S(2)}) copy-start(f32[8]{0:T(128)} %and_convert_fusion.1) | copy-start | bytes 100
  116.0 2.5 %copy-start.3 = (f32[1,112,1024]{2,1,0:T(8,128)S(1)}, f32[1,112,1024]{2,1,0:T(8,128)}, u32[]{:S(2)}) copy-start(f32[1,112,1024]{2,1,0:T(8,128)} %fusion.9) | copy-start | bytes 1376260
  117.1 2.6 %copy-start.2 = (bf16[112,1792]{1,0:T(8,128)(2,1)S(1)}, bf16[112,1792]{1,0:T(8,128)(2,1)}, u32[]{:S(2)}) copy-start(bf16[112,1792]{1,0:T(8,128)(2,1)} %param.12) | copy-start | bytes 1204228
  117.1 2.6 %copy-start.7 = (f32[112]{0:T(128)S(1)}, f32[112]{0:T(128)}, u32[]{:S(2)}) copy-start(f32[112]{0:T(128)} %param.11) | copy-start | bytes 1348
  122.9 0.7 copy-start.8
  122.9 0.7 copy-start.1
  122.9 1.5 copy-start.9
  122.9 2.1 %copy-start.11 = (s32[4]{0:T(128)S(1)}, s32[4]{0:T(128)}, u32[]{:S(2)}) copy-start(s32[4]{0:T(128)} %get-tuple-element.37) | copy-start | bytes 52
  122.9 2.1 %copy-start.10 = (s32[4]{0:T(128)S(1)}, s32[4]{0:T(128)}, u32[]{:S(2)}) copy-start(s32[4]{0:T(128)} %get-tuple-element.35) | copy-start | bytes 52
  123.0 2.2 %copy-start.5 = (bf16[1024,1,256]{0,2,1:T(8,128)(2,1)S(1)}, bf16[1024,1,256]{0,2,1:T(8,128)(2,1)}, u32[]{:S(2)}) copy-start(bf16[1024,1,256]{0,2,1:T(8,128)(2,1)} %copy-done.4) | copy-start | bytes 1572868
  125.4 10.0 %collective-permute-start.6 = (bf16[4,2,112]{2,0,1:T(4,128)(2,1)S(1)}, bf16[4,2,112]{2,0,1:T(4,128)(2,1)S(1)}, u32[]{:S(2)}, u32[]{:S(2)}) collective-permute-start(bf16[4,2,112]{2,0,1:T(4,128)(2,1)S(1)} %get-tuple-element.40), channel_id=1, source_target_pairs={{0,64},{64,0},{128,192},{192,128},{256,320},{320,256},{384,448},{4... | collective-permute-start | bytes 5384 | tf_op jit(solution)/shard_map/ppermute | solution.py:29
  128.4 10.0 %collective-permute-start.3 = (bf16[4,1,273]{2,0,1:T(4,128)(2,1)S(1)}, bf16[4,1,273]{2,0,1:T(4,128)(2,1)S(1)}, u32[]{:S(2)}, u32[]{:S(2)}) collective-permute-start(bf16[4,1,273]{2,0,1:T(4,128)(2,1)S(1)} %convert_bitcast_fusion.3), channel_id=1, source_target_pairs={{0,64},{64,0},{128,192},{192,128},{256,320},{320,256},{384,448},{4... | collective-permute-start | bytes 6560 | tf_op jit(solution)/shard_map/ppermute | solution.py:29
  133.1 15.6 %collective-permute-start = (bf16[1,4,273,112]{3,2,1,0:T(8,128)(2,1)S(1)}, bf16[1,4,273,112]{3,2,1,0:T(8,128)(2,1)S(1)}, u32[]{:S(2)}, u32[]{:S(2)}) collective-permute-start(bf16[1,4,273,112]{3,2,1,0:T(8,128)(2,1)S(1)} %convert_bitcast_fusion), channel_id=1, source_target_pairs={{0,64},{64,0},{128,192},{192,128},{256,320},{320,256},{384,448},{4... | collective-permute-start | bytes 733832 | tf_op jit(solution)/shard_map/ppermute | solution.py:29
  135.3 5.9 %collective-permute-start.7 = (bf16[4,2,112]{2,0,1:T(4,128)(2,1)S(1)}, bf16[4,2,112]{2,0,1:T(4,128)(2,1)S(1)}, u32[]{:S(2)}, u32[]{:S(2)}) collective-permute-start(bf16[4,2,112]{2,0,1:T(4,128)(2,1)S(1)} %fusion.77), channel_id=1, source_target_pairs={{0,128},{64,192},{128,0},{192,64},{256,384},{320,448},{384,256},{4... | collective-permute-start | bytes 5384 | tf_op jit(solution)/shard_map/ppermute | solution.py:29
  138.4 6.5 %collective-permute-start.4 = (bf16[4,1,273]{2,0,1:T(4,128)(2,1)S(1)}, bf16[4,1,273]{2,0,1:T(4,128)(2,1)S(1)}, u32[]{:S(2)}, u32[]{:S(2)}) collective-permute-start(bf16[4,1,273]{2,0,1:T(4,128)(2,1)S(1)} %fusion.78), channel_id=1, source_target_pairs={{0,128},{64,192},{128,0},{192,64},{256,384},{320,448},{384,256},{4... | collective-permute-start | bytes 6560 | tf_op jit(solution)/shard_map/ppermute | solution.py:29
  141.2 10.6 %collective-permute-start.8 = (bf16[4,2,112]{2,0,1:T(4,128)(2,1)S(1)}, bf16[4,2,112]{2,0,1:T(4,128)(2,1)S(1)}, u32[]{:S(2)}, u32[]{:S(2)}) collective-permute-start(bf16[4,2,112]{2,0,1:T(4,128)(2,1)S(1)} %fusion.79), channel_id=1, source_target_pairs={{0,256},{64,320},{128,384},{192,448},{256,0},{320,64},{384,128},{4... | collective-permute-start | bytes 5384 | tf_op jit(solution)/shard_map/ppermute | solution.py:29
  145.0 17.5 %collective-permute-start.5 = (bf16[4,1,273]{2,0,1:T(4,128)(2,1)S(1)}, bf16[4,1,273]{2,0,1:T(4,128)(2,1)S(1)}, u32[]{:S(2)}, u32[]{:S(2)}) collective-permute-start(bf16[4,1,273]{2,0,1:T(4,128)(2,1)S(1)} %fusion.76), channel_id=1, source_target_pairs={{0,256},{64,320},{128,384},{192,448},{256,0},{320,64},{384,128},{4... | collective-permute-start | bytes 6560 | tf_op jit(solution)/shard_map/ppermute | solution.py:29
  148.7 9.7 %collective-permute-start.1 = (bf16[1,4,273,112]{3,2,1,0:T(8,128)(2,1)S(1)}, bf16[1,4,273,112]{3,2,1,0:T(8,128)(2,1)S(1)}, u32[]{:S(2)}, u32[]{:S(2)}) collective-permute-start(bf16[1,4,273,112]{3,2,1,0:T(8,128)(2,1)S(1)} %fusion.50), channel_id=1, source_target_pairs={{0,128},{64,192},{128,0},{192,64},{256,384},{320,448},{384,256},{4... | collective-permute-start | bytes 733832 | tf_op jit(solution)/shard_map/ppermute | solution.py:29
  158.5 10.4 %collective-permute-start.2 = (bf16[1,4,273,112]{3,2,1,0:T(8,128)(2,1)S(1)}, bf16[1,4,273,112]{3,2,1,0:T(8,128)(2,1)S(1)}, u32[]{:S(2)}, u32[]{:S(2)}) collective-permute-start(bf16[1,4,273,112]{3,2,1,0:T(8,128)(2,1)S(1)} %fusion.32), channel_id=1, source_target_pairs={{0,256},{64,320},{128,384},{192,448},{256,0},{320,64},{384,128},{4... | collective-permute-start | bytes 733832 | tf_op jit(solution)/shard_map/ppermute | solution.py:29
Sparse Core Ops, SparseCore 0:
  10.1 81.1 all-gather.2
  123.1 75.5 reduce-scatter.1
